TPU v7x, 512 devices: a whole 4x4x16 slice. The times are simulated.
512 devices in a mesh: dp: 64 (over z, y), fsdp: 8 (over x, core).
Axes of the slice: x: 4, y: 4, z: 16, core: 2. Of those that a mesh axis runs over, the one named last changes fastest.
Arguments:
- tokens: bfloat16 [65536, 2048], P('dp', 'fsdp'), may hold values from -6 to 6
- norm_gain: bfloat16 [2048], replicated, may hold values from 0.25 to 1.75
- query_gain: bfloat16 [128], replicated, as said below
- key_gain: bfloat16 [128], replicated, as said below
- w_query: bfloat16 [2048, 2048], P('dp', 'fsdp'), as said below
- w_key: bfloat16 [2048, 1024], P('dp', 'fsdp'), as said below
- w_value: bfloat16 [2048, 1024], P('dp', 'fsdp'), may hold values from -0.125 to 0.125
- w_out: bfloat16 [2048, 2048], P('dp', 'fsdp'), may hold values from -0.125 to 0.125
- prompt_lengths: int32 [64, 8], replicated, may hold values from 1 to 512, 1024 in all within a row
- span_group: int32 [64, 64], replicated, may hold values from 0 to 63, as said below
Outputs:
- attention_update: bfloat16 [65536, 2048], P('dp', 'fsdp')
- kv_cache: bfloat16 [65536, 8, 256], P('dp', 'fsdp')
Inputs may be any that keep to these rules, and one draw needn't show every extreme that they name: `prompt_lengths`: row g sums to 1024. `span_group`: row i names, in arrival order, the group of each of its 64 blocks of 16 rows; every group is named exactly 64 times in all; every row names exactly one group twice and leaves exactly one group out, and every group is the one named twice by exactly one row. `query_gain`: Positive. `key_gain`: Positive. `w_query`: entries of size about one over the square root of 2048. `w_key`: entries of size about one over the square root of 2048.
All inputs are finite; a program needn't handle non-finite values.
Results may differ from a plain program's by a relative error of at most 0.0075.
The roundings to bfloat16 on the way count: a program that leaves them out, or rounds other values in their place, can miss the bound.
Values may be sent and summed in bfloat16 or wider, within the bound.
No kernel may reach another device: no remote copies, remote signals or barrier semaphores. Data moves between devices by JAX's collectives and lax.ppermute only.
A program may use at most 64 MiB of HBM per device.

v0:
```python
import math

import jax
import jax.numpy as jnp
from jax import lax
from jax.sharding import PartitionSpec as P

QH = 16
KVH = 8
HD = 128


epsilon = 1e-06
rope_base = 1000000.0


def for_sending(x):

    def short(part):
        return part.astype(jnp.bfloat16) if part.dtype == jnp.float32 else part

    return jax.tree.map(short, x)


def head_norm(inputs, gains):
    inv_rms = lax.rsqrt(jnp.mean(inputs * inputs, axis=-1, keepdims=True) + epsilon)
    return inputs * inv_rms * gains.astype(jnp.float32)


def rotate(inputs, offsets):
    half_dim = inputs.shape[-1] // 2
    frequency = jnp.power(
        rope_base, -2.0 * jnp.arange(half_dim, dtype=jnp.float32) / inputs.shape[-1]
    )
    angles = offsets.astype(jnp.float32)[:, None] * frequency[None, :]
    cosine = jnp.cos(angles)[:, None, :]
    sine_part = jnp.sin(angles)[:, None, :]
    first_half = inputs[..., :half_dim]
    second = inputs[..., half_dim:]
    return jnp.concatenate(
        [first_half * cosine - second * sine_part, second * cosine + first_half * sine_part],
        axis=-1,
    )


def prompt_layout(lengths, group_rows):
    prompt_end = jnp.cumsum(lengths)
    begins = prompt_end - lengths
    position = jnp.arange(group_rows, dtype=jnp.int32)
    inside = (position[:, None] >= begins[None, :]) & (position[:, None] < prompt_end[None, :])
    starts = jnp.sum(jnp.where(inside, begins[None, :], 0), axis=1)
    return (position, starts)


def attend(query_block, key_rot, value_rows, pos_block, start_block, position):
    scores = jnp.einsum(
        "qkrd,skd->krqs", query_block, key_rot, preferred_element_type=jnp.float32
    ) * (1.0 / math.sqrt(HD))
    allowed = (position[None, :] <= pos_block[:, None]) & (
        position[None, :] >= start_block[:, None]
    )
    masked = jnp.where(allowed[None, None], scores, -jnp.inf)
    row_max = jnp.max(masked, axis=-1, keepdims=True)
    exp_scores = jnp.exp(masked - row_max)
    probs = (exp_scores / jnp.sum(exp_scores, axis=-1, keepdims=True)).astype(jnp.bfloat16)
    return jnp.einsum(
        "krqs,skd->qkrd", probs, value_rows, preferred_element_type=jnp.float32
    ).astype(jnp.bfloat16)


def with_zero_row(array):
    return jnp.concatenate([array, jnp.zeros((1,) + array.shape[1:], array.dtype)], axis=0)


def local(
    tokens,
    norm_gain,
    query_gain,
    key_gain,
    w_query,
    w_key,
    w_value,
    w_out,
    prompt_lengths,
    span_group,
):
    group_rows, width_local = tokens.shape
    groups = lax.axis_size("dp")
    arrival_rows = group_rows // groups
    capacity = 2 * arrival_rows
    device_index = lax.axis_index("dp")
    group_ids = jnp.arange(groups, dtype=jnp.int32)
    slot_ids = jnp.arange(capacity, dtype=jnp.int32)
    own_blocks = lax.dynamic_index_in_dim(span_group, device_index, 0, keepdims=False)
    counts = jnp.sum((span_group == device_index).astype(jnp.int32), axis=1)
    offsets = jnp.cumsum(counts) - counts
    row_dest = jnp.repeat(own_blocks, arrival_rows)
    onehot = (row_dest[:, None] == group_ids[None, :]).astype(jnp.int32)
    slot_rank = jnp.sum((jnp.cumsum(onehot, axis=0) - 1) * onehot, axis=1)
    send_slot = row_dest * capacity + slot_rank
    slot_source = (
        jnp.full((groups * capacity,), group_rows, jnp.int32)
        .at[send_slot]
        .set(jnp.arange(group_rows, dtype=jnp.int32))
    )
    outgoing = with_zero_row(tokens)[slot_source].reshape(groups, capacity, width_local)
    incoming = lax.all_to_all(outgoing, "dp", split_axis=0, concat_axis=0, tiled=True)
    is_valid = slot_ids[None, :] < arrival_rows * counts[:, None]
    target = arrival_rows * offsets[:, None] + slot_ids[None, :]
    flat_slot = group_ids[:, None] * capacity + slot_ids[None, :]
    back_index = jnp.where(is_valid, target, group_rows)
    source_of = (
        jnp.zeros((group_rows,), jnp.int32)
        .at[back_index.reshape(-1)]
        .set(flat_slot.reshape(-1), mode="drop")
    )
    arrived = incoming.reshape(groups * capacity, width_local)[source_of]
    full_rows = lax.all_gather(arrived, "fsdp", axis=1, tiled=True)
    query_full, key_full, value_full, out_full = (
        lax.all_gather(w_query, "dp", axis=0, tiled=True),
        lax.all_gather(w_key, "dp", axis=0, tiled=True),
        lax.all_gather(w_value, "dp", axis=0, tiled=True),
        lax.all_gather(w_out, "dp", axis=0, tiled=True),
    )
    lengths = lax.dynamic_index_in_dim(prompt_lengths, device_index, 0, keepdims=False)
    position, starts = prompt_layout(lengths, group_rows)
    within = position - starts
    floats = full_rows.astype(jnp.float32)
    normed = (
        floats
        * lax.rsqrt(jnp.mean(floats * floats, axis=-1, keepdims=True) + epsilon)
        * norm_gain.astype(jnp.float32)
    ).astype(jnp.bfloat16)
    query = jnp.dot(normed, query_full, preferred_element_type=jnp.float32).reshape(
        group_rows, -1, HD
    )
    key_rows = jnp.dot(normed, key_full, preferred_element_type=jnp.float32).reshape(
        group_rows, -1, HD
    )
    value_rows = (
        jnp.dot(normed, value_full, preferred_element_type=jnp.float32)
        .reshape(group_rows, -1, HD)
        .astype(jnp.bfloat16)
    )
    query_rot = rotate(head_norm(query, query_gain), within).astype(jnp.bfloat16)
    key_rot = rotate(head_norm(key_rows, key_gain), within).astype(jnp.bfloat16)
    kv_heads = key_rot.shape[1]
    group_ratio = QH // KVH
    cache_rows = jnp.concatenate([key_rot, value_rows], axis=-1)
    block_count = group_rows // 512
    block_len = group_rows // block_count
    query_heads = query_rot.reshape(block_count, block_len, kv_heads, group_ratio, HD)

    def one_block(pieces):
        query_block, pos_block, start_block = pieces
        return attend(query_block, key_rot, value_rows, pos_block, start_block, position)

    mixed = lax.map(
        one_block,
        (
            query_heads,
            position.reshape(block_count, block_len),
            starts.reshape(block_count, block_len),
        ),
    )
    mixed = mixed.reshape(group_rows, kv_heads * group_ratio * HD)
    heads_all = lax.all_gather(mixed, "fsdp", axis=1, tiled=True)
    update = jnp.dot(heads_all, out_full, preferred_element_type=jnp.float32).astype(jnp.bfloat16)
    arrays = (update, cache_rows)
    sent = tuple((with_zero_row(array)[back_index] for array in arrays))
    back = jax.tree.map(
        lambda part, own: part.astype(own.dtype),
        lax.all_to_all(for_sending(sent), "dp", split_axis=0, concat_axis=0, tiled=True),
        sent,
    )
    attention_out, cache_out = tuple(
        (piece.reshape((groups * capacity,) + piece.shape[2:])[send_slot] for piece in back)
    )
    return (attention_out, cache_out)


def solution(mesh):
    return jax.shard_map(
        local,
        mesh=mesh,
        in_specs=(
            P("dp", "fsdp"),
            P(),
            P(),
            P(),
            P("dp", "fsdp"),
            P("dp", "fsdp"),
            P("dp", "fsdp"),
            P("dp", "fsdp"),
            P(),
            P(),
        ),
        out_specs=(P("dp", "fsdp"), P("dp", "fsdp", None)),
        check_vma=False,
    )
```

profile of v0, /device:TPU:24, one launch (start us, length us, event | category | flops | bytes accessed | tf_op | source)
XLA Modules:
  0.0 579.3 jit_solution(6005886002139596010)
XLA Ops:
  8.9 18.0 %reduce-window.24 = s32[64,8,128]{2,1,0:T(8,128)S(1)} reduce-window(s32[64,8,128]{2,1,0:T(8,128)S(1)} %fusion.41, s32[]{:T(128)} %copy.68), window={size=1x1x128 pad=0_0x0_0x127_0}, to_apply=%region_0.1 | reduce-window | flops 8323072 | bytes 524292 | tf_op jit(solution)/shard_map/reduce-window
  27.8 4.3 scatter_custom_fusion
  33.3 9.0 %gather_fusion = bf16[2048,256]{1,0:T(8,128)(2,1)} fusion(bf16[1025,256]{1,0:T(8,128)(2,1)S(1)} %concatenate.40, s32[2048]{0:T(1024)S(1)} %fusion.43), kind=kCustom, calls=%fused_computation | custom fusion | bytes 2105344 | tf_op jit(solution)/shard_map/gather | solution.py:106
  42.3 18.6 %all-to-all-start = ((bf16[64,32,256]{2,1,0:T(8,128)(2,1)}), bf16[64,32,256]{2,1,0:T(8,128)(2,1)S(1)}, u32[]{:S(2)}, u32[]{:S(2)}) async-start(bf16[64,32,256]{2,1,0:T(8,128)(2,1)} %bitcast.9), calls=%async_computation | async-start | bytes 2097152 | tf_op jit(solution)/shard_map/all_to_all | solution.py:107
  61.8 8.0 %scatter_custom_fusion.1 = s32[1024]{0:T(1024)S(1)} fusion(s32[2048]{0:T(1024)S(1)} %bitcast.151, s32[2048]{0:T(1024)S(1)} %reshape.638, s32[]{:T(128)} %copy.68), kind=kCustom, calls=%fused_computation.100 | custom fusion | bytes 4100 | tf_op jit(solution)/shard_map/scatter | solution.py:115
  69.9 46.3 %all-to-all-done = bf16[64,32,256]{2,1,0:T(8,128)(2,1)S(1)} async-done(((bf16[64,32,256]{2,1,0:T(8,128)(2,1)}), bf16[64,32,256]{2,1,0:T(8,128)(2,1)S(1)}, u32[]{:S(2)}, u32[]{:S(2)}) %all-to-all-start) | async-done | bytes 1048608 | tf_op jit(solution)/shard_map/all_to_all | solution.py:107
  116.1 5.0 gather_fusion.1
  123.2 97.6 %all_gather.20 = bf16[2048,128]{1,0:T(8,128)(2,1)S(1)} all-gather(bf16[32,128]{1,0:T(8,128)(2,1)S(1)} %copy-done.4), channel_id=1, replica_groups=mesh['dp'=64,'fsdp'=8] {'dp'}, dimensions={0}, use_global_device_ids=true | all-gather | bytes 532480 | tf_op jit(solution)/shard_map/all_gather | solution.py:121
  220.9 99.2 %all_gather.21 = bf16[2048,128]{1,0:T(8,128)(2,1)S(1)} all-gather(bf16[32,128]{1,0:T(8,128)(2,1)S(1)} %copy-done.5), channel_id=1, replica_groups=mesh['dp'=64,'fsdp'=8] {'dp'}, dimensions={0}, use_global_device_ids=true | all-gather | bytes 532480 | tf_op jit(solution)/shard_map/all_gather | solution.py:122
  321.1 3.2 fusion.21
  330.4 3.8 multiply_reduce_fusion
  336.3 9.5 %while.12 = (s32[]{:T(128)}, bf16[2,512,1,2,128]{4,3,1,0,2:T(2,128)(2,1)S(1)}, s32[2,512]{1,0:T(2,128)S(1)}, s32[2,512]{1,0:T(2,128)S(1)}, bf16[2,512,1,2,128]{4...) while((s32[]{:T(128)}, ...), condition=%wide.region_15.16_spmd.clone.clone, body=%wide.region_12.15_spmd.clone.clone.sunk | while | flops 551155712 | bytes 16285793 | solution.py:158
  339.1 1.6 fusion.72
  343.9 1.6 fusion.72
  347.1 9.0 %gather_fusion.4 = bf16[2048,256]{1,0:T(8,128)(2,1)} fusion(bf16[1025,256]{1,0:T(8,128)(2,1)S(1)} %copy.44, s32[2048]{0:T(1024)S(1)} %broadcast_clamp_fusion), kind=kCustom, calls=%fused_computation.4 | custom fusion | bytes 2105344 | tf_op jit(solution)/shard_map/gather | solution.py:170
  356.1 6.9 %all-to-all-start.2 = ((bf16[64,32,1,256]{3,1,2,0:T(8,128)(2,1)}), bf16[64,32,1,256]{3,1,2,0:T(8,128)(2,1)S(1)}, u32[]{:S(2)}, u32[]{:S(2)}) async-start(bf16[64,32,1,256]{3,1,2,0:T(8,128)(2,1)} %bitcast.20), calls=%async_computation.2 | async-start | bytes 2097152 | tf_op jit(solution)/shard_map/all_to_all | solution.py:173
  363.0 77.8 %all-gather.10.cloned.1.call-done = bf16[2048,256]{1,0:T(8,128)(2,1)} async-done(((bf16[32,256]{1,0:T(8,128)(2,1)}), bf16[2048,256]{1,0:T(8,128)(2,1)}) %all-gather.10.cloned.1.call-update) | async-done | bytes 1048592 | tf_op jit(solution)/shard_map/all_gather | solution.py:123
  440.9 42.9 %all-gather.8.cloned.1.call-done = bf16[1024,2048]{1,0:T(8,128)(2,1)} async-done(((bf16[1024,256]{1,0:T(8,128)(2,1)}), bf16[1024,2048]{1,0:T(8,128)(2,1)}) %all-gather.8.cloned.1.call-update) | async-done | bytes 4194320 | tf_op jit(solution)/shard_map/all_gather | solution.py:167
  483.7 3.7 convolution_convert_fusion
  487.5 9.0 %gather_fusion.2 = bf16[2048,256]{1,0:T(8,128)(2,1)} fusion(bf16[1025,256]{1,0:T(8,128)(2,1)S(1)} %concatenate.45, s32[2048]{0:T(1024)S(1)} %broadcast_clamp_fusion), kind=kCustom, calls=%fused_computation.2 | custom fusion | bytes 2105344 | tf_op jit(solution)/shard_map/gather | solution.py:170
  496.5 15.7 %all-to-all-start.1 = ((bf16[64,32,256]{2,1,0:T(8,128)(2,1)}), bf16[64,32,256]{2,1,0:T(8,128)(2,1)S(1)}, u32[]{:S(2)}, u32[]{:S(2)}) async-start(bf16[64,32,256]{2,1,0:T(8,128)(2,1)} %bitcast.16), calls=%async_computation.1 | async-start | bytes 2097152 | tf_op jit(solution)/shard_map/all_to_all | solution.py:173
  512.2 5.0 gather_fusion.5
  517.2 50.6 %all-to-all-done.1 = bf16[64,32,256]{2,1,0:T(8,128)(2,1)S(1)} async-done(((bf16[64,32,256]{2,1,0:T(8,128)(2,1)}), bf16[64,32,256]{2,1,0:T(8,128)(2,1)S(1)}, u32[]{:S(2)}, u32[]{:S(2)}) %all-to-all-start.1) | async-done | bytes 1048608 | tf_op jit(solution)/shard_map/all_to_all | solution.py:173
  567.8 5.0 gather_fusion.3
  (111 shorter events, 23.1 us)
Async XLA Ops:
  7.2 115.5 %copy-start = (s32[64,8]{0,1:T(8,128)S(1)}, s32[64,8]{0,1:T(8,128)}, u32[]{:S(2)}) copy-start(s32[64,8]{0,1:T(8,128)} %param.20) | copy-start | bytes 6148
  33.2 27.7 %copy-start.3 = (s32[64,64]{1,0:T(8,128)S(1)}, s32[64,64]{1,0:T(8,128)}, u32[]{:S(2)}) copy-start(s32[64,64]{1,0:T(8,128)} %param.21) | copy-start | bytes 49156
  42.3 80.9 %copy-start.6 = (bf16[2048]{0:T(1024)(128)(2,1)S(1)}, bf16[2048]{0:T(1024)(128)(2,1)}, u32[]{:S(2)}) copy-start(bf16[2048]{0:T(1024)(128)(2,1)} %param.13) | copy-start | bytes 12292
  42.3 80.9 %copy-start.4 = (bf16[32,128]{1,0:T(8,128)(2,1)S(1)}, bf16[32,128]{1,0:T(8,128)(2,1)}, u32[]{:S(2)}) copy-start(bf16[32,128]{1,0:T(8,128)(2,1)} %param.17) | copy-start | bytes 24580
  42.3 178.6 %copy-start.7 = (bf16[128]{0:T(256)(128)(2,1)S(1)}, bf16[128]{0:T(256)(128)(2,1)}, u32[]{:S(2)}) copy-start(bf16[128]{0:T(256)(128)(2,1)} %param.15) | copy-start | bytes 772
  42.3 178.6 %copy-start.5 = (bf16[32,128]{1,0:T(8,128)(2,1)S(1)}, bf16[32,128]{1,0:T(8,128)(2,1)}, u32[]{:S(2)}) copy-start(bf16[32,128]{1,0:T(8,128)(2,1)} %param.18) | copy-start | bytes 24580
  42.3 277.8 %copy-start.8 = (bf16[128]{0:T(256)(128)(2,1)S(1)}, bf16[128]{0:T(256)(128)(2,1)}, u32[]{:S(2)}) copy-start(bf16[128]{0:T(256)(128)(2,1)} %param.14) | copy-start | bytes 772
  42.3 73.9 %all-to-all-start = ((bf16[64,32,256]{2,1,0:T(8,128)(2,1)}), bf16[64,32,256]{2,1,0:T(8,128)(2,1)S(1)}, u32[]{:S(2)}, u32[]{:S(2)}) async-start(bf16[64,32,256]{2,1,0:T(8,128)(2,1)} %bitcast.9), calls=%async_computation | async-start | bytes 2097152 | tf_op jit(solution)/shard_map/all_to_all | solution.py:107
  60.9 260.2 %all-gather.12.cloned.1.call-start = ((), (), s32[]{:S(2)}) async-start(), calls=%async_computation.6 | async-start | bytes 4718592 | tf_op jit(solution)/shard_map/all_gather | solution.py:118
  121.1 209.2 %all-gather.6.cloned.1.call-start = ((), (), s32[]{:S(2)}) async-start(), calls=%async_computation.3 | async-start | bytes 1064960 | tf_op jit(solution)/shard_map/all_gather | solution.py:120
  121.9 319.0 %all-gather.10.cloned.1.call-start = ((), (), s32[]{:S(2)}) async-start(), calls=%async_computation.5 | async-start | bytes 1064960 | tf_op jit(solution)/shard_map/all_gather | solution.py:123
  122.6 361.1 %all-gather.8.cloned.1.call-start = ((), (), s32[]{:S(2)}) async-start(), calls=%async_computation.4 | async-start | bytes 4718592 | tf_op jit(solution)/shard_map/all_gather | solution.py:167
  321.1 3.5 copy-start.2
  325.6 4.5 copy-start.1
  356.1 140.4 %all-to-all-start.2 = ((bf16[64,32,1,256]{3,1,2,0:T(8,128)(2,1)}), bf16[64,32,1,256]{3,1,2,0:T(8,128)(2,1)S(1)}, u32[]{:S(2)}, u32[]{:S(2)}) async-start(bf16[64,32,1,256]{3,1,2,0:T(8,128)(2,1)} %bitcast.20), calls=%async_computation.2 | async-start | bytes 2097152 | tf_op jit(solution)/shard_map/all_to_all | solution.py:173
  496.5 71.3 %all-to-all-start.1 = ((bf16[64,32,256]{2,1,0:T(8,128)(2,1)}), bf16[64,32,256]{2,1,0:T(8,128)(2,1)S(1)}, u32[]{:S(2)}, u32[]{:S(2)}) async-start(bf16[64,32,256]{2,1,0:T(8,128)(2,1)} %bitcast.16), calls=%async_computation.1 | async-start | bytes 2097152 | tf_op jit(solution)/shard_map/all_to_all | solution.py:173
Sparse Core Ops, SparseCore 0:
  121.3 34.7 all-gather.11
  159.0 139.8 all-gather.5
  301.9 138.9 all-gather.9
  443.4 40.2 all-gather.7
where the time goes:
time: 580 us; the launch traced here: 579 us
  waiting for transfers between devices  219 us (38%)
  blocking collectives  197 us (34%)
  local copies, waits for them, and re-layouts  60.6 us (10%)
  starting transfers between devices  41.4 us (7%)
  other arithmetic  31.2 us (5%)
  matrix products  15.8 us (3%)
  between operations  14.3 us (2%)
    all_gather x1, blocking collectives, local(): lax.all_gather(w_value, 'dp', axis=0, tiled=True)  99.2 us
    all_gather x1, blocking collectives, local(): lax.all_gather(w_key, 'dp', axis=0, tiled=True)  97.6 us
    all_gather x1, waiting for transfers between devices, local(): lax.all_gather(w_out, 'dp', axis=0, tiled=True)  77.8 us
    all_to_all x2, waiting for transfers between devices, local(): lax.all_to_all(for_sending(sent), 'dp', split_axis=0, concat_axis=0, tile...  50.6 us
    all_to_all x1, waiting for transfers between devices, local(): lax.all_to_all(outgoing, 'dp', split_axis=0, concat_axis=0, tiled=True)  46.3 us
    all_gather x1, waiting for transfers between devices, local(): heads_all = lax.all_gather(mixed, 'fsdp', axis=1, tiled=True)  42.9 us
    all_to_all x2, starting transfers between devices, local(): lax.all_to_all(for_sending(sent), 'dp', split_axis=0, concat_axis=0, tile...  22.6 us
    another operation x7, other arithmetic  19.9 us
  transfers between devices with their start and end apart: 7, of which 4 were waited for; matrix products, arithmetic and copies ran while one was open for 11% of the time, Pallas kernels for 0%

commit v1 on v0

--- a/solution.py
+++ b/solution.py
@@ -3,11 +3,12 @@
 import jax
 import jax.numpy as jnp
 from jax import lax
-from jax.sharding import PartitionSpec as P
+from jax.sharding import Mesh, PartitionSpec as P
 
 QH = 16
 KVH = 8
 HD = 128
+DP = ("z", "y")
 
 
 epsilon = 1e-06
@@ -85,10 +86,10 @@
     span_group,
 ):
     group_rows, width_local = tokens.shape
-    groups = lax.axis_size("dp")
+    groups = lax.axis_size(DP)
     arrival_rows = group_rows // groups
     capacity = 2 * arrival_rows
-    device_index = lax.axis_index("dp")
+    device_index = lax.axis_index(DP)
     group_ids = jnp.arange(groups, dtype=jnp.int32)
     slot_ids = jnp.arange(capacity, dtype=jnp.int32)
     own_blocks = lax.dynamic_index_in_dim(span_group, device_index, 0, keepdims=False)
@@ -104,7 +105,7 @@
         .set(jnp.arange(group_rows, dtype=jnp.int32))
     )
     outgoing = with_zero_row(tokens)[slot_source].reshape(groups, capacity, width_local)
-    incoming = lax.all_to_all(outgoing, "dp", split_axis=0, concat_axis=0, tiled=True)
+    incoming = lax.all_to_all(outgoing, DP, split_axis=0, concat_axis=0, tiled=True)
     is_valid = slot_ids[None, :] < arrival_rows * counts[:, None]
     target = arrival_rows * offsets[:, None] + slot_ids[None, :]
     flat_slot = group_ids[:, None] * capacity + slot_ids[None, :]
@@ -116,11 +117,13 @@
     )
     arrived = incoming.reshape(groups * capacity, width_local)[source_of]
     full_rows = lax.all_gather(arrived, "fsdp", axis=1, tiled=True)
+    weights = jnp.concatenate([w_query, w_key, w_value, w_out], axis=1)
+    weights = lax.all_gather(weights, "y", axis=0, tiled=True)
+    weights = lax.all_gather(weights, "z", axis=0, tiled=True)
+    cuts = [w_query.shape[1], w_key.shape[1], w_value.shape[1], w_out.shape[1]]
+    bounds = [sum(cuts[:k]) for k in range(5)]
     query_full, key_full, value_full, out_full = (
-        lax.all_gather(w_query, "dp", axis=0, tiled=True),
-        lax.all_gather(w_key, "dp", axis=0, tiled=True),
-        lax.all_gather(w_value, "dp", axis=0, tiled=True),
-        lax.all_gather(w_out, "dp", axis=0, tiled=True),
+        weights[:, bounds[k] : bounds[k + 1]] for k in range(4)
     )
     lengths = lax.dynamic_index_in_dim(prompt_lengths, device_index, 0, keepdims=False)
     position, starts = prompt_layout(lengths, group_rows)
@@ -170,7 +173,7 @@
     sent = tuple((with_zero_row(array)[back_index] for array in arrays))
     back = jax.tree.map(
         lambda part, own: part.astype(own.dtype),
-        lax.all_to_all(for_sending(sent), "dp", split_axis=0, concat_axis=0, tiled=True),
+        lax.all_to_all(for_sending(sent), DP, split_axis=0, concat_axis=0, tiled=True),
         sent,
     )
     attention_out, cache_out = tuple(
@@ -180,21 +183,23 @@
 
 
 def solution(mesh):
+    z_size = mesh.shape["dp"] // 4
+    fine = Mesh(mesh.devices.reshape(z_size, 4, mesh.shape["fsdp"]), ("z", "y", "fsdp"))
     return jax.shard_map(
         local,
-        mesh=mesh,
+        mesh=fine,
         in_specs=(
-            P("dp", "fsdp"),
-            P(),
-            P(),
-            P(),
-            P("dp", "fsdp"),
-            P("dp", "fsdp"),
-            P("dp", "fsdp"),
-            P("dp", "fsdp"),
+            P(DP, "fsdp"),
+            P(),
+            P(),
+            P(),
+            P(DP, "fsdp"),
+            P(DP, "fsdp"),
+            P(DP, "fsdp"),
+            P(DP, "fsdp"),
             P(),
             P(),
         ),
-        out_specs=(P("dp", "fsdp"), P("dp", "fsdp", None)),
+        out_specs=(P(DP, "fsdp"), P(DP, "fsdp", None)),
         check_vma=False,
     )

time: 580 us -> 397 us (0.68)
  blocking collectives: 197 us -> 12.9 us
    all_gather x2 -> x1, blocking collectives: 197 us -> 12.9 us  [local(): weights = lax.all_gather(weights, 'y', axis=0, tiled=True)]
    all_gather x1, waiting for transfers between devices: 42.9 us -> 19.5 us  [local(): heads_all = lax.all_gather(mixed, 'fsdp', axis=1, tiled=True)]
    all_gather x1, waiting for transfers between devices: 0.02 us -> 20.3 us  [local(): full_rows = lax.all_gather(arrived, 'fsdp', axis=1, tiled=True)]
    all_to_all x3, waiting for transfers between devices: 96.9 us -> 107 us  [the longest x2 60.4 us: local(): lax.all_to_all(for_sending(sent), DP, split_axis=0, concat_axis=0, tiled=...]
    all_gather x2 -> x1, waiting for transfers between devices: 77.8 us -> 72.2 us  [local(): weights = lax.all_gather(weights, 'z', axis=0, tiled=True)]
  transfers between devices with their start and end apart: 7 -> 6, of which waited for: 4 -> 6; matrix products, arithmetic and copies ran while one was open for 11% -> 11% of each run, Pallas kernels for 0% -> 0%
where the time goes in v1:
time: 397 us; the launch traced here: 396 us
  waiting for transfers between devices  219 us (55%)
  local copies, waits for them, and re-layouts  60.8 us (15%)
  starting transfers between devices  35.9 us (9%)
  other arithmetic  33 us (8%)
  matrix products  20.4 us (5%)
  between operations  14.3 us (4%)
  blocking collectives  12.9 us (3%)
    all_gather x1, waiting for transfers between devices, local(): weights = lax.all_gather(weights, 'z', axis=0, tiled=True)  72.2 us
    all_to_all x2, waiting for transfers between devices, local(): lax.all_to_all(for_sending(sent), DP, split_axis=0, concat_axis=0, tiled=...  60.4 us
    all_to_all x1, waiting for transfers between devices, local(): lax.all_to_all(outgoing, DP, split_axis=0, concat_axis=0, tiled=True)  46.3 us
    all_gather x1, waiting for transfers between devices, local(): full_rows = lax.all_gather(arrived, 'fsdp', axis=1, tiled=True)  20.3 us
    another operation x7, other arithmetic  19.8 us
    all_gather x1, waiting for transfers between devices, local(): heads_all = lax.all_gather(mixed, 'fsdp', axis=1, tiled=True)  19.5 us
    all_to_all x1, starting transfers between devices, local(): lax.all_to_all(outgoing, DP, split_axis=0, concat_axis=0, tiled=True)  18.6 us
    gather x2, local copies, waits for them, and re-layouts, local(): sent = tuple((with_zero_row(array)[back_index] for array in arrays))  18 us
  transfers between devices with their start and end apart: 6, of which 6 were waited for; matrix products, arithmetic and copies ran while one was open for 11% of the time, Pallas kernels for 0%

profile of v1, /device:TPU:24, one launch (start us, length us, event | category | flops | bytes accessed | tf_op | source)
XLA Modules:
  0.0 396.1 jit_solution(274333781366797643)
XLA Ops:
  9.0 18.0 %reduce-window.24 = s32[64,8,128]{2,1,0:T(8,128)S(1)} reduce-window(s32[64,8,128]{2,1,0:T(8,128)S(1)} %fusion.47, s32[]{:T(128)} %copy.68), window={size=1x1x128 pad=0_0x0_0x127_0}, to_apply=%region_0.1 | reduce-window | flops 8323072 | bytes 524292 | tf_op jit(solution)/shard_map/reduce-window
  27.8 4.3 %scatter_custom_fusion = s32[2048]{0:T(1024)S(1)} fusion(s32[1024]{0:T(1024)S(1)} %bitcast.145, s32[1024]{0:T(1024)S(1)} %iota.56, s32[]{:T(128)} %constant.37.clone.1), kind=kCustom, calls=%fused_computation.103 | custom fusion | bytes 8196 | tf_op jit(solution)/shard_map/scatter | solution.py:105
  33.3 9.0 %gather_fusion = bf16[2048,256]{1,0:T(8,128)(2,1)} fusion(bf16[1025,256]{1,0:T(8,128)(2,1)S(1)} %concatenate.43, s32[2048]{0:T(1024)S(1)} %fusion.49), kind=kCustom, calls=%fused_computation | custom fusion | bytes 2105344 | tf_op jit(solution)/shard_map/gather | solution.py:107
  42.3 18.6 %all-to-all-start = ((bf16[64,32,256]{2,1,0:T(8,128)(2,1)}), bf16[64,32,256]{2,1,0:T(8,128)(2,1)S(1)}, u32[]{:S(2)}, u32[]{:S(2)}) async-start(bf16[64,32,256]{2,1,0:T(8,128)(2,1)} %bitcast.9), calls=%async_computation | async-start | bytes 2097152 | tf_op jit(solution)/shard_map/all_to_all | solution.py:108
  61.8 8.0 %scatter_custom_fusion.1 = s32[1024]{0:T(1024)S(1)} fusion(s32[2048]{0:T(1024)S(1)} %bitcast.147, s32[2048]{0:T(1024)S(1)} %reshape.638, s32[]{:T(128)} %copy.68), kind=kCustom, calls=%fused_computation.107 | custom fusion | bytes 4100 | tf_op jit(solution)/shard_map/scatter | solution.py:116
  69.9 46.3 %all-to-all-done = bf16[64,32,256]{2,1,0:T(8,128)(2,1)S(1)} async-done(((bf16[64,32,256]{2,1,0:T(8,128)(2,1)}), bf16[64,32,256]{2,1,0:T(8,128)(2,1)S(1)}, u32[]{:S(2)}, u32[]{:S(2)}) %all-to-all-start) | async-done | bytes 1048608 | tf_op jit(solution)/shard_map/all_to_all | solution.py:108
  116.2 5.0 %gather_fusion.1 = bf16[1024,256]{1,0:T(8,128)(2,1)} fusion(bf16[2048,256]{1,0:T(8,128)(2,1)S(1)} %bitcast.134, s32[1024]{0:T(1024)S(1)} %fusion.50), kind=kCustom, calls=%fused_computation.1 | custom fusion | bytes 1052672 | tf_op jit(solution)/shard_map/gather | solution.py:118
  121.3 12.9 %all_gather.13 = bf16[128,768]{1,0:T(8,128)(2,1)} all-gather(bf16[32,768]{1,0:T(8,128)(2,1)S(1)} %pad_maximum_fusion.2), channel_id=1, replica_groups=mesh['z'=16,'y'=4,'fsdp'=8] {'y'}, dimensions={0}, use_global_device_ids=true | all-gather | bytes 245760 | tf_op jit(solution)/shard_map/all_gather | solution.py:121
  135.8 20.3 %all-gather.9.cloned.1.call-done = bf16[1024,2048]{1,0:T(8,128)(2,1)} async-done(((bf16[1024,256]{1,0:T(8,128)(2,1)}), bf16[1024,2048]{1,0:T(8,128)(2,1)}) %all-gather.9.cloned.1.call-update) | async-done | bytes 4194320 | tf_op jit(solution)/shard_map/all_gather | solution.py:119
  162.5 72.2 %all-gather.5.cloned.1.call-done = bf16[2048,768]{1,0:T(8,128)(2,1)} async-done(((bf16[128,768]{1,0:T(8,128)(2,1)}), bf16[2048,768]{1,0:T(8,128)(2,1)}) %all-gather.5.cloned.1.call-update) | async-done | bytes 3145744 | tf_op jit(solution)/shard_map/all_gather | solution.py:122
  234.7 3.8 multiply_reduce_fusion
  240.6 3.8 multiply_reduce_fusion.1
  245.9 3.8 fusion.27
  249.9 9.5 %while.12 = (s32[]{:T(128)}, bf16[2,512,1,2,128]{4,3,1,0,2:T(2,128)(2,1)S(1)}, s32[2,512]{1,0:T(2,128)S(1)}, s32[2,512]{1,0:T(2,128)S(1)}, bf16[2,512,1,2,128]{4...) while((s32[]{:T(128)}, ...), condition=%wide.region_15.16_spmd.clone.clone, body=%wide.region_12.15_spmd.clone.clone.sunk | while | flops 551155712 | bytes 16285801 | solution.py:161
  260.8 9.0 %gather_fusion.4 = bf16[2048,256]{1,0:T(8,128)(2,1)} fusion(bf16[1025,256]{1,0:T(8,128)(2,1)S(1)} %copy.44, s32[2048]{0:T(1024)S(1)} %broadcast_clamp_fusion), kind=kCustom, calls=%fused_computation.4 | custom fusion | bytes 2105344 | tf_op jit(solution)/shard_map/gather | solution.py:173
  269.8 11.2 %all-to-all-start.2 = ((bf16[64,32,1,256]{3,1,2,0:T(8,128)(2,1)}), bf16[64,32,1,256]{3,1,2,0:T(8,128)(2,1)S(1)}, u32[]{:S(2)}, u32[]{:S(2)}) async-start(bf16[64,32,1,256]{3,1,2,0:T(8,128)(2,1)} %bitcast.20), calls=%async_computation.2 | async-start | bytes 2097152 | tf_op jit(solution)/shard_map/all_to_all | solution.py:176
  281.0 19.5 %all-gather.7.cloned.1.call-done = bf16[1024,2048]{1,0:T(8,128)(2,1)} async-done(((bf16[1024,256]{1,0:T(8,128)(2,1)}), bf16[1024,2048]{1,0:T(8,128)(2,1)}) %all-gather.7.cloned.1.call-update) | async-done | bytes 4194320 | tf_op jit(solution)/shard_map/all_gather | solution.py:170
  300.5 3.7 convolution_convert_fusion
  304.3 9.0 %gather_fusion.2 = bf16[2048,256]{1,0:T(8,128)(2,1)} fusion(bf16[1025,256]{1,0:T(8,128)(2,1)S(1)} %concatenate.49, s32[2048]{0:T(1024)S(1)} %broadcast_clamp_fusion), kind=kCustom, calls=%fused_computation.2 | custom fusion | bytes 2105344 | tf_op jit(solution)/shard_map/gather | solution.py:173
  313.3 13.1 %all-to-all-done.2 = bf16[64,32,1,256]{3,1,2,0:T(8,128)(2,1)S(1)} async-done(((bf16[64,32,1,256]{3,1,2,0:T(8,128)(2,1)}), bf16[64,32,1,256]{3,1,2,0:T(8,128)(2,1)S(1)}, u32[]{:S(2)}, u32[]{:S(2)}) %all-to-all-start.2) | async-done | bytes 1048608 | tf_op jit(solution)/shard_map/all_to_all | solution.py:176
  326.4 5.9 %all-to-all-start.1 = ((bf16[64,32,256]{2,1,0:T(8,128)(2,1)}), bf16[64,32,256]{2,1,0:T(8,128)(2,1)S(1)}, u32[]{:S(2)}, u32[]{:S(2)}) async-start(bf16[64,32,256]{2,1,0:T(8,128)(2,1)} %bitcast.16), calls=%async_computation.1 | async-start | bytes 2097152 | tf_op jit(solution)/shard_map/all_to_all | solution.py:176
  332.3 5.0 %gather_fusion.5 = bf16[1024,256]{1,0:T(8,128)(2,1)} fusion(bf16[2048,256]{1,0:T(8,128)(2,1)S(1)} %bitcast.135, s32[1024]{0:T(1024)S(1)} %broadcast_clamp_fusion.1), kind=kCustom, calls=%fused_computation.5 | custom fusion | bytes 1052672 | tf_op jit(solution)/shard_map/gather | solution.py:180
  337.3 47.2 %all-to-all-done.1 = bf16[64,32,256]{2,1,0:T(8,128)(2,1)S(1)} async-done(((bf16[64,32,256]{2,1,0:T(8,128)(2,1)}), bf16[64,32,256]{2,1,0:T(8,128)(2,1)S(1)}, u32[]{:S(2)}, u32[]{:S(2)}) %all-to-all-start.1) | async-done | bytes 1048608 | tf_op jit(solution)/shard_map/all_to_all | solution.py:176
  384.6 5.0 %gather_fusion.3 = bf16[1024,256]{1,0:T(8,128)(2,1)} fusion(bf16[2048,256]{1,0:T(8,128)(2,1)S(1)} %bitcast.136, s32[1024]{0:T(1024)S(1)} %broadcast_clamp_fusion.1), kind=kCustom, calls=%fused_computation.3 | custom fusion | bytes 1052672 | tf_op jit(solution)/shard_map/gather | solution.py:180
  (110 shorter events, 26.9 us)
Async XLA Ops:
  7.2 127.1 %copy-start = (s32[64,8]{0,1:T(8,128)S(1)}, s32[64,8]{0,1:T(8,128)}, u32[]{:S(2)}) copy-start(s32[64,8]{0,1:T(8,128)} %param.20) | copy-start | bytes 6148
  33.3 27.8 %copy-start.2 = (s32[64,64]{1,0:T(8,128)S(1)}, s32[64,64]{1,0:T(8,128)}, u32[]{:S(2)}) copy-start(s32[64,64]{1,0:T(8,128)} %param.21) | copy-start | bytes 49156
  42.3 79.0 %copy-start.3 = (bf16[32,256]{1,0:T(8,128)(2,1)S(1)}, bf16[32,256]{1,0:T(8,128)(2,1)}, u32[]{:S(2)}) copy-start(bf16[32,256]{1,0:T(8,128)(2,1)} %param.19) | copy-start | bytes 49156
  42.3 79.0 %copy-start.4 = (bf16[32,256]{1,0:T(8,128)(2,1)S(1)}, bf16[32,256]{1,0:T(8,128)(2,1)}, u32[]{:S(2)}) copy-start(bf16[32,256]{1,0:T(8,128)(2,1)} %param.16) | copy-start | bytes 49156
  42.3 79.0 %copy-start.5 = (bf16[32,128]{1,0:T(8,128)(2,1)S(1)}, bf16[32,128]{1,0:T(8,128)(2,1)}, u32[]{:S(2)}) copy-start(bf16[32,128]{1,0:T(8,128)(2,1)} %param.18) | copy-start | bytes 24580
  42.3 79.0 %copy-start.6 = (bf16[32,128]{1,0:T(8,128)(2,1)S(1)}, bf16[32,128]{1,0:T(8,128)(2,1)}, u32[]{:S(2)}) copy-start(bf16[32,128]{1,0:T(8,128)(2,1)} %param.17) | copy-start | bytes 24580
  42.3 92.4 %copy-start.8 = (bf16[128]{0:T(256)(128)(2,1)S(1)}, bf16[128]{0:T(256)(128)(2,1)}, u32[]{:S(2)}) copy-start(bf16[128]{0:T(256)(128)(2,1)} %param.14) | copy-start | bytes 772
  42.3 92.4 %copy-start.7 = (bf16[2048]{0:T(1024)(128)(2,1)S(1)}, bf16[2048]{0:T(1024)(128)(2,1)}, u32[]{:S(2)}) copy-start(bf16[2048]{0:T(1024)(128)(2,1)} %param.13) | copy-start | bytes 12292
  42.3 92.4 %copy-start.9 = (bf16[128]{0:T(256)(128)(2,1)S(1)}, bf16[128]{0:T(256)(128)(2,1)}, u32[]{:S(2)}) copy-start(bf16[128]{0:T(256)(128)(2,1)} %param.15) | copy-start | bytes 772
  42.3 73.9 %all-to-all-start = ((bf16[64,32,256]{2,1,0:T(8,128)(2,1)}), bf16[64,32,256]{2,1,0:T(8,128)(2,1)S(1)}, u32[]{:S(2)}, u32[]{:S(2)}) async-start(bf16[64,32,256]{2,1,0:T(8,128)(2,1)} %bitcast.9), calls=%async_computation | async-start | bytes 2097152 | tf_op jit(solution)/shard_map/all_to_all | solution.py:108
  61.0 95.2 %all-gather.9.cloned.1.call-start = ((), (), s32[]{:S(2)}) async-start(), calls=%async_computation.5 | async-start | bytes 4718592 | tf_op jit(solution)/shard_map/all_gather | solution.py:119
  121.2 113.5 %all-gather.5.cloned.1.call-start = ((), (), s32[]{:S(2)}) async-start(), calls=%async_computation.3 | async-start | bytes 3342336 | tf_op jit(solution)/shard_map/all_gather | solution.py:122
  134.2 166.3 %all-gather.7.cloned.1.call-start = ((), (), s32[]{:S(2)}) async-start(), calls=%async_computation.4 | async-start | bytes 4718592 | tf_op jit(solution)/shard_map/all_gather | solution.py:170
  156.1 3.4 copy-start.1
  269.8 56.6 %all-to-all-start.2 = ((bf16[64,32,1,256]{3,1,2,0:T(8,128)(2,1)}), bf16[64,32,1,256]{3,1,2,0:T(8,128)(2,1)S(1)}, u32[]{:S(2)}, u32[]{:S(2)}) async-start(bf16[64,32,1,256]{3,1,2,0:T(8,128)(2,1)} %bitcast.20), calls=%async_computation.2 | async-start | bytes 2097152 | tf_op jit(solution)/shard_map/all_to_all | solution.py:176
  326.4 58.2 %all-to-all-start.1 = ((bf16[64,32,256]{2,1,0:T(8,128)(2,1)}), bf16[64,32,256]{2,1,0:T(8,128)(2,1)S(1)}, u32[]{:S(2)}, u32[]{:S(2)}) async-start(bf16[64,32,256]{2,1,0:T(8,128)(2,1)} %bitcast.16), calls=%async_computation.1 | async-start | bytes 2097152 | tf_op jit(solution)/shard_map/all_to_all | solution.py:176
Sparse Core Ops, SparseCore 0:
  121.3 34.7 all-gather.8
  158.2 76.4 all-gather.4
  260.4 39.9 all-gather.6

commit v2 on v1

--- a/solution.py
+++ b/solution.py
@@ -67,10 +67,6 @@
     return jnp.einsum(
         "krqs,skd->qkrd", probs, value_rows, preferred_element_type=jnp.float32
     ).astype(jnp.bfloat16)
-
-
-def with_zero_row(array):
-    return jnp.concatenate([array, jnp.zeros((1,) + array.shape[1:], array.dtype)], axis=0)
 
 
 def local(
@@ -88,38 +84,40 @@
     group_rows, width_local = tokens.shape
     groups = lax.axis_size(DP)
     arrival_rows = group_rows // groups
-    capacity = 2 * arrival_rows
     device_index = lax.axis_index(DP)
-    group_ids = jnp.arange(groups, dtype=jnp.int32)
-    slot_ids = jnp.arange(capacity, dtype=jnp.int32)
+    block_ids = jnp.arange(groups, dtype=jnp.int32)
+
+    weights = jnp.concatenate([w_query, w_key, w_value, w_out], axis=1)
+    weights = lax.all_gather(weights, "y", axis=0, tiled=True)
+    weights, tokens = lax.optimization_barrier((weights, tokens))
+    weights = lax.all_gather(weights, "z", axis=0, tiled=True)
+
     own_blocks = lax.dynamic_index_in_dim(span_group, device_index, 0, keepdims=False)
+    same = own_blocks[:, None] == own_blocks[None, :]
+    dup_rank = jnp.sum(same & (block_ids[None, :] < block_ids[:, None]), axis=1).astype(jnp.int32)
+    send_slot = own_blocks * 2 + dup_rank
+    slot_source = jnp.zeros((groups * 2,), jnp.int32).at[send_slot].set(block_ids)
+    token_blocks = tokens.reshape(groups, arrival_rows, width_local)
+    outgoing = jnp.take(token_blocks, slot_source, axis=0, mode="clip").reshape(
+        groups, 2 * arrival_rows, width_local
+    )
+    incoming = lax.all_to_all(outgoing, DP, split_axis=0, concat_axis=0, tiled=True)
     counts = jnp.sum((span_group == device_index).astype(jnp.int32), axis=1)
     offsets = jnp.cumsum(counts) - counts
-    row_dest = jnp.repeat(own_blocks, arrival_rows)
-    onehot = (row_dest[:, None] == group_ids[None, :]).astype(jnp.int32)
-    slot_rank = jnp.sum((jnp.cumsum(onehot, axis=0) - 1) * onehot, axis=1)
-    send_slot = row_dest * capacity + slot_rank
-    slot_source = (
-        jnp.full((groups * capacity,), group_rows, jnp.int32)
-        .at[send_slot]
-        .set(jnp.arange(group_rows, dtype=jnp.int32))
-    )
-    outgoing = with_zero_row(tokens)[slot_source].reshape(groups, capacity, width_local)
-    incoming = lax.all_to_all(outgoing, DP, split_axis=0, concat_axis=0, tiled=True)
-    is_valid = slot_ids[None, :] < arrival_rows * counts[:, None]
-    target = arrival_rows * offsets[:, None] + slot_ids[None, :]
-    flat_slot = group_ids[:, None] * capacity + slot_ids[None, :]
-    back_index = jnp.where(is_valid, target, group_rows)
+    sub_ids = jnp.arange(2, dtype=jnp.int32)
+    is_valid = sub_ids[None, :] < counts[:, None]
+    back_index = jnp.where(is_valid, offsets[:, None] + sub_ids[None, :], groups)
+    flat_slot = block_ids[:, None] * 2 + sub_ids[None, :]
     source_of = (
-        jnp.zeros((group_rows,), jnp.int32)
+        jnp.zeros((groups,), jnp.int32)
         .at[back_index.reshape(-1)]
         .set(flat_slot.reshape(-1), mode="drop")
     )
-    arrived = incoming.reshape(groups * capacity, width_local)[source_of]
+    arrived = jnp.take(
+        incoming.reshape(groups * 2, arrival_rows, width_local), source_of, axis=0, mode="clip"
+    ).reshape(group_rows, width_local)
+    arrived, weights = lax.optimization_barrier((arrived, weights))
     full_rows = lax.all_gather(arrived, "fsdp", axis=1, tiled=True)
-    weights = jnp.concatenate([w_query, w_key, w_value, w_out], axis=1)
-    weights = lax.all_gather(weights, "y", axis=0, tiled=True)
-    weights = lax.all_gather(weights, "z", axis=0, tiled=True)
     cuts = [w_query.shape[1], w_key.shape[1], w_value.shape[1], w_out.shape[1]]
     bounds = [sum(cuts[:k]) for k in range(5)]
     query_full, key_full, value_full, out_full = (
@@ -169,16 +167,18 @@
     mixed = mixed.reshape(group_rows, kv_heads * group_ratio * HD)
     heads_all = lax.all_gather(mixed, "fsdp", axis=1, tiled=True)
     update = jnp.dot(heads_all, out_full, preferred_element_type=jnp.float32).astype(jnp.bfloat16)
-    arrays = (update, cache_rows)
-    sent = tuple((with_zero_row(array)[back_index] for array in arrays))
-    back = jax.tree.map(
-        lambda part, own: part.astype(own.dtype),
-        lax.all_to_all(for_sending(sent), DP, split_axis=0, concat_axis=0, tiled=True),
-        sent,
-    )
-    attention_out, cache_out = tuple(
-        (piece.reshape((groups * capacity,) + piece.shape[2:])[send_slot] for piece in back)
-    )
+    cache_flat = cache_rows.reshape(group_rows, -1)
+    update_width = update.shape[1]
+    joined = jnp.concatenate([update, cache_flat], axis=1).reshape(groups, arrival_rows, -1)
+    sent = jnp.take(joined, back_index.reshape(-1), axis=0, mode="clip").reshape(
+        groups, 2 * arrival_rows, -1
+    )
+    back = lax.all_to_all(sent, DP, split_axis=0, concat_axis=0, tiled=True)
+    mine = jnp.take(
+        back.reshape(groups * 2, arrival_rows, -1), send_slot, axis=0, mode="clip"
+    ).reshape(group_rows, -1)
+    attention_out = mine[:, :update_width]
+    cache_out = mine[:, update_width:].reshape(cache_rows.shape)
     return (attention_out, cache_out)
 
 

time: 397 us -> 380 us (0.957)
  waiting for transfers between devices: 219 us -> 274 us
  local copies, waits for them, and re-layouts: 60.8 us -> 16.6 us
  other arithmetic: 33 us -> 14.1 us
  matrix products: 20.4 us -> 13 us
  starting transfers between devices: 35.9 us -> 31.8 us
    all_gather x1, waiting for transfers between devices: 72.2 us -> 27.6 us  [local(): weights = lax.all_gather(weights, 'z', axis=0, tiled=True)]
    all_to_all x2 -> x1, waiting for transfers between devices: 60.4 us -> 101 us  [local(): back = lax.all_to_all(sent, DP, split_axis=0, concat_axis=0, tiled=True)]
    gather x6 -> x4, local copies, waits for them, and re-layouts: 41.9 us -> 6.65 us  [the longest x1 2.03 us: local(): jnp.take(joined, back_index.reshape(-1), axis=0, mode='clip')]
    all_gather x1, waiting for transfers between devices: 19.5 us -> 43.8 us  [local(): heads_all = lax.all_gather(mixed, 'fsdp', axis=1, tiled=True)]
    all_gather x1, waiting for transfers between devices: 20.3 us -> 40.1 us  [local(): full_rows = lax.all_gather(arrived, 'fsdp', axis=1, tiled=True)]
    another operation x7 -> x5, other arithmetic: 19.8 us -> 1.91 us
    all_to_all x1, waiting for transfers between devices: 46.3 us -> 62 us  [local(): lax.all_to_all(outgoing, DP, split_axis=0, concat_axis=0, tiled=True)]
    scatter x2, local copies, waits for them, and re-layouts: 12.4 us -> 1.75 us  [the longest x1 0.98 us: local(): source_of = jnp.zeros((groups,), jnp.int32).at[back_index.reshape(-1)].se...]
  transfers between devices with their start and end apart: 6 -> 5, of which waited for: 6 -> 5; matrix products, arithmetic and copies ran while one was open for 11% -> 2% of each run, Pallas kernels for 0% -> 0%
where the time goes in v2:
time: 380 us; the launch traced here: 379 us
  waiting for transfers between devices  274 us (72%)
  starting transfers between devices  31.8 us (8%)
  local copies, waits for them, and re-layouts  16.6 us (4%)
  blocking collectives  15.2 us (4%)
  between operations  14.2 us (4%)
  other arithmetic  14.1 us (4%)
  matrix products  13 us (3%)
    all_to_all x1, waiting for transfers between devices, local(): back = lax.all_to_all(sent, DP, split_axis=0, concat_axis=0, tiled=True)  101 us
    all_to_all x1, waiting for transfers between devices, local(): lax.all_to_all(outgoing, DP, split_axis=0, concat_axis=0, tiled=True)  62 us
    all_gather x1, waiting for transfers between devices, local(): heads_all = lax.all_gather(mixed, 'fsdp', axis=1, tiled=True)  43.8 us
    all_gather x1, waiting for transfers between devices, local(): full_rows = lax.all_gather(arrived, 'fsdp', axis=1, tiled=True)  40.1 us
    all_gather x1, waiting for transfers between devices, local(): weights = lax.all_gather(weights, 'z', axis=0, tiled=True)  27.6 us
    all_to_all x1, starting transfers between devices, local(): lax.all_to_all(outgoing, DP, split_axis=0, concat_axis=0, tiled=True)  16 us
    all_to_all x1, starting transfers between devices, local(): back = lax.all_to_all(sent, DP, split_axis=0, concat_axis=0, tiled=True)  15.7 us
    all_gather x1, blocking collectives, local(): weights = lax.all_gather(weights, 'y', axis=0, tiled=True)  15.2 us
  transfers between devices with their start and end apart: 5, of which 5 were waited for; matrix products, arithmetic and copies ran while one was open for 2% of the time, Pallas kernels for 0%

profile of v2, /device:TPU:24, one launch (start us, length us, event | category | flops | bytes accessed | tf_op | source)
XLA Modules:
  0.0 379.2 jit_solution(14914745712318260603)
XLA Ops:
  8.1 15.2 %all_gather.12 = bf16[128,768]{1,0:T(8,128)(2,1)} all-gather(bf16[32,768]{1,0:T(8,128)(2,1)S(1)} %pad_maximum_fusion.3), channel_id=1, replica_groups=mesh['z'=16,'y'=4,'fsdp'=8] {'y'}, dimensions={0}, use_global_device_ids=true | all-gather | bytes 245760 | tf_op jit(solution)/shard_map/all_gather | solution.py:91
  25.7 1.6 gather_fusion
  27.3 16.0 %all-to-all-start = ((bf16[64,32,256]{2,1,0:T(8,128)(2,1)}), bf16[64,32,256]{2,1,0:T(8,128)(2,1)S(1)}, u32[]{:S(2)}, u32[]{:S(2)}) async-start(bf16[64,32,256]{2,1,0:T(8,128)(2,1)} %bitcast.9), calls=%async_computation | async-start | bytes 2097152 | tf_op jit(solution)/shard_map/all_to_all | solution.py:104
  45.3 62.0 %all-to-all-done = bf16[64,32,256]{2,1,0:T(8,128)(2,1)S(1)} async-done(((bf16[64,32,256]{2,1,0:T(8,128)(2,1)}), bf16[64,32,256]{2,1,0:T(8,128)(2,1)S(1)}, u32[]{:S(2)}, u32[]{:S(2)}) %all-to-all-start) | async-done | bytes 1048608 | tf_op jit(solution)/shard_map/all_to_all | solution.py:104
  107.3 1.4 gather_fusion.1
  108.7 27.6 %all-gather.4.cloned.1.call-done = bf16[2048,768]{1,0:T(8,128)(2,1)} async-done(((bf16[128,768]{1,0:T(8,128)(2,1)}), bf16[2048,768]{1,0:T(8,128)(2,1)}) %all-gather.4.cloned.1.call-update) | async-done | bytes 3145744 | tf_op jit(solution)/shard_map/all_gather | solution.py:93
  137.9 40.1 %all-gather.6.cloned.1.call-done = bf16[1024,2048]{1,0:T(8,128)(2,1)} async-done(((bf16[1024,256]{1,0:T(8,128)(2,1)}), bf16[1024,2048]{1,0:T(8,128)(2,1)}) %all-gather.6.cloned.1.call-update) | async-done | bytes 4194320 | tf_op jit(solution)/shard_map/all_gather | solution.py:120
  178.0 3.2 fusion.21
  183.4 1.5 multiply_reduce_fusion.1
  184.9 1.3 multiply_reduce_fusion
  186.2 1.2 convolution_convert_fusion.1
  187.6 1.3 fusion.35
  191.8 9.4 %while.12 = (s32[]{:T(128)}, bf16[2,512,1,2,128]{4,3,1,0,2:T(2,128)(2,1)S(1)}, s32[2,512]{1,0:T(2,128)S(1)}, s32[2,512]{1,0:T(2,128)S(1)}, bf16[2,512,1,2,128]{4...) while((s32[]{:T(128)}, ...), condition=%wide.region_13.14_spmd.clone.clone, body=%wide.region_10.13_spmd.clone.clone.sunk | while | flops 551155712 | bytes 16285793 | solution.py:159
  193.5 1.2 fusion.62
  194.6 1.6 fusion.63
  198.2 1.2 fusion.62
  199.4 1.6 fusion.63
  202.7 43.8 %all-gather.8.cloned.1.call-done = bf16[1024,2048]{1,0:T(8,128)(2,1)} async-done(((bf16[1024,256]{1,0:T(8,128)(2,1)}), bf16[1024,2048]{1,0:T(8,128)(2,1)}) %all-gather.8.cloned.1.call-update) | async-done | bytes 4194320 | tf_op jit(solution)/shard_map/all_gather | solution.py:168
  246.5 3.7 convolution_convert_fusion
  250.5 2.0 gather_fusion.2
  252.5 15.7 %all-to-all-start.1 = ((bf16[64,32,512]{2,1,0:T(8,128)(2,1)}), bf16[64,32,512]{2,1,0:T(8,128)(2,1)S(1)}, u32[]{:S(2)}, u32[]{:S(2)}) async-start(bf16[64,32,512]{2,1,0:T(8,128)(2,1)} %bitcast.127), calls=%async_computation.1 | async-start | bytes 4194304 | tf_op jit(solution)/shard_map/all_to_all | solution.py:176
  268.3 100.5 %all-to-all-done.1 = bf16[64,32,512]{2,1,0:T(8,128)(2,1)S(1)} async-done(((bf16[64,32,512]{2,1,0:T(8,128)(2,1)}), bf16[64,32,512]{2,1,0:T(8,128)(2,1)S(1)}, u32[]{:S(2)}, u32[]{:S(2)}) %all-to-all-start.1) | async-done | bytes 2097184 | tf_op jit(solution)/shard_map/all_to_all | solution.py:176
  368.8 1.6 gather_fusion.3
  370.4 2.2 slice_bitcast_fusion
  (86 shorter events, 17.2 us)
Async XLA Ops:
  7.2 18.5 %copy-start = (bf16[1024,256]{1,0:T(8,128)(2,1)S(1)}, bf16[1024,256]{1,0:T(8,128)(2,1)}, u32[]{:S(2)}) copy-start(bf16[1024,256]{1,0:T(8,128)(2,1)} %param.12) | copy-start | bytes 1572868
  7.2 36.2 %copy-start.4 = (s32[64,64]{1,0:T(8,128)S(1)}, s32[64,64]{1,0:T(8,128)}, u32[]{:S(2)}) copy-start(s32[64,64]{1,0:T(8,128)} %param.21) | copy-start | bytes 49156
  7.2 129.2 %copy-start.5 = (bf16[2048]{0:T(1024)(128)(2,1)S(1)}, bf16[2048]{0:T(1024)(128)(2,1)}, u32[]{:S(2)}) copy-start(bf16[2048]{0:T(1024)(128)(2,1)} %param.13) | copy-start | bytes 12292
  7.2 129.2 %copy-start.7 = (bf16[128]{0:T(256)(128)(2,1)S(1)}, bf16[128]{0:T(256)(128)(2,1)}, u32[]{:S(2)}) copy-start(bf16[128]{0:T(256)(128)(2,1)} %param.15) | copy-start | bytes 772
  7.2 129.2 %copy-start.6 = (s32[64,8]{0,1:T(8,128)S(1)}, s32[64,8]{0,1:T(8,128)}, u32[]{:S(2)}) copy-start(s32[64,8]{0,1:T(8,128)} %param.20) | copy-start | bytes 6148
  7.2 129.6 %copy-start.8 = (bf16[128]{0:T(256)(128)(2,1)S(1)}, bf16[128]{0:T(256)(128)(2,1)}, u32[]{:S(2)}) copy-start(bf16[128]{0:T(256)(128)(2,1)} %param.14) | copy-start | bytes 772
  7.2 129.1 %all-gather.4.cloned.1.call-start = ((), (), s32[]{:S(2)}) async-start(), calls=%async_computation.2 | async-start | bytes 3342336 | tf_op jit(solution)/shard_map/all_gather | solution.py:93
  27.3 80.0 %all-to-all-start = ((bf16[64,32,256]{2,1,0:T(8,128)(2,1)}), bf16[64,32,256]{2,1,0:T(8,128)(2,1)S(1)}, u32[]{:S(2)}, u32[]{:S(2)}) async-start(bf16[64,32,256]{2,1,0:T(8,128)(2,1)} %bitcast.9), calls=%async_computation | async-start | bytes 2097152 | tf_op jit(solution)/shard_map/all_to_all | solution.py:104
  43.4 134.7 %all-gather.6.cloned.1.call-start = ((), (), s32[]{:S(2)}) async-start(), calls=%async_computation.3 | async-start | bytes 4718592 | tf_op jit(solution)/shard_map/all_gather | solution.py:120
  136.3 110.2 %all-gather.8.cloned.1.call-start = ((), (), s32[]{:S(2)}) async-start(), calls=%async_computation.4 | async-start | bytes 4718592 | tf_op jit(solution)/shard_map/all_gather | solution.py:168
  178.0 3.4 copy-start.1
  181.5 1.9 copy-start.3
  190.0 1.7 copy-start.2
  252.5 116.3 %all-to-all-start.1 = ((bf16[64,32,512]{2,1,0:T(8,128)(2,1)}), bf16[64,32,512]{2,1,0:T(8,128)(2,1)S(1)}, u32[]{:S(2)}, u32[]{:S(2)}) async-start(bf16[64,32,512]{2,1,0:T(8,128)(2,1)} %bitcast.127), calls=%async_computation.1 | async-start | bytes 4194304 | tf_op jit(solution)/shard_map/all_to_all | solution.py:176
Sparse Core Ops, SparseCore 0:
  23.4 112.8 all-gather.3
  139.0 39.0 all-gather.5
  202.3 44.1 all-gather.7

commit v3 on v2

--- a/solution.py
+++ b/solution.py
@@ -87,35 +87,47 @@
     device_index = lax.axis_index(DP)
     block_ids = jnp.arange(groups, dtype=jnp.int32)
 
-    weights = jnp.concatenate([w_query, w_key, w_value, w_out], axis=1)
-    weights = lax.all_gather(weights, "y", axis=0, tiled=True)
-    weights, tokens = lax.optimization_barrier((weights, tokens))
-    weights = lax.all_gather(weights, "z", axis=0, tiled=True)
-
     own_blocks = lax.dynamic_index_in_dim(span_group, device_index, 0, keepdims=False)
     same = own_blocks[:, None] == own_blocks[None, :]
     dup_rank = jnp.sum(same & (block_ids[None, :] < block_ids[:, None]), axis=1).astype(jnp.int32)
-    send_slot = own_blocks * 2 + dup_rank
-    slot_source = jnp.zeros((groups * 2,), jnp.int32).at[send_slot].set(block_ids)
+    first_dest = jnp.where(dup_rank == 0, own_blocks, groups)
+    slot_source = jnp.zeros((groups,), jnp.int32).at[first_dest].set(block_ids, mode="drop")
+    dup_block = jnp.sum(jnp.where(dup_rank == 1, block_ids, 0))
     token_blocks = tokens.reshape(groups, arrival_rows, width_local)
-    outgoing = jnp.take(token_blocks, slot_source, axis=0, mode="clip").reshape(
-        groups, 2 * arrival_rows, width_local
-    )
+    dup_tokens = lax.dynamic_index_in_dim(token_blocks, dup_block, 0, keepdims=False)
+
+    weights = jnp.concatenate([w_query, w_key, w_value, w_out], axis=1)
+    weight_rows, weight_width = weights.shape
+    dup_size = arrival_rows * width_local
+    dup_rows = -(-dup_size // weight_width)
+    dup_flat = jnp.pad(dup_tokens.reshape(-1), (0, dup_rows * weight_width - dup_size))
+    packed = jnp.concatenate([weights, dup_flat.reshape(dup_rows, weight_width)], axis=0)
+    packed = lax.all_gather(packed, "y", axis=0, tiled=True)
+    packed, token_blocks = lax.optimization_barrier((packed, token_blocks))
+    packed = lax.all_gather(packed, "z", axis=0, tiled=True)
+    packed = packed.reshape(groups, weight_rows + dup_rows, weight_width)
+    weights = packed[:, :weight_rows].reshape(groups * weight_rows, weight_width)
+    dup_all = (
+        packed[:, weight_rows:]
+        .reshape(groups, -1)[:, :dup_size]
+        .reshape(groups, arrival_rows, width_local)
+    )
+
+    outgoing = jnp.take(token_blocks, slot_source, axis=0, mode="clip")
     incoming = lax.all_to_all(outgoing, DP, split_axis=0, concat_axis=0, tiled=True)
     counts = jnp.sum((span_group == device_index).astype(jnp.int32), axis=1)
     offsets = jnp.cumsum(counts) - counts
-    sub_ids = jnp.arange(2, dtype=jnp.int32)
-    is_valid = sub_ids[None, :] < counts[:, None]
-    back_index = jnp.where(is_valid, offsets[:, None] + sub_ids[None, :], groups)
-    flat_slot = block_ids[:, None] * 2 + sub_ids[None, :]
+    first_pos = jnp.where(counts >= 1, offsets, groups)
+    second_pos = jnp.where(counts == 2, offsets + 1, groups)
     source_of = (
         jnp.zeros((groups,), jnp.int32)
-        .at[back_index.reshape(-1)]
-        .set(flat_slot.reshape(-1), mode="drop")
-    )
-    arrived = jnp.take(
-        incoming.reshape(groups * 2, arrival_rows, width_local), source_of, axis=0, mode="clip"
-    ).reshape(group_rows, width_local)
+        .at[first_pos]
+        .set(block_ids, mode="drop")
+        .at[second_pos]
+        .set(block_ids + groups, mode="drop")
+    )
+    pool = jnp.concatenate([incoming, dup_all], axis=0)
+    arrived = jnp.take(pool, source_of, axis=0, mode="clip").reshape(group_rows, width_local)
     arrived, weights = lax.optimization_barrier((arrived, weights))
     full_rows = lax.all_gather(arrived, "fsdp", axis=1, tiled=True)
     cuts = [w_query.shape[1], w_key.shape[1], w_value.shape[1], w_out.shape[1]]
@@ -170,12 +182,15 @@
     cache_flat = cache_rows.reshape(group_rows, -1)
     update_width = update.shape[1]
     joined = jnp.concatenate([update, cache_flat], axis=1).reshape(groups, arrival_rows, -1)
-    sent = jnp.take(joined, back_index.reshape(-1), axis=0, mode="clip").reshape(
-        groups, 2 * arrival_rows, -1
-    )
+    sent = jnp.take(joined, offsets, axis=0, mode="clip")
+    dup_position = jnp.sum(jnp.where(counts == 2, offsets + 1, 0))
+    dup_result = lax.dynamic_index_in_dim(joined, dup_position, 0, keepdims=True)
+    dup_result = lax.all_gather(dup_result, "y", axis=0, tiled=True)
+    dup_result = lax.all_gather(dup_result, "z", axis=0, tiled=True)
     back = lax.all_to_all(sent, DP, split_axis=0, concat_axis=0, tiled=True)
+    pool_back = jnp.concatenate([back, dup_result], axis=0)
     mine = jnp.take(
-        back.reshape(groups * 2, arrival_rows, -1), send_slot, axis=0, mode="clip"
+        pool_back, own_blocks + groups * dup_rank, axis=0, mode="clip"
     ).reshape(group_rows, -1)
     attention_out = mine[:, :update_width]
     cache_out = mine[:, update_width:].reshape(cache_rows.shape)

time: 380 us -> 368 us (0.968)
  waiting for transfers between devices: 274 us -> 232 us
  blocking collectives: 15.2 us -> 27.3 us
  local copies, waits for them, and re-layouts: 16.6 us -> 27.2 us
  between operations: 14.2 us -> 18.1 us
    all_gather x1 -> x2, waiting for transfers between devices: 27.6 us -> 149 us  [the longest x1 75.4 us: local(): dup_result = lax.all_gather(dup_result, 'z', axis=0, tiled=True)]
    all_to_all x1, waiting for transfers between devices: 101 us -> 0.01 us  [local(): back = lax.all_to_all(sent, DP, split_axis=0, concat_axis=0, tiled=True)]
    all_to_all x1, waiting for transfers between devices: 62 us -> 0.01 us  [local(): lax.all_to_all(outgoing, DP, split_axis=0, concat_axis=0, tiled=True)]
    all_gather x1 -> x2, blocking collectives: 15.2 us -> 27.3 us  [the longest x1 14.6 us: local(): packed = lax.all_gather(packed, 'y', axis=0, tiled=True)]
    reshape x0 -> x2, local copies, waits for them, and re-layouts: none -> 5.93 us  [the longest x1 5.9 us: local(): packed = packed.reshape(groups, weight_rows + dup_rows, weight_width)]
    slice x0 -> x4, local copies, waits for them, and re-layouts: none -> 3.89 us  [the longest x1 3.85 us: local(): packed[:, :weight_rows].reshape(groups * weight_rows, weight_width)]
  transfers between devices with their start and end apart: 5 -> 6, of which waited for: 5 -> 4; matrix products, arithmetic and copies ran while one was open for 2% -> 5% of each run, Pallas kernels for 0% -> 0%
where the time goes in v3:
time: 368 us
  waiting for transfers between devices  232 us (63%)
  starting transfers between devices  32 us (9%)
  blocking collectives  27.3 us (7%)
  local copies, waits for them, and re-layouts  27.2 us (7%)
  between operations  18.1 us (5%)
  other arithmetic  17.9 us (5%)
  matrix products  13 us (4%)
    all_gather x1, waiting for transfers between devices, local(): dup_result = lax.all_gather(dup_result, 'z', axis=0, tiled=True)  75.4 us
    all_gather x1, waiting for transfers between devices, local(): packed = lax.all_gather(packed, 'z', axis=0, tiled=True)  73.8 us
    all_gather x1, waiting for transfers between devices, local(): heads_all = lax.all_gather(mixed, 'fsdp', axis=1, tiled=True)  44 us
    all_gather x1, waiting for transfers between devices, local(): full_rows = lax.all_gather(arrived, 'fsdp', axis=1, tiled=True)  38.8 us
    all_to_all x1, starting transfers between devices, local(): lax.all_to_all(outgoing, DP, split_axis=0, concat_axis=0, tiled=True)  16 us
    all_to_all x1, starting transfers between devices, local(): back = lax.all_to_all(sent, DP, split_axis=0, concat_axis=0, tiled=True)  15.9 us
    all_gather x1, blocking collectives, local(): packed = lax.all_gather(packed, 'y', axis=0, tiled=True)  14.6 us
    all_gather x1, blocking collectives, local(): dup_result = lax.all_gather(dup_result, 'y', axis=0, tiled=True)  12.8 us
  transfers between devices with their start and end apart: 6, of which 4 were waited for; matrix products, arithmetic and copies ran while one was open for 5% of the time, Pallas kernels for 0%

profile of v3, /device:TPU:24, one launch (start us, length us, event | category | flops | bytes accessed | tf_op | source)
XLA Modules:
  0.0 367.7 jit_solution(4721704235906050034)
XLA Ops:
  11.6 14.6 %all-gather = bf16[4,38,768]{2,1,0:T(8,128)(2,1)S(1)} all-gather(bf16[1,38,768]{2,1,0:T(8,128)(2,1)S(1)} %maximum_bitcast_fusion), channel_id=1, replica_groups=mesh['z'=16,'y'=4,'fsdp'=8] {'y'}, dimensions={0}, use_global_device_ids=true | all-gather | bytes 291840 | tf_op jit(solution)/shard_map/all_gather | solution.py:105
  28.8 1.4 gather_fusion
  30.2 16.0 %all-to-all-start = ((bf16[64,16,256]{2,1,0:T(8,128)(2,1)}), bf16[64,16,256]{2,1,0:T(8,128)(2,1)S(1)}, u32[]{:S(2)}, u32[]{:S(2)}) async-start(bf16[64,16,256]{2,1,0:T(8,128)(2,1)} %gather_fusion), calls=%async_computation | async-start | bytes 1048576 | tf_op jit(solution)/shard_map/all_to_all | solution.py:117
  49.0 73.8 %all-gather.6.cloned.1.call-done = bf16[2432,768]{1,0:T(8,128)(2,1)} async-done(((bf16[152,768]{1,0:T(8,128)(2,1)}), bf16[2432,768]{1,0:T(8,128)(2,1)}) %all-gather.6.cloned.1.call-update) | async-done | bytes 3735568 | tf_op jit(solution)/shard_map/all_gather | solution.py:107
  122.8 5.9 %reshape.480 = bf16[64,38,768]{2,1,0:T(8,128)(2,1)} reshape(bf16[2432,768]{1,0:T(8,128)(2,1)} %all-gather.6.cloned.1.call-done) | data formatting | bytes 7471104 | tf_op jit(solution)/shard_map/reshape | solution.py:108
  128.7 3.9 %slice.62 = bf16[64,32,768]{2,1,0:T(8,128)(2,1)} slice(bf16[64,38,768]{2,1,0:T(8,128)(2,1)} %reshape.480), slice={[0:64], [0:32], [0:768]} | slice | bytes 6291456 | tf_op jit(solution)/shard_map/slice | solution.py:109
  133.0 1.4 gather_fusion.1
  136.0 38.8 %all-gather.8.cloned.1.call-done = bf16[1024,2048]{1,0:T(8,128)(2,1)} async-done(((bf16[1024,256]{1,0:T(8,128)(2,1)}), bf16[1024,2048]{1,0:T(8,128)(2,1)}) %all-gather.8.cloned.1.call-update) | async-done | bytes 4194320 | tf_op jit(solution)/shard_map/all_gather | solution.py:132
  174.8 3.2 fusion.21
  180.1 1.5 multiply_reduce_fusion.1
  181.7 1.3 multiply_reduce_fusion
  184.4 1.3 fusion.35
  188.5 9.4 %while.12 = (s32[]{:T(128)}, bf16[2,512,1,2,128]{4,3,1,0,2:T(2,128)(2,1)S(1)}, s32[2,512]{1,0:T(2,128)S(1)}, s32[2,512]{1,0:T(2,128)S(1)}, bf16[2,512,1,2,128]{4...) while((s32[]{:T(128)}, ...), condition=%wide.region_15.16_spmd.clone.clone, body=%wide.region_12.15_spmd.clone.clone.sunk | while | flops 551155712 | bytes 16285793 | solution.py:171
  191.4 1.6 fusion.69
  196.1 1.6 fusion.69
  199.3 44.0 %all-gather.10.cloned.1.call-done = bf16[1024,2048]{1,0:T(8,128)(2,1)} async-done(((bf16[1024,256]{1,0:T(8,128)(2,1)}), bf16[1024,2048]{1,0:T(8,128)(2,1)}) %all-gather.10.cloned.1.call-update) | async-done | bytes 4194320 | tf_op jit(solution)/shard_map/all_gather | solution.py:180
  243.2 3.7 %convolution_convert_fusion = bf16[1024,256]{1,0:T(8,128)(2,1)S(1)} fusion(bf16[1024,2048]{1,0:T(8,128)(2,1)} %all-gather.10.cloned.1.call-done, bf16[2048,768]{1,0:T(8,128)(2,1)} %bitcast.135), kind=kOutput, calls=%fused_computation.37 | convolution fusion | flops 1074003968 | bytes 5767168 | tf_op jit(solution)/shard_map/dot_general | solution.py:181
  247.3 1.6 gather_fusion.2
  248.9 15.9 %all-to-all-start.1 = ((bf16[64,16,512]{2,1,0:T(8,128)(2,1)}), bf16[64,16,512]{2,1,0:T(8,128)(2,1)}, u32[]{:S(2)}, u32[]{:S(2)}) async-start(bf16[64,16,512]{2,1,0:T(8,128)(2,1)} %gather_fusion.2), calls=%async_computation.1 | async-start | bytes 2097152 | tf_op jit(solution)/shard_map/all_to_all | solution.py:190
  267.4 12.8 %all_gather.22 = bf16[4,16,512]{2,1,0:T(8,128)(2,1)} all-gather(bf16[1,16,512]{2,1,0:T(8,128)(2,1)S(1)} %constant_dynamic-slice_fusion.2), channel_id=1, replica_groups=mesh['z'=16,'y'=4,'fsdp'=8] {'y'}, dimensions={0}, use_global_device_ids=true | all-gather | bytes 81920 | tf_op jit(solution)/shard_map/all_gather | solution.py:188
  280.2 75.4 %all-gather.12.cloned.1.call-done = bf16[64,16,512]{2,1,0:T(8,128)(2,1)} async-done(((bf16[4,16,512]{2,1,0:T(8,128)(2,1)}), bf16[64,16,512]{2,1,0:T(8,128)(2,1)}) %all-gather.12.cloned.1.call-update) | async-done | bytes 1048592 | tf_op jit(solution)/shard_map/all_gather | solution.py:189
  355.6 1.7 pad_maximum_fusion
  357.3 1.6 gather_fusion.3
  359.0 2.2 slice_bitcast_fusion
  (104 shorter events, 24.4 us)
Async XLA Ops:
  7.2 3.6 copy-start
  7.2 115.6 %all-gather.6.cloned.1.call-start = ((), (), s32[]{:S(2)}) async-start(), calls=%async_computation.2 | async-start | bytes 3969024 | tf_op jit(solution)/shard_map/all_gather | solution.py:107
  30.2 102.7 %all-to-all-start = ((bf16[64,16,256]{2,1,0:T(8,128)(2,1)}), bf16[64,16,256]{2,1,0:T(8,128)(2,1)S(1)}, u32[]{:S(2)}, u32[]{:S(2)}) async-start(bf16[64,16,256]{2,1,0:T(8,128)(2,1)} %gather_fusion), calls=%async_computation | async-start | bytes 1048576 | tf_op jit(solution)/shard_map/all_to_all | solution.py:117
  46.2 128.6 %all-gather.8.cloned.1.call-start = ((), (), s32[]{:S(2)}) async-start(), calls=%async_computation.3 | async-start | bytes 4718592 | tf_op jit(solution)/shard_map/all_gather | solution.py:132
  128.7 3.9 %slice-start = ((bf16[64,38,768]{2,1,0:T(8,128)(2,1)}), bf16[64,6,768]{2,1,0:T(8,128)(2,1)S(1)}, s32[]{:S(2)}) async-start(bf16[64,38,768]{2,1,0:T(8,128)(2,1)} %reshape.480), calls=%async_computation.6 | async-start | bytes 1572864 | tf_op jit(solution)/shard_map/slice | solution.py:111
  132.6 1.9 copy-start.4
  132.6 1.9 copy-start.6
  132.6 1.9 copy-start.5
  132.6 2.3 copy-start.7
  134.4 108.8 %all-gather.10.cloned.1.call-start = ((), (), s32[]{:S(2)}) async-start(), calls=%async_computation.4 | async-start | bytes 4718592 | tf_op jit(solution)/shard_map/all_gather | solution.py:180
  174.8 3.4 copy-start.1
  178.2 1.9 copy-start.2
  186.8 1.7 copy-start.3
  248.9 106.7 %all-to-all-start.1 = ((bf16[64,16,512]{2,1,0:T(8,128)(2,1)}), bf16[64,16,512]{2,1,0:T(8,128)(2,1)}, u32[]{:S(2)}, u32[]{:S(2)}) async-start(bf16[64,16,512]{2,1,0:T(8,128)(2,1)} %gather_fusion.2), calls=%async_computation.1 | async-start | bytes 2097152 | tf_op jit(solution)/shard_map/all_to_all | solution.py:190
  264.8 90.8 %all-gather.12.cloned.1.call-start = ((), (), s32[]{:S(2)}) async-start(), calls=%async_computation.5 | async-start | bytes 1114112 | tf_op jit(solution)/shard_map/all_gather | solution.py:189
Sparse Core Ops, SparseCore 0:
  27.1 95.7 all-gather.5
  134.5 40.2 all-gather.7
  199.0 44.1 all-gather.9
  280.3 75.2 all-gather.11

commit v4 on v3

--- a/solution.py
+++ b/solution.py
@@ -8,7 +8,7 @@
 QH = 16
 KVH = 8
 HD = 128
-DP = ("z", "y")
+DP = ("z_hi", "z_lo", "y")
 
 
 epsilon = 1e-06
@@ -98,20 +98,13 @@
 
     weights = jnp.concatenate([w_query, w_key, w_value, w_out], axis=1)
     weight_rows, weight_width = weights.shape
-    dup_size = arrival_rows * width_local
-    dup_rows = -(-dup_size // weight_width)
-    dup_flat = jnp.pad(dup_tokens.reshape(-1), (0, dup_rows * weight_width - dup_size))
-    packed = jnp.concatenate([weights, dup_flat.reshape(dup_rows, weight_width)], axis=0)
+    packed = jnp.concatenate([weights, dup_tokens.reshape(weight_rows, -1)], axis=1)
     packed = lax.all_gather(packed, "y", axis=0, tiled=True)
     packed, token_blocks = lax.optimization_barrier((packed, token_blocks))
-    packed = lax.all_gather(packed, "z", axis=0, tiled=True)
-    packed = packed.reshape(groups, weight_rows + dup_rows, weight_width)
-    weights = packed[:, :weight_rows].reshape(groups * weight_rows, weight_width)
-    dup_all = (
-        packed[:, weight_rows:]
-        .reshape(groups, -1)[:, :dup_size]
-        .reshape(groups, arrival_rows, width_local)
-    )
+    packed = lax.all_gather(packed, "z_lo", axis=0, tiled=True)
+    packed = lax.all_gather(packed, "z_hi", axis=0, tiled=True)
+    weights = packed[:, :weight_width]
+    dup_all = packed[:, weight_width:].reshape(groups, arrival_rows, width_local)
 
     outgoing = jnp.take(token_blocks, slot_source, axis=0, mode="clip")
     incoming = lax.all_to_all(outgoing, DP, split_axis=0, concat_axis=0, tiled=True)
@@ -186,7 +179,8 @@
     dup_position = jnp.sum(jnp.where(counts == 2, offsets + 1, 0))
     dup_result = lax.dynamic_index_in_dim(joined, dup_position, 0, keepdims=True)
     dup_result = lax.all_gather(dup_result, "y", axis=0, tiled=True)
-    dup_result = lax.all_gather(dup_result, "z", axis=0, tiled=True)
+    dup_result = lax.all_gather(dup_result, "z_lo", axis=0, tiled=True)
+    dup_result = lax.all_gather(dup_result, "z_hi", axis=0, tiled=True)
     back = lax.all_to_all(sent, DP, split_axis=0, concat_axis=0, tiled=True)
     pool_back = jnp.concatenate([back, dup_result], axis=0)
     mine = jnp.take(
@@ -199,7 +193,9 @@
 
 def solution(mesh):
     z_size = mesh.shape["dp"] // 4
-    fine = Mesh(mesh.devices.reshape(z_size, 4, mesh.shape["fsdp"]), ("z", "y", "fsdp"))
+    fine = Mesh(
+        mesh.devices.reshape(z_size // 4, 4, 4, mesh.shape["fsdp"]), ("z_hi", "z_lo", "y", "fsdp")
+    )
     return jax.shard_map(
         local,
         mesh=fine,

time: 368 us -> 477 us (1.30)
  blocking collectives: 27.3 us -> 86.5 us
  waiting for transfers between devices: 232 us -> 283 us
    all_gather x0 -> x2, blocking collectives: none -> 59.9 us  [the longest x1 41 us: local(): dup_result = lax.all_gather(dup_result, 'z_lo', axis=0, tiled=True)]
    all_gather x2, waiting for transfers between devices: 149 us -> 202 us  [the longest x1 141 us: local(): packed = lax.all_gather(packed, 'z_hi', axis=0, tiled=True)]
    reshape x2, local copies, waits for them, and re-layouts: 5.93 us -> 0.18 us  [the longest x1 0.17 us: local(): packed[:, weight_width:].reshape(groups, arrival_rows, width_local)]
  transfers between devices with their start and end apart: 6 -> 6, of which waited for: 4 -> 4; matrix products, arithmetic and copies ran while one was open for 5% -> 2% of each run, Pallas kernels for 0% -> 0%
where the time goes in v4:
time: 477 us; the launch traced here: 475 us
  waiting for transfers between devices  283 us (59%)
  blocking collectives  86.5 us (18%)
  starting transfers between devices  32.3 us (7%)
  local copies, waits for them, and re-layouts  24.3 us (5%)
  between operations  18.1 us (4%)
  other arithmetic  17.1 us (4%)
  matrix products  13 us (3%)
    all_gather x1, waiting for transfers between devices, local(): packed = lax.all_gather(packed, 'z_hi', axis=0, tiled=True)  141 us
    all_gather x1, waiting for transfers between devices, local(): dup_result = lax.all_gather(dup_result, 'z_hi', axis=0, tiled=True)  60.9 us
    all_gather x1, waiting for transfers between devices, local(): heads_all = lax.all_gather(mixed, 'fsdp', axis=1, tiled=True)  44 us
    all_gather x1, blocking collectives, local(): dup_result = lax.all_gather(dup_result, 'z_lo', axis=0, tiled=True)  41 us
    all_gather x1, waiting for transfers between devices, local(): full_rows = lax.all_gather(arrived, 'fsdp', axis=1, tiled=True)  37.2 us
    all_gather x1, blocking collectives, local(): packed = lax.all_gather(packed, 'z_lo', axis=0, tiled=True)  18.9 us
    all_to_all x1, starting transfers between devices, local(): lax.all_to_all(outgoing, DP, split_axis=0, concat_axis=0, tiled=True)  16.3 us
    all_to_all x1, starting transfers between devices, local(): back = lax.all_to_all(sent, DP, split_axis=0, concat_axis=0, tiled=True)  15.9 us
  transfers between devices with their start and end apart: 6, of which 4 were waited for; matrix products, arithmetic and copies ran while one was open for 2% of the time, Pallas kernels for 0%

profile of v4, /device:TPU:24, one launch (start us, length us, event | category | flops | bytes accessed | tf_op | source)
XLA Modules:
  0.0 474.6 jit_solution(10181882392468857005)
XLA Ops:
  13.6 14.5 %all_gather.24 = bf16[128,896]{1,0:T(8,128)(2,1)S(1)} all-gather(bf16[32,896]{1,0:T(8,128)(2,1)S(1)} %constant_dynamic-update-slice_fusion), channel_id=1, replica_groups=mesh['z_hi'=4,'z_lo'=4,'y'=4,'fsdp'=8] {'y'}, dimensions={0}, use_global_device_ids=true | all-gather | bytes 286720 | tf_op jit(solution)/shard_map/all_gather | solution.py:102
  28.2 18.9 %all_gather.25 = bf16[512,896]{1,0:T(8,128)(2,1)} all-gather(bf16[128,896]{1,0:T(8,128)(2,1)S(1)} %all_gather.24), channel_id=1, replica_groups=mesh['z_hi'=4,'z_lo'=4,'y'=4,'fsdp'=8] {'z_lo'}, dimensions={0}, use_global_device_ids=true | all-gather | bytes 1146880 | tf_op jit(solution)/shard_map/all_gather | solution.py:104
  50.2 1.4 gather_fusion
  51.5 16.3 %all-to-all-start = ((bf16[64,16,256]{2,1,0:T(8,128)(2,1)}), bf16[64,16,256]{2,1,0:T(8,128)(2,1)S(1)}, u32[]{:S(2)}, u32[]{:S(2)}) async-start(bf16[64,16,256]{2,1,0:T(8,128)(2,1)} %gather_fusion), calls=%async_computation | async-start | bytes 1048576 | tf_op jit(solution)/shard_map/all_to_all | solution.py:110
  69.5 141.0 %all-gather.5.cloned.1.call-done = bf16[2048,896]{1,0:T(8,128)(2,1)} async-done(((bf16[512,896]{1,0:T(8,128)(2,1)}), bf16[2048,896]{1,0:T(8,128)(2,1)}) %all-gather.5.cloned.1.call-update) | async-done | bytes 3670032 | tf_op jit(solution)/shard_map/all_gather | solution.py:105
  211.9 1.4 gather_fusion.1
  213.3 3.8 slice.57
  218.6 37.2 %all-gather.7.cloned.1.call-done = bf16[1024,2048]{1,0:T(8,128)(2,1)} async-done(((bf16[1024,256]{1,0:T(8,128)(2,1)}), bf16[1024,2048]{1,0:T(8,128)(2,1)}) %all-gather.7.cloned.1.call-update) | async-done | bytes 4194320 | tf_op jit(solution)/shard_map/all_gather | solution.py:125
  255.8 3.2 fusion.21
  261.2 1.5 multiply_reduce_fusion.1
  265.4 1.3 fusion.35
  269.6 9.4 %while.12 = (s32[]{:T(128)}, bf16[2,512,1,2,128]{4,3,1,0,2:T(2,128)(2,1)S(1)}, s32[2,512]{1,0:T(2,128)S(1)}, s32[2,512]{1,0:T(2,128)S(1)}, bf16[2,512,1,2,128]{4...) while((s32[]{:T(128)}, ...), condition=%wide.region_15.16_spmd.clone.clone, body=%wide.region_12.15_spmd.clone.clone.sunk | while | flops 551155712 | bytes 16285793 | solution.py:164
  272.4 1.6 fusion.69
  277.1 1.6 fusion.69
  280.3 44.0 %all-gather.9.cloned.1.call-done = bf16[1024,2048]{1,0:T(8,128)(2,1)} async-done(((bf16[1024,256]{1,0:T(8,128)(2,1)}), bf16[1024,2048]{1,0:T(8,128)(2,1)}) %all-gather.9.cloned.1.call-update) | async-done | bytes 4194320 | tf_op jit(solution)/shard_map/all_gather | solution.py:173
  324.3 3.7 convolution_convert_fusion
  328.3 1.6 gather_fusion.2
  330.0 15.9 %all-to-all-start.1 = ((bf16[64,16,512]{2,1,0:T(8,128)(2,1)}), bf16[64,16,512]{2,1,0:T(8,128)(2,1)}, u32[]{:S(2)}, u32[]{:S(2)}) async-start(bf16[64,16,512]{2,1,0:T(8,128)(2,1)} %gather_fusion.2), calls=%async_computation.1 | async-start | bytes 2097152 | tf_op jit(solution)/shard_map/all_to_all | solution.py:184
  348.5 12.1 %all_gather.29 = bf16[4,16,512]{2,1,0:T(8,128)(2,1)S(1)} all-gather(bf16[1,16,512]{2,1,0:T(8,128)(2,1)S(1)} %constant_dynamic-slice_fusion.2), channel_id=1, replica_groups=mesh['z_hi'=4,'z_lo'=4,'y'=4,'fsdp'=8] {'y'}, dimensions={0}, use_global_device_ids=true | all-gather | bytes 81920 | tf_op jit(solution)/shard_map/all_gather | solution.py:181
  360.6 41.0 %all_gather.30 = bf16[16,16,512]{2,1,0:T(8,128)(2,1)} all-gather(bf16[4,16,512]{2,1,0:T(8,128)(2,1)S(1)} %all_gather.29), channel_id=1, replica_groups=mesh['z_hi'=4,'z_lo'=4,'y'=4,'fsdp'=8] {'z_lo'}, dimensions={0}, use_global_device_ids=true | all-gather | bytes 327680 | tf_op jit(solution)/shard_map/all_gather | solution.py:182
  401.6 60.9 %all-gather.11.cloned.1.call-done = bf16[64,16,512]{2,1,0:T(8,128)(2,1)} async-done(((bf16[16,16,512]{2,1,0:T(8,128)(2,1)}), bf16[64,16,512]{2,1,0:T(8,128)(2,1)}) %all-gather.11.cloned.1.call-update) | async-done | bytes 1048592 | tf_op jit(solution)/shard_map/all_gather | solution.py:183
  462.5 1.7 pad_maximum_fusion
  464.2 1.6 gather_fusion.3
  465.8 2.2 slice_bitcast_fusion
  (102 shorter events, 28.0 us)
Async XLA Ops:
  7.2 3.6 copy-start
  7.2 203.3 %all-gather.5.cloned.1.call-start = ((), (), s32[]{:S(2)}) async-start(), calls=%async_computation.2 | async-start | bytes 4587520 | tf_op jit(solution)/shard_map/all_gather | solution.py:105
  51.5 160.2 %all-to-all-start = ((bf16[64,16,256]{2,1,0:T(8,128)(2,1)}), bf16[64,16,256]{2,1,0:T(8,128)(2,1)S(1)}, u32[]{:S(2)}, u32[]{:S(2)}) async-start(bf16[64,16,256]{2,1,0:T(8,128)(2,1)} %gather_fusion), calls=%async_computation | async-start | bytes 1048576 | tf_op jit(solution)/shard_map/all_to_all | solution.py:110
  67.8 188.0 %all-gather.7.cloned.1.call-start = ((), (), s32[]{:S(2)}) async-start(), calls=%async_computation.3 | async-start | bytes 4718592 | tf_op jit(solution)/shard_map/all_gather | solution.py:125
  211.8 5.3 %copy-start.4 = (bf16[2048]{0:T(1024)(128)(2,1)S(1)}, bf16[2048]{0:T(1024)(128)(2,1)}, u32[]{:S(2)}) copy-start(bf16[2048]{0:T(1024)(128)(2,1)} %param.13) | copy-start | bytes 12292
  211.8 5.3 %copy-start.6 = (bf16[128]{0:T(256)(128)(2,1)S(1)}, bf16[128]{0:T(256)(128)(2,1)}, u32[]{:S(2)}) copy-start(bf16[128]{0:T(256)(128)(2,1)} %param.15) | copy-start | bytes 772
  211.8 5.3 %copy-start.5 = (s32[64,8]{0,1:T(8,128)S(1)}, s32[64,8]{0,1:T(8,128)}, u32[]{:S(2)}) copy-start(s32[64,8]{0,1:T(8,128)} %param.20) | copy-start | bytes 6148
  211.9 5.7 %copy-start.7 = (bf16[128]{0:T(256)(128)(2,1)S(1)}, bf16[128]{0:T(256)(128)(2,1)}, u32[]{:S(2)}) copy-start(bf16[128]{0:T(256)(128)(2,1)} %param.14) | copy-start | bytes 772
  217.0 107.2 %all-gather.9.cloned.1.call-start = ((), (), s32[]{:S(2)}) async-start(), calls=%async_computation.4 | async-start | bytes 4718592 | tf_op jit(solution)/shard_map/all_gather | solution.py:173
  255.8 3.4 copy-start.1
  259.3 1.9 copy-start.2
  267.8 1.7 copy-start.3
  330.0 132.6 %all-to-all-start.1 = ((bf16[64,16,512]{2,1,0:T(8,128)(2,1)}), bf16[64,16,512]{2,1,0:T(8,128)(2,1)}, u32[]{:S(2)}, u32[]{:S(2)}) async-start(bf16[64,16,512]{2,1,0:T(8,128)(2,1)} %gather_fusion.2), calls=%async_computation.1 | async-start | bytes 2097152 | tf_op jit(solution)/shard_map/all_to_all | solution.py:184
  345.8 116.7 %all-gather.11.cloned.1.call-start = ((), (), s32[]{:S(2)}) async-start(), calls=%async_computation.5 | async-start | bytes 1310720 | tf_op jit(solution)/shard_map/all_gather | solution.py:183
Sparse Core Ops, SparseCore 0:
  47.2 163.1 all-gather.4
  217.2 38.6 all-gather.6
  280.1 44.1 all-gather.8
  401.7 60.7 all-gather.10

commit v5 on v3

--- a/solution.py
+++ b/solution.py
@@ -126,10 +126,16 @@
         .at[second_pos]
         .set(block_ids + groups, mode="drop")
     )
-    pool = jnp.concatenate([incoming, dup_all], axis=0)
-    arrived = jnp.take(pool, source_of, axis=0, mode="clip").reshape(group_rows, width_local)
-    arrived, weights = lax.optimization_barrier((arrived, weights))
-    full_rows = lax.all_gather(arrived, "fsdp", axis=1, tiled=True)
+    arrived = jnp.take(incoming, source_of, axis=0, mode="clip").reshape(group_rows, width_local)
+    fsdp_size = lax.axis_size("fsdp")
+    spread = jnp.broadcast_to(arrived[None], (fsdp_size,) + arrived.shape)
+    full_rows = lax.all_to_all(spread, "fsdp", split_axis=0, concat_axis=2, tiled=True)
+    full_rows = full_rows.reshape(group_rows, width_local * fsdp_size)
+    dup_source = jnp.sum(jnp.where(counts == 2, block_ids, 0))
+    dup_target = jnp.sum(jnp.where(counts == 2, offsets + 1, 0))
+    dup_mine = lax.dynamic_index_in_dim(dup_all, dup_source, 0, keepdims=False)
+    dup_full = lax.all_gather(dup_mine, "fsdp", axis=1, tiled=True)
+    full_rows = lax.dynamic_update_slice_in_dim(full_rows, dup_full, dup_target * arrival_rows, 0)
     cuts = [w_query.shape[1], w_key.shape[1], w_value.shape[1], w_out.shape[1]]
     bounds = [sum(cuts[:k]) for k in range(5)]
     query_full, key_full, value_full, out_full = (
@@ -179,21 +185,26 @@
     mixed = mixed.reshape(group_rows, kv_heads * group_ratio * HD)
     heads_all = lax.all_gather(mixed, "fsdp", axis=1, tiled=True)
     update = jnp.dot(heads_all, out_full, preferred_element_type=jnp.float32).astype(jnp.bfloat16)
-    cache_flat = cache_rows.reshape(group_rows, -1)
-    update_width = update.shape[1]
-    joined = jnp.concatenate([update, cache_flat], axis=1).reshape(groups, arrival_rows, -1)
-    sent = jnp.take(joined, offsets, axis=0, mode="clip")
-    dup_position = jnp.sum(jnp.where(counts == 2, offsets + 1, 0))
-    dup_result = lax.dynamic_index_in_dim(joined, dup_position, 0, keepdims=True)
-    dup_result = lax.all_gather(dup_result, "y", axis=0, tiled=True)
-    dup_result = lax.all_gather(dup_result, "z", axis=0, tiled=True)
-    back = lax.all_to_all(sent, DP, split_axis=0, concat_axis=0, tiled=True)
-    pool_back = jnp.concatenate([back, dup_result], axis=0)
-    mine = jnp.take(
-        pool_back, own_blocks + groups * dup_rank, axis=0, mode="clip"
-    ).reshape(group_rows, -1)
-    attention_out = mine[:, :update_width]
-    cache_out = mine[:, update_width:].reshape(cache_rows.shape)
+    slot_ids = jnp.arange(2 * arrival_rows, dtype=jnp.int32)
+    row_valid = slot_ids[None, :] < arrival_rows * counts[:, None]
+    row_target = jnp.where(row_valid, arrival_rows * offsets[:, None] + slot_ids[None, :], 0)
+    row_back = row_target.reshape(-1)
+    row_mine = (
+        (own_blocks * 2 + dup_rank)[:, None] * arrival_rows
+        + jnp.arange(arrival_rows, dtype=jnp.int32)[None, :]
+    ).reshape(-1)
+
+    def send_back(rows):
+        sent = jnp.take(rows, row_back, axis=0, mode="clip").reshape(
+            (groups, 2 * arrival_rows) + rows.shape[1:]
+        )
+        back = lax.all_to_all(sent, DP, split_axis=0, concat_axis=0, tiled=True)
+        return jnp.take(
+            back.reshape((groups * 2 * arrival_rows,) + rows.shape[1:]), row_mine, axis=0, mode="clip"
+        )
+
+    cache_out = send_back(cache_rows)
+    attention_out = send_back(update)
     return (attention_out, cache_out)
 
 

time: 368 us -> 346 us (0.940)
  waiting for transfers between devices: 232 us -> 172 us
  local copies, waits for them, and re-layouts: 27.2 us -> 65 us
    all_to_all x1 -> x3, waiting for transfers between devices: 0.01 us -> 120 us  [the longest x2 74.9 us: send_back(): back = lax.all_to_all(sent, DP, split_axis=0, concat_axis=0, tiled=True)]
    all_gather x2 -> x0, waiting for transfers between devices: 114 us -> none  [the longest x1 75.4 us: local(): dup_result = lax.all_gather(dup_result, 'z', axis=0, tiled=True)]
    all_gather x1, waiting for transfers between devices: 73.8 us -> 0.01 us  [local(): packed = lax.all_gather(packed, 'z', axis=0, tiled=True)]
    all_to_all x1, waiting for transfers between devices: 0.01 us -> 33.9 us  [local(): lax.all_to_all(outgoing, DP, split_axis=0, concat_axis=0, tiled=True)]
    all_gather x1, waiting for transfers between devices: 44 us -> 17.8 us  [local(): heads_all = lax.all_gather(mixed, 'fsdp', axis=1, tiled=True)]
    gather x3 -> x5, local copies, waits for them, and re-layouts: 4.64 us -> 28.6 us  [the longest x2 18 us: send_back(): jnp.take(rows, row_back, axis=0, mode='clip')]
    dynamic_update_slice x0 -> x1, local copies, waits for them, and re-layouts: none -> 6.49 us  [local(): lax.dynamic_update_slice_in_dim(full_rows, dup_full, dup_target * arrival...]
    all_to_all x0 -> x1, local copies, waits for them, and re-layouts: none -> 6.44 us  [local(): lax.all_to_all(spread, 'fsdp', split_axis=0, concat_axis=2, tiled=True)]
  transfers between devices with their start and end apart: 6 -> 6, of which waited for: 4 -> 5; matrix products, arithmetic and copies ran while one was open for 5% -> 12% of each run, Pallas kernels for 0% -> 0%
where the time goes in v5:
time: 346 us; the launch traced here: 345 us
  waiting for transfers between devices  172 us (50%)
  local copies, waits for them, and re-layouts  65 us (19%)
  starting transfers between devices  32.6 us (9%)
  blocking collectives  27.7 us (8%)
  between operations  19.1 us (6%)
  other arithmetic  14.7 us (4%)
  matrix products  13.8 us (4%)
    all_to_all x2, waiting for transfers between devices, send_back(): back = lax.all_to_all(sent, DP, split_axis=0, concat_axis=0, tiled=True)  74.9 us
    all_to_all x1, waiting for transfers between devices, local(): lax.all_to_all(spread, 'fsdp', split_axis=0, concat_axis=2, tiled=True)  45.3 us
    all_to_all x1, waiting for transfers between devices, local(): lax.all_to_all(outgoing, DP, split_axis=0, concat_axis=0, tiled=True)  33.9 us
    gather x2, local copies, waits for them, and re-layouts, send_back(): jnp.take(rows, row_back, axis=0, mode='clip')  18 us
    all_gather x1, waiting for transfers between devices, local(): heads_all = lax.all_gather(mixed, 'fsdp', axis=1, tiled=True)  17.8 us
    all_to_all x1, starting transfers between devices, local(): lax.all_to_all(outgoing, DP, split_axis=0, concat_axis=0, tiled=True)  16 us
    all_gather x1, blocking collectives, local(): packed = lax.all_gather(packed, 'y', axis=0, tiled=True)  14.6 us
    all_gather x1, blocking collectives, local(): dup_full = lax.all_gather(dup_mine, 'fsdp', axis=1, tiled=True)  13.1 us
  transfers between devices with their start and end apart: 6, of which 5 were waited for; matrix products, arithmetic and copies ran while one was open for 12% of the time, Pallas kernels for 0%

profile of v5, /device:TPU:24, one launch (start us, length us, event | category | flops | bytes accessed | tf_op | source)
XLA Modules:
  0.0 345.0 jit_solution(15337659761837456792)
XLA Ops:
  12.9 14.6 %all-gather.1 = bf16[4,38,768]{2,1,0:T(8,128)(2,1)S(1)} all-gather(bf16[1,38,768]{2,1,0:T(8,128)(2,1)S(1)} %maximum_bitcast_fusion.1), channel_id=1, replica_groups=mesh['z'=16,'y'=4,'fsdp'=8] {'y'}, dimensions={0}, use_global_device_ids=true | all-gather | bytes 291840 | tf_op jit(solution)/shard_map/all_gather | solution.py:105
  30.8 16.0 %all-to-all-start = ((bf16[64,16,256]{2,1,0:T(8,128)(2,1)}), bf16[64,16,256]{2,1,0:T(8,128)(2,1)S(1)}, u32[]{:S(2)}, u32[]{:S(2)}) async-start(bf16[64,16,256]{2,1,0:T(8,128)(2,1)} %gather_fusion), calls=%async_computation | async-start | bytes 1048576 | tf_op jit(solution)/shard_map/all_to_all | solution.py:117
  48.4 33.9 %all-to-all-done = bf16[64,16,256]{2,1,0:T(8,128)(2,1)S(1)} async-done(((bf16[64,16,256]{2,1,0:T(8,128)(2,1)}), bf16[64,16,256]{2,1,0:T(8,128)(2,1)S(1)}, u32[]{:S(2)}, u32[]{:S(2)}) %all-to-all-start) | async-done | bytes 524320 | tf_op jit(solution)/shard_map/all_to_all | solution.py:117
  82.9 2.2 broadcast_in_dim.118
  85.1 4.7 %all-to-all-start.1 = ((bf16[8,1024,256]{2,1,0:T(8,128)(2,1)}), bf16[8,1024,256]{2,1,0:T(8,128)(2,1)}, u32[]{:S(2)}, u32[]{:S(2)}) async-start(bf16[8,1024,256]{2,1,0:T(8,128)(2,1)} %broadcast_in_dim.118), calls=%async_computation.1 | async-start | bytes 8388608 | tf_op jit(solution)/shard_map/all_to_all | solution.py:132
  94.1 45.3 %all-to-all-done.1 = bf16[8,1024,256]{2,1,0:T(8,128)(2,1)} async-done(((bf16[8,1024,256]{2,1,0:T(8,128)(2,1)}), bf16[8,1024,256]{2,1,0:T(8,128)(2,1)}, u32[]{:S(2)}, u32[]{:S(2)}) %all-to-all-start.1) | async-done | bytes 4194336 | tf_op jit(solution)/shard_map/all_to_all | solution.py:132
  139.5 6.4 %copy.83 = bf16[8,1024,256]{1,2,0:T(8,128)(2,1)} copy(bf16[8,1024,256]{2,1,0:T(8,128)(2,1)} %all-to-all-done.1) | data formatting | bytes 8388608 | tf_op jit(solution)/shard_map/all_to_all | solution.py:132
  145.9 5.9 %reshape.548 = bf16[64,38,768]{2,1,0:T(8,128)(2,1)} reshape(bf16[2432,768]{1,0:T(8,128)(2,1)} %all-gather.5.cloned.1.call-done) | data formatting | bytes 7471104 | tf_op jit(solution)/shard_map/reshape | solution.py:108
  151.8 3.9 %slice.58 = bf16[64,32,768]{2,1,0:T(8,128)(2,1)} slice(bf16[64,38,768]{2,1,0:T(8,128)(2,1)} %reshape.548), slice={[0:64], [0:32], [0:768]} | slice | bytes 6291456 | tf_op jit(solution)/shard_map/slice | solution.py:109
  156.1 13.1 %all-gather = bf16[1,16,2048]{1,2,0:T(8,128)(2,1)S(1)} all-gather(bf16[1,16,256]{1,2,0:T(8,128)(2,1)S(1)} %copy.94), channel_id=2, replica_groups=mesh['z'=16,'y'=4,'fsdp'=8] {'fsdp'}, dimensions={2}, use_global_device_ids=true | all-gather | bytes 73728 | tf_op jit(solution)/shard_map/all_gather | solution.py:137
  169.2 6.5 %dynamic_update_slice.7 = bf16[1024,2048]{0,1:T(8,128)(2,1)} dynamic-update-slice(bf16[1024,2048]{0,1:T(8,128)(2,1)} %bitcast.136, bf16[16,2048]{0,1:T(8,128)(2,1)S(1)} %bitcast.146, s32[]{:T(128)S(6)} %select_n.121, s32[]{:T(128)} %copy.115) | dynamic-update-slice | bytes 131076 | tf_op jit(solution)/shard_map/dynamic_update_slice | solution.py:138
  175.7 3.3 fusion.21
  188.9 11.5 %while.12 = (s32[]{:T(128)}, bf16[2,512,1,2,128]{4,3,1,0,2:T(2,128)(2,1)S(1)}, s32[2,512]{1,0:T(2,128)S(1)}, s32[2,512]{1,0:T(2,128)S(1)}, bf16[2,512,1,2,128]{4...) while((s32[]{:T(128)}, ...), condition=%wide.region_17.18_spmd.clone.clone, body=%wide.region_14.17_spmd.clone.clone.sunk | while | flops 551155712 | bytes 17334396 | solution.py:177
  189.6 2.0 fusion.67
  201.7 9.0 %gather_fusion.4 = bf16[2048,256]{1,0:T(8,128)(2,1)} fusion(bf16[1024,256]{1,0:T(8,128)(2,1)S(1)} %copy.89, s32[2048]{0:T(1024)S(1)} %broadcast_clamp_fusion), kind=kCustom, calls=%fused_computation.4 | custom fusion | bytes 2105344 | tf_op jit(solution)/shard_map/jit(_take)/gather | solution.py:198
  210.7 5.9 %all-to-all-start.3 = ((bf16[64,32,1,256]{3,1,2,0:T(8,128)(2,1)}), bf16[64,32,1,256]{3,1,2,0:T(8,128)(2,1)S(1)}, u32[]{:S(2)}, u32[]{:S(2)}) async-start(bf16[64,32,1,256]{3,1,2,0:T(8,128)(2,1)} %bitcast.23), calls=%async_computation.3 | async-start | bytes 2097152 | tf_op jit(solution)/shard_map/all_to_all | solution.py:201
  216.7 17.8 %all-gather.7.cloned.1.call-done = bf16[1024,2048]{1,0:T(8,128)(2,1)} async-done(((bf16[1024,256]{1,0:T(8,128)(2,1)}), bf16[1024,2048]{1,0:T(8,128)(2,1)}) %all-gather.7.cloned.1.call-update) | async-done | bytes 4194320 | tf_op jit(solution)/shard_map/all_gather | solution.py:186
  234.5 3.7 %convolution_convert_fusion = bf16[1024,256]{1,0:T(8,128)(2,1)S(1)} fusion(bf16[1024,2048]{1,0:T(8,128)(2,1)} %all-gather.7.cloned.1.call-done, bf16[2048,768]{1,0:T(8,128)(2,1)} %bitcast.141), kind=kOutput, calls=%fused_computation.38 | convolution fusion | flops 1074003968 | bytes 5767168 | tf_op jit(solution)/shard_map/dot_general | solution.py:187
  238.2 9.0 %gather_fusion.2 = bf16[2048,256]{1,0:T(8,128)(2,1)} fusion(bf16[1024,256]{1,0:T(8,128)(2,1)S(1)} %convolution_convert_fusion, s32[2048]{0:T(1024)S(1)} %broadcast_clamp_fusion), kind=kCustom, calls=%fused_computation.2 | custom fusion | bytes 2105344 | tf_op jit(solution)/shard_map/jit(_take)/gather | solution.py:198
  247.2 25.2 %all-to-all-done.3 = bf16[64,32,1,256]{3,1,2,0:T(8,128)(2,1)S(1)} async-done(((bf16[64,32,1,256]{3,1,2,0:T(8,128)(2,1)}), bf16[64,32,1,256]{3,1,2,0:T(8,128)(2,1)S(1)}, u32[]{:S(2)}, u32[]{:S(2)}) %all-to-all-start.3) | async-done | bytes 1048608 | tf_op jit(solution)/shard_map/all_to_all | solution.py:201
  272.4 5.9 %all-to-all-start.2 = ((bf16[64,32,256]{2,1,0:T(8,128)(2,1)}), bf16[64,32,256]{2,1,0:T(8,128)(2,1)S(1)}, u32[]{:S(2)}, u32[]{:S(2)}) async-start(bf16[64,32,256]{2,1,0:T(8,128)(2,1)} %bitcast.140), calls=%async_computation.2 | async-start | bytes 2097152 | tf_op jit(solution)/shard_map/all_to_all | solution.py:201
  278.5 5.0 %gather_fusion.5 = bf16[1024,256]{1,0:T(8,128)(2,1)} fusion(bf16[2048,256]{1,0:T(8,128)(2,1)S(1)} %bitcast.137, s32[1024]{0:T(1024)S(1)} %broadcast_clamp_fusion.1), kind=kCustom, calls=%fused_computation.5 | custom fusion | bytes 1052672 | tf_op jit(solution)/shard_map/jit(_take)/gather | solution.py:202
  283.5 49.7 %all-to-all-done.2 = bf16[64,32,256]{2,1,0:T(8,128)(2,1)S(1)} async-done(((bf16[64,32,256]{2,1,0:T(8,128)(2,1)}), bf16[64,32,256]{2,1,0:T(8,128)(2,1)S(1)}, u32[]{:S(2)}, u32[]{:S(2)}) %all-to-all-start.2) | async-done | bytes 1048608 | tf_op jit(solution)/shard_map/all_to_all | solution.py:201
  333.2 5.0 %gather_fusion.3 = bf16[1024,256]{1,0:T(8,128)(2,1)} fusion(bf16[2048,256]{1,0:T(8,128)(2,1)S(1)} %bitcast.138, s32[1024]{0:T(1024)S(1)} %broadcast_clamp_fusion.1), kind=kCustom, calls=%fused_computation.3 | custom fusion | bytes 1052672 | tf_op jit(solution)/shard_map/jit(_take)/gather | solution.py:202
  (109 shorter events, 31.7 us)
Async XLA Ops:
  7.2 4.9 %copy-start = (bf16[1024,256]{1,0:T(8,128)(2,1)S(1)}, bf16[1024,256]{1,0:T(8,128)(2,1)}, u32[]{:S(2)}) copy-start(bf16[1024,256]{1,0:T(8,128)(2,1)} %param.12) | copy-start | bytes 1572868
  7.2 138.7 %all-gather.5.cloned.1.call-start = ((), (), s32[]{:S(2)}) async-start(), calls=%async_computation.4 | async-start | bytes 3969024 | tf_op jit(solution)/shard_map/all_gather | solution.py:107
  30.8 51.5 %all-to-all-start = ((bf16[64,16,256]{2,1,0:T(8,128)(2,1)}), bf16[64,16,256]{2,1,0:T(8,128)(2,1)S(1)}, u32[]{:S(2)}, u32[]{:S(2)}) async-start(bf16[64,16,256]{2,1,0:T(8,128)(2,1)} %gather_fusion), calls=%async_computation | async-start | bytes 1048576 | tf_op jit(solution)/shard_map/all_to_all | solution.py:117
  85.1 6.8 %copy-start.4 = (bf16[2048]{0:T(1024)(128)(2,1)S(1)}, bf16[2048]{0:T(1024)(128)(2,1)}, u32[]{:S(2)}) copy-start(bf16[2048]{0:T(1024)(128)(2,1)} %param.13) | copy-start | bytes 12292
  85.1 6.8 %copy-start.6 = (bf16[128]{0:T(256)(128)(2,1)S(1)}, bf16[128]{0:T(256)(128)(2,1)}, u32[]{:S(2)}) copy-start(bf16[128]{0:T(256)(128)(2,1)} %param.15) | copy-start | bytes 772
  85.1 6.8 %copy-start.5 = (s32[64,8]{0,1:T(8,128)S(1)}, s32[64,8]{0,1:T(8,128)}, u32[]{:S(2)}) copy-start(s32[64,8]{0,1:T(8,128)} %param.20) | copy-start | bytes 6148
  85.1 7.2 %copy-start.7 = (bf16[128]{0:T(256)(128)(2,1)S(1)}, bf16[128]{0:T(256)(128)(2,1)}, u32[]{:S(2)}) copy-start(bf16[128]{0:T(256)(128)(2,1)} %param.14) | copy-start | bytes 772
  85.1 54.3 %all-to-all-start.1 = ((bf16[8,1024,256]{2,1,0:T(8,128)(2,1)}), bf16[8,1024,256]{2,1,0:T(8,128)(2,1)}, u32[]{:S(2)}, u32[]{:S(2)}) async-start(bf16[8,1024,256]{2,1,0:T(8,128)(2,1)} %broadcast_in_dim.118), calls=%async_computation.1 | async-start | bytes 8388608 | tf_op jit(solution)/shard_map/all_to_all | solution.py:132
  89.8 144.7 %all-gather.7.cloned.1.call-start = ((), (), s32[]{:S(2)}) async-start(), calls=%async_computation.5 | async-start | bytes 4718592 | tf_op jit(solution)/shard_map/all_gather | solution.py:186
  151.8 3.9 %slice-start = ((bf16[64,38,768]{2,1,0:T(8,128)(2,1)}), bf16[64,6,768]{2,1,0:T(8,128)(2,1)S(1)}, s32[]{:S(2)}) async-start(bf16[64,38,768]{2,1,0:T(8,128)(2,1)} %reshape.548), calls=%async_computation.6 | async-start | bytes 1572864 | tf_op jit(solution)/shard_map/slice | solution.py:111
  175.7 3.4 copy-start.1
  179.2 1.9 copy-start.2
  189.6 3.2 copy-start.3
  195.3 3.2 copy-start.3
  210.7 61.6 %all-to-all-start.3 = ((bf16[64,32,1,256]{3,1,2,0:T(8,128)(2,1)}), bf16[64,32,1,256]{3,1,2,0:T(8,128)(2,1)S(1)}, u32[]{:S(2)}, u32[]{:S(2)}) async-start(bf16[64,32,1,256]{3,1,2,0:T(8,128)(2,1)} %bitcast.23), calls=%async_computation.3 | async-start | bytes 2097152 | tf_op jit(solution)/shard_map/all_to_all | solution.py:201
  272.4 60.8 %all-to-all-start.2 = ((bf16[64,32,256]{2,1,0:T(8,128)(2,1)}), bf16[64,32,256]{2,1,0:T(8,128)(2,1)S(1)}, u32[]{:S(2)}, u32[]{:S(2)}) async-start(bf16[64,32,256]{2,1,0:T(8,128)(2,1)} %bitcast.140), calls=%async_computation.2 | async-start | bytes 2097152 | tf_op jit(solution)/shard_map/all_to_all | solution.py:201
Sparse Core Ops, SparseCore 0:
  28.4 95.1 all-gather.4
  201.4 32.9 all-gather.6

commit v6 on v5

--- a/solution.py
+++ b/solution.py
@@ -98,20 +98,12 @@
 
     weights = jnp.concatenate([w_query, w_key, w_value, w_out], axis=1)
     weight_rows, weight_width = weights.shape
-    dup_size = arrival_rows * width_local
-    dup_rows = -(-dup_size // weight_width)
-    dup_flat = jnp.pad(dup_tokens.reshape(-1), (0, dup_rows * weight_width - dup_size))
-    packed = jnp.concatenate([weights, dup_flat.reshape(dup_rows, weight_width)], axis=0)
+    packed = jnp.concatenate([weights, dup_tokens.reshape(weight_rows, -1)], axis=1)
     packed = lax.all_gather(packed, "y", axis=0, tiled=True)
     packed, token_blocks = lax.optimization_barrier((packed, token_blocks))
     packed = lax.all_gather(packed, "z", axis=0, tiled=True)
-    packed = packed.reshape(groups, weight_rows + dup_rows, weight_width)
-    weights = packed[:, :weight_rows].reshape(groups * weight_rows, weight_width)
-    dup_all = (
-        packed[:, weight_rows:]
-        .reshape(groups, -1)[:, :dup_size]
-        .reshape(groups, arrival_rows, width_local)
-    )
+    weights = packed[:, :weight_width]
+    dup_all = packed[:, weight_width:].reshape(groups, arrival_rows, width_local)
 
     outgoing = jnp.take(token_blocks, slot_source, axis=0, mode="clip")
     incoming = lax.all_to_all(outgoing, DP, split_axis=0, concat_axis=0, tiled=True)
@@ -129,13 +121,12 @@
     arrived = jnp.take(incoming, source_of, axis=0, mode="clip").reshape(group_rows, width_local)
     fsdp_size = lax.axis_size("fsdp")
     spread = jnp.broadcast_to(arrived[None], (fsdp_size,) + arrived.shape)
-    full_rows = lax.all_to_all(spread, "fsdp", split_axis=0, concat_axis=2, tiled=True)
-    full_rows = full_rows.reshape(group_rows, width_local * fsdp_size)
+    pieces = lax.all_to_all(spread, "fsdp", split_axis=0, concat_axis=0, tiled=True)
     dup_source = jnp.sum(jnp.where(counts == 2, block_ids, 0))
     dup_target = jnp.sum(jnp.where(counts == 2, offsets + 1, 0))
     dup_mine = lax.dynamic_index_in_dim(dup_all, dup_source, 0, keepdims=False)
-    dup_full = lax.all_gather(dup_mine, "fsdp", axis=1, tiled=True)
-    full_rows = lax.dynamic_update_slice_in_dim(full_rows, dup_full, dup_target * arrival_rows, 0)
+    dup_pieces = lax.all_gather(dup_mine, "fsdp", axis=0, tiled=False)
+    pieces = lax.dynamic_update_slice_in_dim(pieces, dup_pieces, dup_target * arrival_rows, 1)
     cuts = [w_query.shape[1], w_key.shape[1], w_value.shape[1], w_out.shape[1]]
     bounds = [sum(cuts[:k]) for k in range(5)]
     query_full, key_full, value_full, out_full = (
@@ -144,23 +135,24 @@
     lengths = lax.dynamic_index_in_dim(prompt_lengths, device_index, 0, keepdims=False)
     position, starts = prompt_layout(lengths, group_rows)
     within = position - starts
-    floats = full_rows.astype(jnp.float32)
+    floats = pieces.astype(jnp.float32)
     normed = (
         floats
-        * lax.rsqrt(jnp.mean(floats * floats, axis=-1, keepdims=True) + epsilon)
-        * norm_gain.astype(jnp.float32)
+        * lax.rsqrt(jnp.mean(floats * floats, axis=(0, 2), keepdims=True) + epsilon)
+        * norm_gain.astype(jnp.float32).reshape(fsdp_size, 1, width_local)
     ).astype(jnp.bfloat16)
-    query = jnp.dot(normed, query_full, preferred_element_type=jnp.float32).reshape(
-        group_rows, -1, HD
-    )
-    key_rows = jnp.dot(normed, key_full, preferred_element_type=jnp.float32).reshape(
-        group_rows, -1, HD
-    )
-    value_rows = (
-        jnp.dot(normed, value_full, preferred_element_type=jnp.float32)
-        .reshape(group_rows, -1, HD)
-        .astype(jnp.bfloat16)
-    )
+
+    def project(matrix):
+        return jnp.einsum(
+            "fnk,fkc->nc",
+            normed,
+            matrix.reshape(fsdp_size, width_local, -1),
+            preferred_element_type=jnp.float32,
+        )
+
+    query = project(query_full).reshape(group_rows, -1, HD)
+    key_rows = project(key_full).reshape(group_rows, -1, HD)
+    value_rows = project(value_full).reshape(group_rows, -1, HD).astype(jnp.bfloat16)
     query_rot = rotate(head_norm(query, query_gain), within).astype(jnp.bfloat16)
     key_rot = rotate(head_norm(key_rows, key_gain), within).astype(jnp.bfloat16)
     kv_heads = key_rot.shape[1]
@@ -185,24 +177,21 @@
     mixed = mixed.reshape(group_rows, kv_heads * group_ratio * HD)
     heads_all = lax.all_gather(mixed, "fsdp", axis=1, tiled=True)
     update = jnp.dot(heads_all, out_full, preferred_element_type=jnp.float32).astype(jnp.bfloat16)
-    slot_ids = jnp.arange(2 * arrival_rows, dtype=jnp.int32)
-    row_valid = slot_ids[None, :] < arrival_rows * counts[:, None]
-    row_target = jnp.where(row_valid, arrival_rows * offsets[:, None] + slot_ids[None, :], 0)
-    row_back = row_target.reshape(-1)
-    row_mine = (
-        (own_blocks * 2 + dup_rank)[:, None] * arrival_rows
-        + jnp.arange(arrival_rows, dtype=jnp.int32)[None, :]
+    sub_ids = jnp.arange(2, dtype=jnp.int32)
+    block_back = jnp.where(
+        sub_ids[None, :] < counts[:, None], offsets[:, None] + sub_ids[None, :], 0
     ).reshape(-1)
+    block_mine = own_blocks * 2 + dup_rank
 
     def send_back(rows):
-        sent = jnp.take(rows, row_back, axis=0, mode="clip").reshape(
-            (groups, 2 * arrival_rows) + rows.shape[1:]
-        )
+        tail = rows.shape[1:]
+        sent = jnp.take(
+            rows.reshape((groups, arrival_rows) + tail), block_back, axis=0, mode="clip"
+        ).reshape((groups, 2 * arrival_rows) + tail)
         back = lax.all_to_all(sent, DP, split_axis=0, concat_axis=0, tiled=True)
         return jnp.take(
-            back.reshape((groups * 2 * arrival_rows,) + rows.shape[1:]), row_mine, axis=0, mode="clip"
-        )
-
+            back.reshape((groups * 2, arrival_rows) + tail), block_mine, axis=0, mode="clip"
+        ).reshape(rows.shape)
     cache_out = send_back(cache_rows)
     attention_out = send_back(update)
     return (attention_out, cache_out)

time: 346 us -> 312 us (0.902)
  local copies, waits for them, and re-layouts: 65 us -> 23.7 us
  blocking collectives: 27.7 us -> 35.7 us
  matrix products: 13.8 us -> 20.6 us
  waiting for transfers between devices: 172 us -> 166 us
    all_to_all x1, waiting for transfers between devices: 45.3 us -> 0.01 us  [local(): lax.all_to_all(spread, 'fsdp', split_axis=0, concat_axis=0, tiled=True)]
    all_gather x1, waiting for transfers between devices: 0.01 us -> 28.2 us  [local(): packed = lax.all_gather(packed, 'z', axis=0, tiled=True)]
    gather x4, local copies, waits for them, and re-layouts: 28 us -> 6.03 us  [the longest x2 3.25 us: send_back(): jnp.take(rows.reshape((groups, arrival_rows) + tail), block_back, axis=0,...]
    dot_general x3, matrix products: 2.9 us -> 11.7 us  [project(): jnp.einsum('fnk,fkc->nc', normed, matrix.reshape(fsdp_size, width_local,...]
    all_gather x1, waiting for transfers between devices: 17.8 us -> 25.5 us  [local(): heads_all = lax.all_gather(mixed, 'fsdp', axis=1, tiled=True)]
    all_gather x1, blocking collectives: 13.1 us -> 20.5 us  [local(): dup_pieces = lax.all_gather(dup_mine, 'fsdp', axis=0, tiled=False)]
    all_to_all x1 -> x0, local copies, waits for them, and re-layouts: 6.44 us -> none  [local(): lax.all_to_all(spread, 'fsdp', split_axis=0, concat_axis=2, tiled=True)]
    dynamic_update_slice x1, local copies, waits for them, and re-layouts: 6.49 us -> 0.63 us  [local(): lax.dynamic_update_slice_in_dim(pieces, dup_pieces, dup_target * arrival_...]
  transfers between devices with their start and end apart: 6 -> 6, of which waited for: 5 -> 5; matrix products, arithmetic and copies ran while one was open for 12% -> 6% of each run, Pallas kernels for 0% -> 0%
where the time goes in v6:
time: 312 us; the launch traced here: 311 us
  waiting for transfers between devices  166 us (53%)
  blocking collectives  35.7 us (11%)
  starting transfers between devices  32.6 us (10%)
  local copies, waits for them, and re-layouts  23.7 us (8%)
  matrix products  20.6 us (7%)
  between operations  19.2 us (6%)
  other arithmetic  13.4 us (4%)
    all_to_all x2, waiting for transfers between devices, send_back(): back = lax.all_to_all(sent, DP, split_axis=0, concat_axis=0, tiled=True)  78.3 us
    all_to_all x1, waiting for transfers between devices, local(): lax.all_to_all(outgoing, DP, split_axis=0, concat_axis=0, tiled=True)  33.7 us
    all_gather x1, waiting for transfers between devices, local(): packed = lax.all_gather(packed, 'z', axis=0, tiled=True)  28.2 us
    all_gather x1, waiting for transfers between devices, local(): heads_all = lax.all_gather(mixed, 'fsdp', axis=1, tiled=True)  25.5 us
    all_gather x1, blocking collectives, local(): dup_pieces = lax.all_gather(dup_mine, 'fsdp', axis=0, tiled=False)  20.5 us
    all_to_all x1, starting transfers between devices, local(): lax.all_to_all(outgoing, DP, split_axis=0, concat_axis=0, tiled=True)  16.1 us
    all_gather x1, blocking collectives, local(): packed = lax.all_gather(packed, 'y', axis=0, tiled=True)  15.3 us
    all_to_all x2, starting transfers between devices, send_back(): back = lax.all_to_all(sent, DP, split_axis=0, concat_axis=0, tiled=True)  11.8 us
  transfers between devices with their start and end apart: 6, of which 5 were waited for; matrix products, arithmetic and copies ran while one was open for 6% of the time, Pallas kernels for 0%

profile of v6, /device:TPU:24, one launch (start us, length us, event | category | flops | bytes accessed | tf_op | source)
XLA Modules:
  0.0 311.1 jit_solution(3458453829169546722)
XLA Ops:
  14.9 15.3 %all_gather.13 = bf16[128,896]{1,0:T(8,128)(2,1)} all-gather(bf16[32,896]{1,0:T(8,128)(2,1)S(1)} %constant_dynamic-update-slice_fusion), channel_id=1, replica_groups=mesh['z'=16,'y'=4,'fsdp'=8] {'y'}, dimensions={0}, use_global_device_ids=true | all-gather | bytes 286720 | tf_op jit(solution)/shard_map/all_gather | solution.py:102
  32.7 16.1 %all-to-all-start = ((bf16[64,16,256]{2,1,0:T(8,128)(2,1)}), bf16[64,16,256]{2,1,0:T(8,128)(2,1)S(1)}, u32[]{:S(2)}, u32[]{:S(2)}) async-start(bf16[64,16,256]{2,1,0:T(8,128)(2,1)} %gather_fusion), calls=%async_computation | async-start | bytes 1048576 | tf_op jit(solution)/shard_map/all_to_all | solution.py:109
  50.4 33.7 %all-to-all-done = bf16[64,16,256]{2,1,0:T(8,128)(2,1)S(1)} async-done(((bf16[64,16,256]{2,1,0:T(8,128)(2,1)}), bf16[64,16,256]{2,1,0:T(8,128)(2,1)S(1)}, u32[]{:S(2)}, u32[]{:S(2)}) %all-to-all-start) | async-done | bytes 524320 | tf_op jit(solution)/shard_map/all_to_all | solution.py:109
  84.7 2.2 broadcast_in_dim.115
  87.0 4.7 %all-to-all-start.1 = ((bf16[8,1024,256]{2,1,0:T(8,128)(2,1)}), bf16[8,1024,256]{2,1,0:T(8,128)(2,1)}, u32[]{:S(2)}, u32[]{:S(2)}) async-start(bf16[8,1024,256]{2,1,0:T(8,128)(2,1)} %broadcast_in_dim.115), calls=%async_computation.1 | async-start | bytes 8388608 | tf_op jit(solution)/shard_map/all_to_all | solution.py:124
  94.9 1.8 multiply_cosine_fusion.1
  96.7 28.2 %all-gather.3.cloned.1.call-done = bf16[2048,896]{1,0:T(8,128)(2,1)} async-done(((bf16[128,896]{1,0:T(8,128)(2,1)}), bf16[2048,896]{1,0:T(8,128)(2,1)}) %all-gather.3.cloned.1.call-update) | async-done | bytes 3670032 | tf_op jit(solution)/shard_map/all_gather | solution.py:104
  125.0 1.5 fusion.58
  126.7 20.5 %all_gather.15 = bf16[8,16,256]{2,1,0:T(8,128)(2,1)S(1)} all-gather(bf16[1,16,256]{2,1,0:T(8,128)(2,1)S(1)} %constant_dynamic-slice_fusion.2), channel_id=1, replica_groups=mesh['z'=16,'y'=4,'fsdp'=8] {'fsdp'}, dimensions={0}, use_global_device_ids=true | all-gather | bytes 73728 | tf_op jit(solution)/shard_map/all_gather | solution.py:128
  147.8 3.1 fusion.21
  150.8 4.2 %fusion.29 = bf16[1024,128]{1,0:T(8,128)(2,1)} fusion(bf16[8,256,128]{2,1,0:T(8,128)(2,1)S(1)} %bitcast.153, bf16[8,1024,256]{2,1,0:T(8,128)(2,1)} %constant_dynamic-update-slice_fusion.5, f32[8,256]{1,0:T(8,128)S(1)} %reshape.576, f32[1024]{0:T(1024)S(1)} %add_rsqrt_fusion.2), kind=kOutput, calls=%fused_computation.44 | convolution fusion | flops 545390592 | bytes 4993024 | tf_op jit(solution)/shard_map/fnk,fkc->nc/dot_general | solution.py:146
  155.0 3.7 %multiply_reduce_fusion.1 = (f32[1024]{0:T(1024)S(1)}, f32[1024,128]{0,1:T(8,128)S(1)}) fusion(bf16[8,256,128]{2,1,0:T(8,128)(2,1)S(1)} %bitcast.152, bf16[8,1024,256]{2,1,0:T(8,128)(2,1)} %constant_dynamic-update-slice_fusion.5, f32[8,256]{1,0:T(8,128)S(1)} %reshape.576, f32[1024]{0:T(1024)S(1)} %add_rsqrt_fusion.2), kind=kOutput, calls=%fused_computation.53 | convolution fusion | flops 545520640 | bytes 5259264 | tf_op jit(solution)/shard_map/fnk,fkc->nc/dot_general | solution.py:146
  162.1 3.8 %multiply_reduce_fusion = (f32[1024,2]{0,1:T(2,128)S(1)}, f32[1024,2,128]{0,2,1:T(8,128)S(1)}) fusion(bf16[2,128,8,256]{3,2,1,0:T(8,128)(2,1)S(1)} %bitcast.148, f32[8,256]{1,0:T(8,128)S(1)} %reshape.576, f32[1024]{0:T(1024)S(1)} %add_rsqrt_fusion.2, bf16[8,1024,256]{2,1,0:T(8,128)(2,1)} %constant_dynamic-update-slice_fusion.5), kind=kOutput, calls=%fused_computation.48 | convolution fusion | flops 1082652672 | bytes 6311936 | tf_op jit(solution)/shard_map/fnk,fkc->nc/dot_general | solution.py:146
  167.7 9.4 %while.12 = (s32[]{:T(128)}, bf16[2,512,1,2,128]{4,3,1,0,2:T(2,128)(2,1)S(1)}, s32[2,512]{1,0:T(2,128)S(1)}, s32[2,512]{1,0:T(2,128)S(1)}, bf16[2,512,1,2,128]{4...) while((s32[]{:T(128)}, ...), condition=%wide.region_17.18_spmd.clone.clone, body=%wide.region_14.17_spmd.clone.clone.sunk | while | flops 551155712 | bytes 16285793 | solution.py:169
  170.6 1.6 fusion.73
  175.3 1.6 fusion.73
  178.9 1.6 gather_fusion.4
  180.5 5.8 %all-to-all-start.3 = ((bf16[64,32,1,256]{3,1,2,0:T(8,128)(2,1)}), bf16[64,32,1,256]{3,1,2,0:T(8,128)(2,1)S(1)}, u32[]{:S(2)}, u32[]{:S(2)}) async-start(bf16[64,32,1,256]{3,1,2,0:T(8,128)(2,1)} %bitcast.31), calls=%async_computation.3 | async-start | bytes 2097152 | tf_op jit(solution)/shard_map/all_to_all | solution.py:191
  186.4 25.5 %all-gather.5.cloned.1.call-done = bf16[1024,2048]{1,0:T(8,128)(2,1)} async-done(((bf16[1024,256]{1,0:T(8,128)(2,1)}), bf16[1024,2048]{1,0:T(8,128)(2,1)}) %all-gather.5.cloned.1.call-update) | async-done | bytes 4194320 | tf_op jit(solution)/shard_map/all_gather | solution.py:178
  211.9 3.7 %convolution_convert_fusion = bf16[1024,256]{1,0:T(8,128)(2,1)S(1)} fusion(bf16[1024,2048]{1,0:T(8,128)(2,1)} %all-gather.5.cloned.1.call-done, bf16[2048,896]{1,0:T(8,128)(2,1)} %all-gather.3.cloned.1.call-done), kind=kOutput, calls=%fused_computation.41 | convolution fusion | flops 1074003968 | bytes 5767168 | tf_op jit(solution)/shard_map/dot_general | solution.py:179
  215.7 1.6 gather_fusion.2
  217.3 24.8 %all-to-all-done.3 = bf16[64,32,1,256]{3,1,2,0:T(8,128)(2,1)S(1)} async-done(((bf16[64,32,1,256]{3,1,2,0:T(8,128)(2,1)}), bf16[64,32,1,256]{3,1,2,0:T(8,128)(2,1)S(1)}, u32[]{:S(2)}, u32[]{:S(2)}) %all-to-all-start.3) | async-done | bytes 1048608 | tf_op jit(solution)/shard_map/all_to_all | solution.py:191
  242.1 5.9 %all-to-all-start.2 = ((bf16[64,32,256]{2,1,0:T(8,128)(2,1)}), bf16[64,32,256]{2,1,0:T(8,128)(2,1)S(1)}, u32[]{:S(2)}, u32[]{:S(2)}) async-start(bf16[64,32,256]{2,1,0:T(8,128)(2,1)} %bitcast.24), calls=%async_computation.2 | async-start | bytes 2097152 | tf_op jit(solution)/shard_map/all_to_all | solution.py:191
  249.4 53.5 %all-to-all-done.2 = bf16[64,32,256]{2,1,0:T(8,128)(2,1)S(1)} async-done(((bf16[64,32,256]{2,1,0:T(8,128)(2,1)}), bf16[64,32,256]{2,1,0:T(8,128)(2,1)S(1)}, u32[]{:S(2)}, u32[]{:S(2)}) %all-to-all-start.2) | async-done | bytes 1048608 | tf_op jit(solution)/shard_map/all_to_all | solution.py:191
  (105 shorter events, 27.5 us)
Async XLA Ops:
  7.2 4.9 %copy-start = (bf16[1024,256]{1,0:T(8,128)(2,1)S(1)}, bf16[1024,256]{1,0:T(8,128)(2,1)}, u32[]{:S(2)}) copy-start(bf16[1024,256]{1,0:T(8,128)(2,1)} %param.12) | copy-start | bytes 1572868
  7.2 117.8 %all-gather.3.cloned.1.call-start = ((), (), s32[]{:S(2)}) async-start(), calls=%async_computation.4 | async-start | bytes 3899392 | tf_op jit(solution)/shard_map/all_gather | solution.py:104
  32.7 51.4 %all-to-all-start = ((bf16[64,16,256]{2,1,0:T(8,128)(2,1)}), bf16[64,16,256]{2,1,0:T(8,128)(2,1)S(1)}, u32[]{:S(2)}, u32[]{:S(2)}) async-start(bf16[64,16,256]{2,1,0:T(8,128)(2,1)} %gather_fusion), calls=%async_computation | async-start | bytes 1048576 | tf_op jit(solution)/shard_map/all_to_all | solution.py:109
  86.9 6.8 %copy-start.6 = (bf16[2048]{0:T(1024)(128)(2,1)S(1)}, bf16[2048]{0:T(1024)(128)(2,1)}, u32[]{:S(2)}) copy-start(bf16[2048]{0:T(1024)(128)(2,1)} %param.13) | copy-start | bytes 12292
  86.9 6.8 %copy-start.8 = (bf16[128]{0:T(256)(128)(2,1)S(1)}, bf16[128]{0:T(256)(128)(2,1)}, u32[]{:S(2)}) copy-start(bf16[128]{0:T(256)(128)(2,1)} %param.15) | copy-start | bytes 772
  86.9 6.8 %copy-start.7 = (s32[64,8]{0,1:T(8,128)S(1)}, s32[64,8]{0,1:T(8,128)}, u32[]{:S(2)}) copy-start(s32[64,8]{0,1:T(8,128)} %param.20) | copy-start | bytes 6148
  86.9 7.2 %copy-start.9 = (bf16[128]{0:T(256)(128)(2,1)S(1)}, bf16[128]{0:T(256)(128)(2,1)}, u32[]{:S(2)}) copy-start(bf16[128]{0:T(256)(128)(2,1)} %param.14) | copy-start | bytes 772
  87.0 60.2 %all-to-all-start.1 = ((bf16[8,1024,256]{2,1,0:T(8,128)(2,1)}), bf16[8,1024,256]{2,1,0:T(8,128)(2,1)}, u32[]{:S(2)}, u32[]{:S(2)}) async-start(bf16[8,1024,256]{2,1,0:T(8,128)(2,1)} %broadcast_in_dim.115), calls=%async_computation.1 | async-start | bytes 8388608 | tf_op jit(solution)/shard_map/all_to_all | solution.py:124
  91.6 120.3 %all-gather.5.cloned.1.call-start = ((), (), s32[]{:S(2)}) async-start(), calls=%async_computation.5 | async-start | bytes 4718592 | tf_op jit(solution)/shard_map/all_gather | solution.py:178
  158.8 2.3 slice-start
  162.1 4.1 %copy-start.1 = (f32[1024,64]{0,1:T(8,128)S(1)}, f32[1024,64]{0,1:T(8,128)}, u32[]{:S(2)}) copy-start(f32[1024,64]{0,1:T(8,128)} %get-tuple-element.151) | copy-start | bytes 786436
  162.1 4.1 %copy-start.2 = (f32[1024,64]{0,1:T(8,128)S(1)}, f32[1024,64]{0,1:T(8,128)}, u32[]{:S(2)}) copy-start(f32[1024,64]{0,1:T(8,128)} %get-tuple-element.152) | copy-start | bytes 786436
  166.0 1.7 copy-start.3
  166.0 1.7 copy-start.4
  166.0 1.7 copy-start.5
  180.5 61.6 %all-to-all-start.3 = ((bf16[64,32,1,256]{3,1,2,0:T(8,128)(2,1)}), bf16[64,32,1,256]{3,1,2,0:T(8,128)(2,1)S(1)}, u32[]{:S(2)}, u32[]{:S(2)}) async-start(bf16[64,32,1,256]{3,1,2,0:T(8,128)(2,1)} %bitcast.31), calls=%async_computation.3 | async-start | bytes 2097152 | tf_op jit(solution)/shard_map/all_to_all | solution.py:191
  242.1 60.8 %all-to-all-start.2 = ((bf16[64,32,256]{2,1,0:T(8,128)(2,1)}), bf16[64,32,256]{2,1,0:T(8,128)(2,1)S(1)}, u32[]{:S(2)}, u32[]{:S(2)}) async-start(bf16[64,32,256]{2,1,0:T(8,128)(2,1)} %bitcast.24), calls=%async_computation.2 | async-start | bytes 2097152 | tf_op jit(solution)/shard_map/all_to_all | solution.py:191
Sparse Core Ops, SparseCore 0:
  30.3 94.5 all-gather.2
  178.2 33.7 all-gather.4

commit v7 on v6

--- a/solution.py
+++ b/solution.py
@@ -125,8 +125,8 @@
     dup_source = jnp.sum(jnp.where(counts == 2, block_ids, 0))
     dup_target = jnp.sum(jnp.where(counts == 2, offsets + 1, 0))
     dup_mine = lax.dynamic_index_in_dim(dup_all, dup_source, 0, keepdims=False)
-    dup_pieces = lax.all_gather(dup_mine, "fsdp", axis=0, tiled=False)
-    pieces = lax.dynamic_update_slice_in_dim(pieces, dup_pieces, dup_target * arrival_rows, 1)
+    dup_spread = jnp.broadcast_to(dup_mine[None], (fsdp_size,) + dup_mine.shape)
+    dup_pieces = lax.all_to_all(dup_spread, "fsdp", split_axis=0, concat_axis=0, tiled=True)
     cuts = [w_query.shape[1], w_key.shape[1], w_value.shape[1], w_out.shape[1]]
     bounds = [sum(cuts[:k]) for k in range(5)]
     query_full, key_full, value_full, out_full = (
@@ -135,14 +135,15 @@
     lengths = lax.dynamic_index_in_dim(prompt_lengths, device_index, 0, keepdims=False)
     position, starts = prompt_layout(lengths, group_rows)
     within = position - starts
-    floats = pieces.astype(jnp.float32)
-    normed = (
-        floats
-        * lax.rsqrt(jnp.mean(floats * floats, axis=(0, 2), keepdims=True) + epsilon)
-        * norm_gain.astype(jnp.float32).reshape(fsdp_size, 1, width_local)
-    ).astype(jnp.bfloat16)
-
-    def project(matrix):
+    def normalize(parts):
+        floats = parts.astype(jnp.float32)
+        return (
+            floats
+            * lax.rsqrt(jnp.mean(floats * floats, axis=(0, 2), keepdims=True) + epsilon)
+            * norm_gain.astype(jnp.float32).reshape(fsdp_size, 1, width_local)
+        ).astype(jnp.bfloat16)
+
+    def project(normed, matrix):
         return jnp.einsum(
             "fnk,fkc->nc",
             normed,
@@ -150,9 +151,16 @@
             preferred_element_type=jnp.float32,
         )
 
-    query = project(query_full).reshape(group_rows, -1, HD)
-    key_rows = project(key_full).reshape(group_rows, -1, HD)
-    value_rows = project(value_full).reshape(group_rows, -1, HD).astype(jnp.bfloat16)
+    def with_dup(matrix):
+        main = project(normed_main, matrix)
+        extra = project(normed_dup, matrix)
+        return lax.dynamic_update_slice_in_dim(main, extra, dup_target * arrival_rows, 0)
+
+    normed_main = normalize(pieces)
+    normed_dup = normalize(dup_pieces)
+    query = with_dup(query_full).reshape(group_rows, -1, HD)
+    key_rows = with_dup(key_full).reshape(group_rows, -1, HD)
+    value_rows = with_dup(value_full).reshape(group_rows, -1, HD).astype(jnp.bfloat16)
     query_rot = rotate(head_norm(query, query_gain), within).astype(jnp.bfloat16)
     key_rot = rotate(head_norm(key_rows, key_gain), within).astype(jnp.bfloat16)
     kv_heads = key_rot.shape[1]

time: 312 us -> 326 us (1.045)
  blocking collectives: 35.7 us -> 15.3 us
  waiting for transfers between devices: 166 us -> 181 us
  other arithmetic: 13.4 us -> 24.9 us
  starting transfers between devices: 32.6 us -> 36 us
    all_to_all x1, waiting for transfers between devices: 0.01 us -> 44 us  [local(): lax.all_to_all(spread, 'fsdp', split_axis=0, concat_axis=0, tiled=True)]
    all_gather x1, waiting for transfers between devices: 28.2 us -> 0.01 us  [local(): packed = lax.all_gather(packed, 'z', axis=0, tiled=True)]
    all_gather x1 -> x0, blocking collectives: 20.5 us -> none  [local(): dup_pieces = lax.all_gather(dup_mine, 'fsdp', axis=0, tiled=False)]
    convert_element_type x0 -> x1, other arithmetic: none -> 5.18 us  [normalize(): return (floats * lax.rsqrt(jnp.mean(floats * floats, axis=(0, 2), keepdim...]
    all_to_all x0 -> x1, starting transfers between devices: none -> 3.35 us  [local(): lax.all_to_all(dup_spread, 'fsdp', split_axis=0, concat_axis=0, tiled=True)]
    dot_general x3 -> x6, matrix products: 11.7 us -> 10 us  [project(): jnp.einsum('fnk,fkc->nc', normed, matrix.reshape(fsdp_size, width_local,...]
  transfers between devices with their start and end apart: 6 -> 7, of which waited for: 5 -> 5; matrix products, arithmetic and copies ran while one was open for 6% -> 12% of each run, Pallas kernels for 0% -> 0%
where the time goes in v7:
time: 326 us; the launch traced here: 324 us
  waiting for transfers between devices  181 us (56%)
  starting transfers between devices  36 us (11%)
  local copies, waits for them, and re-layouts  26.6 us (8%)
  other arithmetic  24.9 us (8%)
  matrix products  21 us (6%)
  between operations  18.9 us (6%)
  blocking collectives  15.3 us (5%)
    all_to_all x2, waiting for transfers between devices, send_back(): back = lax.all_to_all(sent, DP, split_axis=0, concat_axis=0, tiled=True)  77.6 us
    all_to_all x1, waiting for transfers between devices, local(): lax.all_to_all(spread, 'fsdp', split_axis=0, concat_axis=0, tiled=True)  44 us
    all_to_all x1, waiting for transfers between devices, local(): lax.all_to_all(outgoing, DP, split_axis=0, concat_axis=0, tiled=True)  34.1 us
    all_gather x1, waiting for transfers between devices, local(): heads_all = lax.all_gather(mixed, 'fsdp', axis=1, tiled=True)  25.8 us
    all_to_all x1, starting transfers between devices, local(): lax.all_to_all(outgoing, DP, split_axis=0, concat_axis=0, tiled=True)  16.1 us
    all_gather x1, blocking collectives, local(): packed = lax.all_gather(packed, 'y', axis=0, tiled=True)  15.3 us
    all_to_all x2, starting transfers between devices, send_back(): back = lax.all_to_all(sent, DP, split_axis=0, concat_axis=0, tiled=True)  11.6 us
    dot_general x6, matrix products, project(): jnp.einsum('fnk,fkc->nc', normed, matrix.reshape(fsdp_size, width_local,...  10 us
  transfers between devices with their start and end apart: 7, of which 5 were waited for; matrix products, arithmetic and copies ran while one was open for 12% of the time, Pallas kernels for 0%

profile of v7, /device:TPU:24, one launch (start us, length us, event | category | flops | bytes accessed | tf_op | source)
XLA Modules:
  0.0 324.1 jit_solution(15843113511763168172)
XLA Ops:
  15.4 15.3 %all_gather.9 = bf16[128,896]{1,0:T(8,128)(2,1)} all-gather(bf16[32,896]{1,0:T(8,128)(2,1)S(1)} %constant_dynamic-update-slice_fusion), channel_id=1, replica_groups=mesh['z'=16,'y'=4,'fsdp'=8] {'y'}, dimensions={0}, use_global_device_ids=true | all-gather | bytes 286720 | tf_op jit(solution)/shard_map/all_gather | solution.py:102
  33.8 16.1 %all-to-all-start = ((bf16[64,16,256]{2,1,0:T(8,128)(2,1)}), bf16[64,16,256]{2,1,0:T(8,128)(2,1)S(1)}, u32[]{:S(2)}, u32[]{:S(2)}) async-start(bf16[64,16,256]{2,1,0:T(8,128)(2,1)} %gather_fusion), calls=%async_computation | async-start | bytes 1048576 | tf_op jit(solution)/shard_map/all_to_all | solution.py:109
  51.5 34.1 %all-to-all-done = bf16[64,16,256]{2,1,0:T(8,128)(2,1)S(1)} async-done(((bf16[64,16,256]{2,1,0:T(8,128)(2,1)}), bf16[64,16,256]{2,1,0:T(8,128)(2,1)S(1)}, u32[]{:S(2)}, u32[]{:S(2)}) %all-to-all-start) | async-done | bytes 524320 | tf_op jit(solution)/shard_map/all_to_all | solution.py:109
  86.1 2.2 broadcast_in_dim.124
  88.4 4.7 %all-to-all-start.1 = ((bf16[8,1024,256]{2,1,0:T(8,128)(2,1)}), bf16[8,1024,256]{2,1,0:T(8,128)(2,1)}, u32[]{:S(2)}, u32[]{:S(2)}) async-start(bf16[8,1024,256]{2,1,0:T(8,128)(2,1)} %broadcast_in_dim.124), calls=%async_computation.1 | async-start | bytes 8388608 | tf_op jit(solution)/shard_map/all_to_all | solution.py:124
  97.0 1.8 multiply_cosine_fusion.1
  98.8 44.0 %all-to-all-done.1 = bf16[8,1024,256]{2,1,0:T(8,128)(2,1)} async-done(((bf16[8,1024,256]{2,1,0:T(8,128)(2,1)}), bf16[8,1024,256]{2,1,0:T(8,128)(2,1)}, u32[]{:S(2)}, u32[]{:S(2)}) %all-to-all-start.1) | async-done | bytes 4194336 | tf_op jit(solution)/shard_map/all_to_all | solution.py:124
  142.7 3.1 fusion.21
  145.8 5.2 %fusion.23 = bf16[8,1024,256]{2,1,0:T(8,128)(2,1)} fusion(bf16[8,1024,256]{2,1,0:T(8,128)(2,1)} %all-to-all-done.1, f32[8,256]{1,0:T(8,128)S(1)} %reshape.601, f32[1024]{0:T(1024)S(1)} %add_rsqrt_fusion.2), kind=kLoop, calls=%fused_computation.37 | loop fusion | flops 8388608 | bytes 8400896 | tf_op jit(solution)/shard_map/convert_element_type | solution.py:144
  153.3 3.3 %all-to-all-start.2 = ((bf16[8,16,256]{2,1,0:T(8,128)(2,1)}), bf16[8,16,256]{2,1,0:T(8,128)(2,1)S(1)}, u32[]{:S(2)}, u32[]{:S(2)}) async-start(bf16[8,16,256]{2,1,0:T(8,128)(2,1)} %broadcast_in_dim.126), calls=%async_computation.2 | async-start | bytes 131072 | tf_op jit(solution)/shard_map/all_to_all | solution.py:129
  156.9 4.3 %convolution_bitcast_fusion.1 = bf16[1024,1,128]{2,0,1:T(8,128)(2,1)} fusion(bf16[8,1024,256]{2,1,0:T(8,128)(2,1)} %fusion.23, bf16[8,256,128]{2,1,0:T(8,128)(2,1)S(1)} %bitcast.156), kind=kOutput, calls=%fused_computation.40 | convolution fusion | flops 536870912 | bytes 4980736 | tf_op jit(solution)/shard_map/fnk,fkc->nc/dot_general | solution.py:147
  168.0 1.9 fusion.31
  170.8 1.8 convolution_bitcast_fusion.3
  178.4 11.5 %while.12 = (s32[]{:T(128)}, bf16[2,512,1,2,128]{4,3,1,0,2:T(2,128)(2,1)S(1)}, s32[2,512]{1,0:T(2,128)S(1)}, s32[2,512]{1,0:T(2,128)S(1)}, bf16[2,512,1,2,128]{4...) while((s32[]{:T(128)}, ...), condition=%wide.region_18.19_spmd.clone.clone, body=%wide.region_15.18_spmd.clone.clone.sunk | while | flops 551155712 | bytes 17334396 | solution.py:177
  179.0 2.0 fusion.75
  184.8 2.0 fusion.75
  192.6 1.6 gather_fusion.4
  194.2 5.7 %all-to-all-start.4 = ((bf16[64,32,1,256]{3,1,2,0:T(8,128)(2,1)}), bf16[64,32,1,256]{3,1,2,0:T(8,128)(2,1)S(1)}, u32[]{:S(2)}, u32[]{:S(2)}) async-start(bf16[64,32,1,256]{3,1,2,0:T(8,128)(2,1)} %bitcast.33), calls=%async_computation.4 | async-start | bytes 2097152 | tf_op jit(solution)/shard_map/all_to_all | solution.py:199
  199.9 25.8 %all-gather.5.cloned.1.call-done = bf16[1024,2048]{1,0:T(8,128)(2,1)} async-done(((bf16[1024,256]{1,0:T(8,128)(2,1)}), bf16[1024,2048]{1,0:T(8,128)(2,1)}) %all-gather.5.cloned.1.call-update) | async-done | bytes 4194320 | tf_op jit(solution)/shard_map/all_gather | solution.py:186
  225.6 3.7 %convolution_convert_fusion = bf16[1024,256]{1,0:T(8,128)(2,1)S(1)} fusion(bf16[1024,2048]{1,0:T(8,128)(2,1)} %all-gather.5.cloned.1.call-done, bf16[2048,896]{1,0:T(8,128)(2,1)} %all-gather.3.cloned.1.call-done), kind=kOutput, calls=%fused_computation.39 | convolution fusion | flops 1074003968 | bytes 5767168 | tf_op jit(solution)/shard_map/dot_general | solution.py:187
  229.4 1.6 gather_fusion.2
  231.0 24.4 %all-to-all-done.4 = bf16[64,32,1,256]{3,1,2,0:T(8,128)(2,1)S(1)} async-done(((bf16[64,32,1,256]{3,1,2,0:T(8,128)(2,1)}), bf16[64,32,1,256]{3,1,2,0:T(8,128)(2,1)S(1)}, u32[]{:S(2)}, u32[]{:S(2)}) %all-to-all-start.4) | async-done | bytes 1048608 | tf_op jit(solution)/shard_map/all_to_all | solution.py:199
  255.4 5.9 %all-to-all-start.3 = ((bf16[64,32,256]{2,1,0:T(8,128)(2,1)}), bf16[64,32,256]{2,1,0:T(8,128)(2,1)S(1)}, u32[]{:S(2)}, u32[]{:S(2)}) async-start(bf16[64,32,256]{2,1,0:T(8,128)(2,1)} %bitcast.26), calls=%async_computation.3 | async-start | bytes 2097152 | tf_op jit(solution)/shard_map/all_to_all | solution.py:199
  262.7 53.2 %all-to-all-done.3 = bf16[64,32,256]{2,1,0:T(8,128)(2,1)S(1)} async-done(((bf16[64,32,256]{2,1,0:T(8,128)(2,1)}), bf16[64,32,256]{2,1,0:T(8,128)(2,1)S(1)}, u32[]{:S(2)}, u32[]{:S(2)}) %all-to-all-start.3) | async-done | bytes 1048608 | tf_op jit(solution)/shard_map/all_to_all | solution.py:199
  (129 shorter events, 41.5 us)
Async XLA Ops:
  7.2 5.4 %copy-start = (bf16[1024,256]{1,0:T(8,128)(2,1)S(1)}, bf16[1024,256]{1,0:T(8,128)(2,1)}, u32[]{:S(2)}) copy-start(bf16[1024,256]{1,0:T(8,128)(2,1)} %param.12) | copy-start | bytes 1572868
  7.2 143.8 %all-gather.3.cloned.1.call-start = ((), (), s32[]{:S(2)}) async-start(), calls=%async_computation.5 | async-start | bytes 3899392 | tf_op jit(solution)/shard_map/all_gather | solution.py:104
  8.1 25.6 %copy-start.6 = (s32[64]{0:T(128)}, s32[64]{0:T(128)S(1)}, u32[]{:S(2)}) copy-start(s32[64]{0:T(128)S(1)} %convert_reduce_fusion) | copy-start | bytes 772
  33.8 51.8 %all-to-all-start = ((bf16[64,16,256]{2,1,0:T(8,128)(2,1)}), bf16[64,16,256]{2,1,0:T(8,128)(2,1)S(1)}, u32[]{:S(2)}, u32[]{:S(2)}) async-start(bf16[64,16,256]{2,1,0:T(8,128)(2,1)} %gather_fusion), calls=%async_computation | async-start | bytes 1048576 | tf_op jit(solution)/shard_map/all_to_all | solution.py:109
  88.4 5.9 %copy-start.10 = (bf16[2048]{0:T(1024)(128)(2,1)S(1)}, bf16[2048]{0:T(1024)(128)(2,1)}, u32[]{:S(2)}) copy-start(bf16[2048]{0:T(1024)(128)(2,1)} %param.13) | copy-start | bytes 12292
  88.4 6.5 %copy-start.15 = (bf16[128]{0:T(256)(128)(2,1)S(1)}, bf16[128]{0:T(256)(128)(2,1)}, u32[]{:S(2)}) copy-start(bf16[128]{0:T(256)(128)(2,1)} %param.15) | copy-start | bytes 772
  88.4 7.1 %copy-start.11 = (s32[64,8]{0,1:T(8,128)S(1)}, s32[64,8]{0,1:T(8,128)}, u32[]{:S(2)}) copy-start(s32[64,8]{0,1:T(8,128)} %param.20) | copy-start | bytes 6148
  88.4 7.4 %copy-start.16 = (bf16[128]{0:T(256)(128)(2,1)S(1)}, bf16[128]{0:T(256)(128)(2,1)}, u32[]{:S(2)}) copy-start(bf16[128]{0:T(256)(128)(2,1)} %param.14) | copy-start | bytes 772
  88.4 54.3 %all-to-all-start.1 = ((bf16[8,1024,256]{2,1,0:T(8,128)(2,1)}), bf16[8,1024,256]{2,1,0:T(8,128)(2,1)}, u32[]{:S(2)}, u32[]{:S(2)}) async-start(bf16[8,1024,256]{2,1,0:T(8,128)(2,1)} %broadcast_in_dim.124), calls=%async_computation.1 | async-start | bytes 8388608 | tf_op jit(solution)/shard_map/all_to_all | solution.py:124
  97.0 1.8 copy-start.14
  97.0 54.0 %copy-start.5 = (f32[1024]{0:T(1024)}, f32[1024]{0:T(1024)S(1)}, u32[]{:S(2)}) copy-start(f32[1024]{0:T(1024)S(1)} %subtract_convert_fusion.1) | copy-start | bytes 12292
  153.3 12.0 %all-to-all-start.2 = ((bf16[8,16,256]{2,1,0:T(8,128)(2,1)}), bf16[8,16,256]{2,1,0:T(8,128)(2,1)S(1)}, u32[]{:S(2)}, u32[]{:S(2)}) async-start(bf16[8,16,256]{2,1,0:T(8,128)(2,1)} %broadcast_in_dim.126), calls=%async_computation.2 | async-start | bytes 131072 | tf_op jit(solution)/shard_map/all_to_all | solution.py:129
  156.7 68.9 %all-gather.5.cloned.1.call-start = ((), (), s32[]{:S(2)}) async-start(), calls=%async_computation.6 | async-start | bytes 4718592 | tf_op jit(solution)/shard_map/all_gather | solution.py:186
  156.9 5.6 %copy-start.1 = (bf16[8,1024,256]{2,1,0:T(8,128)(2,1)S(1)}, bf16[8,1024,256]{2,1,0:T(8,128)(2,1)}, u32[]{:S(2)}) copy-start(bf16[8,1024,256]{2,1,0:T(8,128)(2,1)} %fusion.23) | copy-start | bytes 12582916
  162.5 1.3 copy-start.2
  173.9 3.6 %copy-start.9 = (f32[16]{0:T(128)S(1)}, f32[16]{0:T(128)}, u32[]{:S(2)}) copy-start(f32[16]{0:T(128)} %copy-done.8) | copy-start | bytes 196
  174.0 4.3 %copy-start.3 = (bf16[2,512,1,2,128]{4,3,1,0,2:T(2,128)(2,1)S(1)}, bf16[2,512,1,2,128]{4,3,1,0,2:T(2,128)(2,1)}, u32[]{:S(2)}) copy-start(bf16[2,512,1,2,128]{4,3,1,0,2:T(2,128)(2,1)} %custom-call.13) | copy-start | bytes 1572868
  178.4 12.4 %copy-start.7 = (s32[64]{0:T(128)S(1)}, s32[64]{0:T(128)}, u32[]{:S(2)}) copy-start(s32[64]{0:T(128)} %copy-done.6) | copy-start | bytes 772
  178.4 12.4 %copy-start.13 = (s32[64]{0:T(128)S(1)}, s32[64]{0:T(128)}, u32[]{:S(2)}) copy-start(s32[64]{0:T(128)} %get-tuple-element.137) | copy-start | bytes 772
  179.0 3.2 copy-start.4
  184.7 3.2 copy-start.4
  194.2 61.2 %all-to-all-start.4 = ((bf16[64,32,1,256]{3,1,2,0:T(8,128)(2,1)}), bf16[64,32,1,256]{3,1,2,0:T(8,128)(2,1)S(1)}, u32[]{:S(2)}, u32[]{:S(2)}) async-start(bf16[64,32,1,256]{3,1,2,0:T(8,128)(2,1)} %bitcast.33), calls=%async_computation.4 | async-start | bytes 2097152 | tf_op jit(solution)/shard_map/all_to_all | solution.py:199
  199.8 61.5 %copy-start.12 = (s32[64]{0:T(128)S(1)}, s32[64]{0:T(128)}, u32[]{:S(2)}) copy-start(s32[64]{0:T(128)} %get-tuple-element.116) | copy-start | bytes 772
  255.4 60.5 %all-to-all-start.3 = ((bf16[64,32,256]{2,1,0:T(8,128)(2,1)}), bf16[64,32,256]{2,1,0:T(8,128)(2,1)S(1)}, u32[]{:S(2)}, u32[]{:S(2)}) async-start(bf16[64,32,256]{2,1,0:T(8,128)(2,1)} %bitcast.26), calls=%async_computation.3 | async-start | bytes 2097152 | tf_op jit(solution)/shard_map/all_to_all | solution.py:199
  (1 other events, 0.6 us)
Sparse Core Ops, SparseCore 0:
  30.8 95.0 all-gather.2
  190.9 34.6 all-gather.4

commit v8 on v6

--- a/solution.py
+++ b/solution.py
@@ -127,6 +127,22 @@
     dup_mine = lax.dynamic_index_in_dim(dup_all, dup_source, 0, keepdims=False)
     dup_pieces = lax.all_gather(dup_mine, "fsdp", axis=0, tiled=False)
     pieces = lax.dynamic_update_slice_in_dim(pieces, dup_pieces, dup_target * arrival_rows, 1)
+    sub_ids = jnp.arange(2, dtype=jnp.int32)
+    block_back = jnp.where(
+        sub_ids[None, :] < counts[:, None], offsets[:, None] + sub_ids[None, :], 0
+    ).reshape(-1)
+    block_mine = own_blocks * 2 + dup_rank
+
+    def send_back(blocks):
+        rows = blocks.shape[1]
+        tail = blocks.shape[2:]
+        sent = jnp.take(blocks, block_back, axis=0, mode="clip").reshape(
+            (groups, 2 * rows) + tail
+        )
+        back = lax.all_to_all(sent, DP, split_axis=0, concat_axis=0, tiled=True)
+        return jnp.take(
+            back.reshape((groups * 2, rows) + tail), block_mine, axis=0, mode="clip"
+        )
     cuts = [w_query.shape[1], w_key.shape[1], w_value.shape[1], w_out.shape[1]]
     bounds = [sum(cuts[:k]) for k in range(5)]
     query_full, key_full, value_full, out_full = (
@@ -174,26 +190,19 @@
             starts.reshape(block_count, block_len),
         ),
     )
-    mixed = mixed.reshape(group_rows, kv_heads * group_ratio * HD)
-    heads_all = lax.all_gather(mixed, "fsdp", axis=1, tiled=True)
-    update = jnp.dot(heads_all, out_full, preferred_element_type=jnp.float32).astype(jnp.bfloat16)
-    sub_ids = jnp.arange(2, dtype=jnp.int32)
-    block_back = jnp.where(
-        sub_ids[None, :] < counts[:, None], offsets[:, None] + sub_ids[None, :], 0
-    ).reshape(-1)
-    block_mine = own_blocks * 2 + dup_rank
-
-    def send_back(rows):
-        tail = rows.shape[1:]
-        sent = jnp.take(
-            rows.reshape((groups, arrival_rows) + tail), block_back, axis=0, mode="clip"
-        ).reshape((groups, 2 * arrival_rows) + tail)
-        back = lax.all_to_all(sent, DP, split_axis=0, concat_axis=0, tiled=True)
-        return jnp.take(
-            back.reshape((groups * 2, arrival_rows) + tail), block_mine, axis=0, mode="clip"
-        ).reshape(rows.shape)
-    cache_out = send_back(cache_rows)
-    attention_out = send_back(update)
+    half_rows = arrival_rows // 2
+    mixed = mixed.reshape(groups, 2, half_rows, kv_heads * group_ratio * HD)
+    update_halves = []
+    for half in range(2):
+        heads_half = lax.all_gather(
+            mixed[:, half].reshape(groups * half_rows, -1), "fsdp", axis=1, tiled=True
+        )
+        update_half = jnp.dot(
+            heads_half, out_full, preferred_element_type=jnp.float32
+        ).astype(jnp.bfloat16)
+        update_halves.append(send_back(update_half.reshape(groups, half_rows, -1)))
+    attention_out = jnp.stack(update_halves, axis=1).reshape(group_rows, -1)
+    cache_out = send_back(cache_rows.reshape((groups, arrival_rows) + cache_rows.shape[1:])).reshape(cache_rows.shape)
     return (attention_out, cache_out)
 
 

time: 312 us -> 328 us (1.051)
  starting transfers between devices: 32.6 us -> 38.6 us
  waiting for transfers between devices: 166 us -> 172 us
    all_to_all x2 -> x3, waiting for transfers between devices: 78.3 us -> 93.1 us  [send_back(): back = lax.all_to_all(sent, DP, split_axis=0, concat_axis=0, tiled=True)]
    all_gather x1 -> x2, waiting for transfers between devices: 25.5 us -> 16.1 us  [local(): lax.all_gather(mixed[:, half].reshape(groups * half_rows, -1), 'fsdp', ax...]
    all_to_all x2 -> x3, starting transfers between devices: 11.8 us -> 17.7 us  [send_back(): back = lax.all_to_all(sent, DP, split_axis=0, concat_axis=0, tiled=True)]
    gather x4 -> x6, local copies, waits for them, and re-layouts: 6.03 us -> 7.07 us  [the longest x3 4.49 us: send_back(): jnp.take(blocks, block_back, axis=0, mode='clip')]
  transfers between devices with their start and end apart: 6 -> 8, of which waited for: 5 -> 6; matrix products, arithmetic and copies ran while one was open for 6% -> 7% of each run, Pallas kernels for 0% -> 0%
where the time goes in v8:
time: 328 us; the launch traced here: 327 us
  waiting for transfers between devices  172 us (52%)
  starting transfers between devices  38.6 us (12%)
  blocking collectives  35.7 us (11%)
  local copies, waits for them, and re-layouts  25.1 us (8%)
  matrix products  22.1 us (7%)
  between operations  18.9 us (6%)
  other arithmetic  14.2 us (4%)
    all_to_all x3, waiting for transfers between devices, send_back(): back = lax.all_to_all(sent, DP, split_axis=0, concat_axis=0, tiled=True)  93.1 us
    all_to_all x1, waiting for transfers between devices, local(): lax.all_to_all(outgoing, DP, split_axis=0, concat_axis=0, tiled=True)  33.7 us
    all_gather x1, waiting for transfers between devices, local(): packed = lax.all_gather(packed, 'z', axis=0, tiled=True)  28.2 us
    all_gather x1, blocking collectives, local(): dup_pieces = lax.all_gather(dup_mine, 'fsdp', axis=0, tiled=False)  20.5 us
    all_to_all x3, starting transfers between devices, send_back(): back = lax.all_to_all(sent, DP, split_axis=0, concat_axis=0, tiled=True)  17.7 us
    all_gather x2, waiting for transfers between devices, local(): lax.all_gather(mixed[:, half].reshape(groups * half_rows, -1), 'fsdp', ax...  16.1 us
    all_to_all x1, starting transfers between devices, local(): lax.all_to_all(outgoing, DP, split_axis=0, concat_axis=0, tiled=True)  16.1 us
    all_gather x1, blocking collectives, local(): packed = lax.all_gather(packed, 'y', axis=0, tiled=True)  15.3 us
  transfers between devices with their start and end apart: 8, of which 6 were waited for; matrix products, arithmetic and copies ran while one was open for 7% of the time, Pallas kernels for 0%

profile of v8, /device:TPU:24, one launch (start us, length us, event | category | flops | bytes accessed | tf_op | source)
XLA Modules:
  0.0 326.6 jit_solution(3392471408532539455)
XLA Ops:
  14.9 15.3 %all_gather.16 = bf16[128,896]{1,0:T(8,128)(2,1)} all-gather(bf16[32,896]{1,0:T(8,128)(2,1)S(1)} %constant_dynamic-update-slice_fusion), channel_id=1, replica_groups=mesh['z'=16,'y'=4,'fsdp'=8] {'y'}, dimensions={0}, use_global_device_ids=true | all-gather | bytes 286720 | tf_op jit(solution)/shard_map/all_gather | solution.py:102
  32.7 16.1 %all-to-all-start = ((bf16[64,16,256]{2,1,0:T(8,128)(2,1)}), bf16[64,16,256]{2,1,0:T(8,128)(2,1)S(1)}, u32[]{:S(2)}, u32[]{:S(2)}) async-start(bf16[64,16,256]{2,1,0:T(8,128)(2,1)} %gather_fusion), calls=%async_computation | async-start | bytes 1048576 | tf_op jit(solution)/shard_map/all_to_all | solution.py:109
  50.4 33.7 %all-to-all-done = bf16[64,16,256]{2,1,0:T(8,128)(2,1)S(1)} async-done(((bf16[64,16,256]{2,1,0:T(8,128)(2,1)}), bf16[64,16,256]{2,1,0:T(8,128)(2,1)S(1)}, u32[]{:S(2)}, u32[]{:S(2)}) %all-to-all-start) | async-done | bytes 524320 | tf_op jit(solution)/shard_map/all_to_all | solution.py:109
  84.7 2.2 broadcast_in_dim.117
  87.0 4.7 %all-to-all-start.1 = ((bf16[8,1024,256]{2,1,0:T(8,128)(2,1)}), bf16[8,1024,256]{2,1,0:T(8,128)(2,1)}, u32[]{:S(2)}, u32[]{:S(2)}) async-start(bf16[8,1024,256]{2,1,0:T(8,128)(2,1)} %broadcast_in_dim.117), calls=%async_computation.1 | async-start | bytes 8388608 | tf_op jit(solution)/shard_map/all_to_all | solution.py:124
  94.9 1.8 multiply_cosine_fusion.1
  96.7 28.2 %all-gather.4.cloned.1.call-done = bf16[2048,896]{1,0:T(8,128)(2,1)} async-done(((bf16[128,896]{1,0:T(8,128)(2,1)}), bf16[2048,896]{1,0:T(8,128)(2,1)}) %all-gather.4.cloned.1.call-update) | async-done | bytes 3670032 | tf_op jit(solution)/shard_map/all_gather | solution.py:104
  126.7 20.5 %all_gather.18 = bf16[8,16,256]{2,1,0:T(8,128)(2,1)S(1)} all-gather(bf16[1,16,256]{2,1,0:T(8,128)(2,1)S(1)} %constant_dynamic-slice_fusion.2), channel_id=1, replica_groups=mesh['z'=16,'y'=4,'fsdp'=8] {'fsdp'}, dimensions={0}, use_global_device_ids=true | all-gather | bytes 73728 | tf_op jit(solution)/shard_map/all_gather | solution.py:128
  147.7 3.1 fusion.21
  150.8 4.2 %fusion.29 = bf16[1024,128]{1,0:T(8,128)(2,1)} fusion(bf16[8,256,128]{2,1,0:T(8,128)(2,1)S(1)} %bitcast.161, bf16[8,1024,256]{2,1,0:T(8,128)(2,1)} %constant_dynamic-update-slice_fusion.5, f32[8,256]{1,0:T(8,128)S(1)} %reshape.588, f32[1024]{0:T(1024)S(1)} %add_rsqrt_fusion.2), kind=kOutput, calls=%fused_computation.45 | convolution fusion | flops 545390592 | bytes 4993024 | tf_op jit(solution)/shard_map/fnk,fkc->nc/dot_general | solution.py:162
  155.0 3.7 %multiply_reduce_fusion.1 = (f32[1024]{0:T(1024)S(1)}, f32[1024,128]{0,1:T(8,128)S(1)}) fusion(bf16[8,256,128]{2,1,0:T(8,128)(2,1)S(1)} %bitcast.160, bf16[8,1024,256]{2,1,0:T(8,128)(2,1)} %constant_dynamic-update-slice_fusion.5, f32[8,256]{1,0:T(8,128)S(1)} %reshape.588, f32[1024]{0:T(1024)S(1)} %add_rsqrt_fusion.2), kind=kOutput, calls=%fused_computation.59 | convolution fusion | flops 545520640 | bytes 5259264 | tf_op jit(solution)/shard_map/fnk,fkc->nc/dot_general | solution.py:162
  162.1 3.8 %multiply_reduce_fusion = (f32[1024,2]{0,1:T(2,128)S(1)}, f32[1024,2,128]{0,2,1:T(8,128)S(1)}) fusion(bf16[2,128,8,256]{3,2,1,0:T(8,128)(2,1)S(1)} %bitcast.155, f32[8,256]{1,0:T(8,128)S(1)} %reshape.588, f32[1024]{0:T(1024)S(1)} %add_rsqrt_fusion.2, bf16[8,1024,256]{2,1,0:T(8,128)(2,1)} %constant_dynamic-update-slice_fusion.5), kind=kOutput, calls=%fused_computation.52 | convolution fusion | flops 1082652672 | bytes 6311936 | tf_op jit(solution)/shard_map/fnk,fkc->nc/dot_general | solution.py:162
  167.7 9.4 %while.12 = (s32[]{:T(128)}, bf16[2,512,1,2,128]{4,3,1,0,2:T(2,128)(2,1)S(1)}, s32[2,512]{1,0:T(2,128)S(1)}, s32[2,512]{1,0:T(2,128)S(1)}, bf16[2,512,1,2,128]{4...) while((s32[]{:T(128)}, ...), condition=%wide.region_17.18_spmd.clone.clone, body=%wide.region_14.17_spmd.clone.clone.sunk | while | flops 551155712 | bytes 16285793 | solution.py:185
  175.3 1.6 fusion.77
  179.2 1.6 gather_fusion.6
  180.8 5.8 %all-to-all-start.4 = ((bf16[64,32,1,256]{3,1,2,0:T(8,128)(2,1)}), bf16[64,32,1,256]{3,1,2,0:T(8,128)(2,1)S(1)}, u32[]{:S(2)}, u32[]{:S(2)}) async-start(bf16[64,32,1,256]{3,1,2,0:T(8,128)(2,1)} %bitcast.38), calls=%async_computation.4 | async-start | bytes 2097152 | tf_op jit(solution)/shard_map/all_to_all | solution.py:142
  187.4 16.1 %all-gather.6.cloned.1.call-done = bf16[512,2048]{1,0:T(8,128)(2,1)} async-done(((bf16[512,256]{1,0:T(8,128)(2,1)}), bf16[512,2048]{1,0:T(8,128)(2,1)}) %all-gather.6.cloned.1.call-update) | async-done | bytes 2097168 | tf_op jit(solution)/shard_map/all_gather | solution.py:197
  203.5 2.7 fusion.30
  207.6 34.8 %all-to-all-done.4 = bf16[64,32,1,256]{3,1,2,0:T(8,128)(2,1)S(1)} async-done(((bf16[64,32,1,256]{3,1,2,0:T(8,128)(2,1)}), bf16[64,32,1,256]{3,1,2,0:T(8,128)(2,1)S(1)}, u32[]{:S(2)}, u32[]{:S(2)}) %all-to-all-start.4) | async-done | bytes 1048608 | tf_op jit(solution)/shard_map/all_to_all | solution.py:142
  242.4 5.9 %all-to-all-start.2 = ((bf16[64,16,256]{2,1,0:T(8,128)(2,1)}), bf16[64,16,256]{2,1,0:T(8,128)(2,1)S(1)}, u32[]{:S(2)}, u32[]{:S(2)}) async-start(bf16[64,16,256]{2,1,0:T(8,128)(2,1)} %bitcast.25), calls=%async_computation.2 | async-start | bytes 1048576 | tf_op jit(solution)/shard_map/all_to_all | solution.py:142
  248.3 2.6 fusion.31
  252.3 28.3 %all-to-all-done.2 = bf16[64,16,256]{2,1,0:T(8,128)(2,1)S(1)} async-done(((bf16[64,16,256]{2,1,0:T(8,128)(2,1)}), bf16[64,16,256]{2,1,0:T(8,128)(2,1)S(1)}, u32[]{:S(2)}, u32[]{:S(2)}) %all-to-all-start.2) | async-done | bytes 524320 | tf_op jit(solution)/shard_map/all_to_all | solution.py:142
  280.7 5.9 %all-to-all-start.3 = ((bf16[64,16,256]{2,1,0:T(8,128)(2,1)}), bf16[64,16,256]{2,1,0:T(8,128)(2,1)S(1)}, u32[]{:S(2)}, u32[]{:S(2)}) async-start(bf16[64,16,256]{2,1,0:T(8,128)(2,1)} %bitcast.30), calls=%async_computation.3 | async-start | bytes 1048576 | tf_op jit(solution)/shard_map/all_to_all | solution.py:142
  288.6 30.0 %all-to-all-done.3 = bf16[64,16,256]{2,1,0:T(8,128)(2,1)S(1)} async-done(((bf16[64,16,256]{2,1,0:T(8,128)(2,1)}), bf16[64,16,256]{2,1,0:T(8,128)(2,1)S(1)}, u32[]{:S(2)}, u32[]{:S(2)}) %all-to-all-start.3) | async-done | bytes 524320 | tf_op jit(solution)/shard_map/all_to_all | solution.py:142
  (115 shorter events, 35.1 us)
Async XLA Ops:
  7.2 4.9 %copy-start = (bf16[1024,256]{1,0:T(8,128)(2,1)S(1)}, bf16[1024,256]{1,0:T(8,128)(2,1)}, u32[]{:S(2)}) copy-start(bf16[1024,256]{1,0:T(8,128)(2,1)} %param.12) | copy-start | bytes 1572868
  7.2 117.8 %all-gather.4.cloned.1.call-start = ((), (), s32[]{:S(2)}) async-start(), calls=%async_computation.5 | async-start | bytes 3899392 | tf_op jit(solution)/shard_map/all_gather | solution.py:104
  32.7 51.4 %all-to-all-start = ((bf16[64,16,256]{2,1,0:T(8,128)(2,1)}), bf16[64,16,256]{2,1,0:T(8,128)(2,1)S(1)}, u32[]{:S(2)}, u32[]{:S(2)}) async-start(bf16[64,16,256]{2,1,0:T(8,128)(2,1)} %gather_fusion), calls=%async_computation | async-start | bytes 1048576 | tf_op jit(solution)/shard_map/all_to_all | solution.py:109
  86.9 6.8 %copy-start.6 = (bf16[2048]{0:T(1024)(128)(2,1)S(1)}, bf16[2048]{0:T(1024)(128)(2,1)}, u32[]{:S(2)}) copy-start(bf16[2048]{0:T(1024)(128)(2,1)} %param.13) | copy-start | bytes 12292
  86.9 6.8 %copy-start.8 = (bf16[128]{0:T(256)(128)(2,1)S(1)}, bf16[128]{0:T(256)(128)(2,1)}, u32[]{:S(2)}) copy-start(bf16[128]{0:T(256)(128)(2,1)} %param.15) | copy-start | bytes 772
  86.9 6.8 %copy-start.7 = (s32[64,8]{0,1:T(8,128)S(1)}, s32[64,8]{0,1:T(8,128)}, u32[]{:S(2)}) copy-start(s32[64,8]{0,1:T(8,128)} %param.20) | copy-start | bytes 6148
  86.9 7.2 %copy-start.9 = (bf16[128]{0:T(256)(128)(2,1)S(1)}, bf16[128]{0:T(256)(128)(2,1)}, u32[]{:S(2)}) copy-start(bf16[128]{0:T(256)(128)(2,1)} %param.14) | copy-start | bytes 772
  87.0 60.2 %all-to-all-start.1 = ((bf16[8,1024,256]{2,1,0:T(8,128)(2,1)}), bf16[8,1024,256]{2,1,0:T(8,128)(2,1)}, u32[]{:S(2)}, u32[]{:S(2)}) async-start(bf16[8,1024,256]{2,1,0:T(8,128)(2,1)} %broadcast_in_dim.117), calls=%async_computation.1 | async-start | bytes 8388608 | tf_op jit(solution)/shard_map/all_to_all | solution.py:124
  91.6 111.8 %all-gather.6.cloned.1.call-start = ((), (), s32[]{:S(2)}) async-start(), calls=%async_computation.6 | async-start | bytes 2359296 | tf_op jit(solution)/shard_map/all_gather | solution.py:197
  158.8 2.3 slice-start
  162.1 4.1 %copy-start.1 = (f32[1024,64]{0,1:T(8,128)S(1)}, f32[1024,64]{0,1:T(8,128)}, u32[]{:S(2)}) copy-start(f32[1024,64]{0,1:T(8,128)} %get-tuple-element.153) | copy-start | bytes 786436
  162.1 4.1 %copy-start.2 = (f32[1024,64]{0,1:T(8,128)S(1)}, f32[1024,64]{0,1:T(8,128)}, u32[]{:S(2)}) copy-start(f32[1024,64]{0,1:T(8,128)} %get-tuple-element.154) | copy-start | bytes 786436
  166.0 1.7 copy-start.3
  166.0 1.7 copy-start.4
  166.0 1.7 copy-start.5
  180.8 61.5 %all-to-all-start.4 = ((bf16[64,32,1,256]{3,1,2,0:T(8,128)(2,1)}), bf16[64,32,1,256]{3,1,2,0:T(8,128)(2,1)S(1)}, u32[]{:S(2)}, u32[]{:S(2)}) async-start(bf16[64,32,1,256]{3,1,2,0:T(8,128)(2,1)} %bitcast.38), calls=%async_computation.4 | async-start | bytes 2097152 | tf_op jit(solution)/shard_map/all_to_all | solution.py:142
  186.7 61.7 %all-gather.8.cloned.1.call-start = ((), (), s32[]{:S(2)}) async-start(), calls=%async_computation.7 | async-start | bytes 2359296 | tf_op jit(solution)/shard_map/all_gather | solution.py:197
  242.4 38.3 %all-to-all-start.2 = ((bf16[64,16,256]{2,1,0:T(8,128)(2,1)}), bf16[64,16,256]{2,1,0:T(8,128)(2,1)S(1)}, u32[]{:S(2)}, u32[]{:S(2)}) async-start(bf16[64,16,256]{2,1,0:T(8,128)(2,1)} %bitcast.25), calls=%async_computation.2 | async-start | bytes 1048576 | tf_op jit(solution)/shard_map/all_to_all | solution.py:142
  280.7 37.9 %all-to-all-start.3 = ((bf16[64,16,256]{2,1,0:T(8,128)(2,1)}), bf16[64,16,256]{2,1,0:T(8,128)(2,1)S(1)}, u32[]{:S(2)}, u32[]{:S(2)}) async-start(bf16[64,16,256]{2,1,0:T(8,128)(2,1)} %bitcast.30), calls=%async_computation.3 | async-start | bytes 1048576 | tf_op jit(solution)/shard_map/all_to_all | solution.py:142
Sparse Core Ops, SparseCore 0:
  30.3 94.5 all-gather.3
  178.5 24.9 all-gather.5
  206.2 35.4 all-gather.7

commit v9 on v6

--- a/solution.py
+++ b/solution.py
@@ -176,6 +176,12 @@
     )
     mixed = mixed.reshape(group_rows, kv_heads * group_ratio * HD)
     heads_all = lax.all_gather(mixed, "fsdp", axis=1, tiled=True)
+    cache_blocks = cache_rows.reshape((groups, arrival_rows) + cache_rows.shape[1:])
+    dup_position = jnp.sum(jnp.where(counts == 2, offsets + 1, 0))
+    dup_cache = lax.dynamic_index_in_dim(cache_blocks, dup_position, 0, keepdims=True)
+    dup_cache, heads_all = lax.optimization_barrier((dup_cache, heads_all))
+    dup_cache = lax.all_gather(dup_cache, "y", axis=0, tiled=True)
+    dup_cache = lax.all_gather(dup_cache, "z", axis=0, tiled=True)
     update = jnp.dot(heads_all, out_full, preferred_element_type=jnp.float32).astype(jnp.bfloat16)
     sub_ids = jnp.arange(2, dtype=jnp.int32)
     block_back = jnp.where(
@@ -192,7 +198,14 @@
         return jnp.take(
             back.reshape((groups * 2, arrival_rows) + tail), block_mine, axis=0, mode="clip"
         ).reshape(rows.shape)
-    cache_out = send_back(cache_rows)
+    sent_cache = jnp.take(cache_blocks, offsets, axis=0, mode="clip")
+    back_cache = lax.all_to_all(sent_cache, DP, split_axis=0, concat_axis=0, tiled=True)
+    cache_out = jnp.take(
+        jnp.concatenate([back_cache, dup_cache], axis=0),
+        own_blocks + groups * dup_rank,
+        axis=0,
+        mode="clip",
+    ).reshape(cache_rows.shape)
     attention_out = send_back(update)
     return (attention_out, cache_out)
 

time: 312 us -> 319 us (1.022)
  waiting for transfers between devices: 166 us -> 87.7 us
  blocking collectives: 35.7 us -> 110 us
  starting transfers between devices: 32.6 us -> 40.5 us
    all_to_all x2 -> x1, waiting for transfers between devices: 78.3 us -> 0.01 us  [send_back(): back = lax.all_to_all(sent, DP, split_axis=0, concat_axis=0, tiled=True)]
    all_gather x0 -> x2, blocking collectives: none -> 73.8 us  [the longest x1 61.8 us: local(): dup_cache = lax.all_gather(dup_cache, 'z', axis=0, tiled=True)]
    all_to_all x0 -> x1, starting transfers between devices: none -> 5.78 us  [local(): lax.all_to_all(sent_cache, DP, split_axis=0, concat_axis=0, tiled=True)]
    all_to_all x2 -> x1, starting transfers between devices: 11.8 us -> 13.8 us  [send_back(): back = lax.all_to_all(sent, DP, split_axis=0, concat_axis=0, tiled=True)]
  transfers between devices with their start and end apart: 6 -> 6, of which waited for: 5 -> 4; matrix products, arithmetic and copies ran while one was open for 6% -> 6% of each run, Pallas kernels for 0% -> 0%
where the time goes in v9:
time: 319 us; the launch traced here: 318 us
  blocking collectives  110 us (34%)
  waiting for transfers between devices  87.7 us (27%)
  starting transfers between devices  40.5 us (13%)
  local copies, waits for them, and re-layouts  23.5 us (7%)
  matrix products  21.9 us (7%)
  between operations  20.7 us (6%)
  other arithmetic  13.7 us (4%)
    all_gather x1, blocking collectives, local(): dup_cache = lax.all_gather(dup_cache, 'z', axis=0, tiled=True)  61.8 us
    all_to_all x1, waiting for transfers between devices, local(): lax.all_to_all(outgoing, DP, split_axis=0, concat_axis=0, tiled=True)  33.7 us
    all_gather x1, waiting for transfers between devices, local(): packed = lax.all_gather(packed, 'z', axis=0, tiled=True)  28.3 us
    all_gather x1, waiting for transfers between devices, local(): heads_all = lax.all_gather(mixed, 'fsdp', axis=1, tiled=True)  23.8 us
    all_gather x1, blocking collectives, local(): dup_pieces = lax.all_gather(dup_mine, 'fsdp', axis=0, tiled=False)  20.6 us
    all_to_all x1, starting transfers between devices, local(): lax.all_to_all(outgoing, DP, split_axis=0, concat_axis=0, tiled=True)  16.1 us
    all_gather x1, blocking collectives, local(): packed = lax.all_gather(packed, 'y', axis=0, tiled=True)  15.3 us
    all_to_all x1, starting transfers between devices, send_back(): back = lax.all_to_all(sent, DP, split_axis=0, concat_axis=0, tiled=True)  13.8 us
  transfers between devices with their start and end apart: 6, of which 4 were waited for; matrix products, arithmetic and copies ran while one was open for 6% of the time, Pallas kernels for 0%

profile of v9, /device:TPU:24, one launch (start us, length us, event | category | flops | bytes accessed | tf_op | source)
XLA Modules:
  0.0 317.7 jit_solution(12630389097061141198)
XLA Ops:
  14.9 15.3 %all_gather.19 = bf16[128,896]{1,0:T(8,128)(2,1)} all-gather(bf16[32,896]{1,0:T(8,128)(2,1)S(1)} %constant_dynamic-update-slice_fusion), channel_id=1, replica_groups=mesh['z'=16,'y'=4,'fsdp'=8] {'y'}, dimensions={0}, use_global_device_ids=true | all-gather | bytes 286720 | tf_op jit(solution)/shard_map/all_gather | solution.py:102
  32.7 16.1 %all-to-all-start = ((bf16[64,16,256]{2,1,0:T(8,128)(2,1)}), bf16[64,16,256]{2,1,0:T(8,128)(2,1)S(1)}, u32[]{:S(2)}, u32[]{:S(2)}) async-start(bf16[64,16,256]{2,1,0:T(8,128)(2,1)} %gather_fusion), calls=%async_computation | async-start | bytes 1048576 | tf_op jit(solution)/shard_map/all_to_all | solution.py:109
  50.4 33.7 %all-to-all-done = bf16[64,16,256]{2,1,0:T(8,128)(2,1)S(1)} async-done(((bf16[64,16,256]{2,1,0:T(8,128)(2,1)}), bf16[64,16,256]{2,1,0:T(8,128)(2,1)S(1)}, u32[]{:S(2)}, u32[]{:S(2)}) %all-to-all-start) | async-done | bytes 524320 | tf_op jit(solution)/shard_map/all_to_all | solution.py:109
  84.7 2.2 broadcast_in_dim.114
  87.0 4.7 %all-to-all-start.1 = ((bf16[8,1024,256]{2,1,0:T(8,128)(2,1)}), bf16[8,1024,256]{2,1,0:T(8,128)(2,1)}, u32[]{:S(2)}, u32[]{:S(2)}) async-start(bf16[8,1024,256]{2,1,0:T(8,128)(2,1)} %broadcast_in_dim.114), calls=%async_computation.1 | async-start | bytes 8388608 | tf_op jit(solution)/shard_map/all_to_all | solution.py:124
  94.8 1.8 multiply_cosine_fusion
  96.6 28.3 %all-gather.3.cloned.1.call-done = bf16[2048,896]{1,0:T(8,128)(2,1)} async-done(((bf16[128,896]{1,0:T(8,128)(2,1)}), bf16[2048,896]{1,0:T(8,128)(2,1)}) %all-gather.3.cloned.1.call-update) | async-done | bytes 3670032 | tf_op jit(solution)/shard_map/all_gather | solution.py:104
  126.6 20.6 %all_gather.21 = bf16[8,16,256]{2,1,0:T(8,128)(2,1)S(1)} all-gather(bf16[1,16,256]{2,1,0:T(8,128)(2,1)S(1)} %constant_dynamic-slice_fusion.4), channel_id=1, replica_groups=mesh['z'=16,'y'=4,'fsdp'=8] {'fsdp'}, dimensions={0}, use_global_device_ids=true | all-gather | bytes 73728 | tf_op jit(solution)/shard_map/all_gather | solution.py:128
  147.8 3.1 fusion.21
  150.9 3.7 %multiply_reduce_fusion.1 = (f32[1024]{0:T(1024)S(1)}, f32[1024,128]{0,1:T(8,128)S(1)}) fusion(bf16[8,256,128]{2,1,0:T(8,128)(2,1)S(1)} %bitcast.164, bf16[8,1024,256]{2,1,0:T(8,128)(2,1)} %constant_dynamic-update-slice_fusion.5, f32[8,256]{1,0:T(8,128)S(1)} %reshape.589, f32[1024]{0:T(1024)S(1)} %add_rsqrt_fusion.2), kind=kOutput, calls=%fused_computation.56 | convolution fusion | flops 545520640 | bytes 5259264 | tf_op jit(solution)/shard_map/fnk,fkc->nc/dot_general | solution.py:146
  156.1 3.6 %fusion.29 = bf16[1024,128]{1,0:T(8,128)(2,1)S(1)} fusion(bf16[8,256,128]{2,1,0:T(8,128)(2,1)S(1)} %bitcast.163, bf16[8,1024,256]{2,1,0:T(8,128)(2,1)} %constant_dynamic-update-slice_fusion.5, f32[8,256]{1,0:T(8,128)S(1)} %reshape.589, f32[1024]{0:T(1024)S(1)} %add_rsqrt_fusion.2), kind=kOutput, calls=%fused_computation.44 | convolution fusion | flops 545390592 | bytes 4993024 | tf_op jit(solution)/shard_map/fnk,fkc->nc/dot_general | solution.py:146
  161.6 3.8 %multiply_reduce_fusion = (f32[1024,2]{0,1:T(2,128)S(1)}, f32[1024,2,128]{0,2,1:T(8,128)S(1)}) fusion(bf16[2,128,8,256]{3,2,1,0:T(8,128)(2,1)S(1)} %bitcast.159, f32[8,256]{1,0:T(8,128)S(1)} %reshape.589, f32[1024]{0:T(1024)S(1)} %add_rsqrt_fusion.2, bf16[8,1024,256]{2,1,0:T(8,128)(2,1)} %constant_dynamic-update-slice_fusion.5), kind=kOutput, calls=%fused_computation.49 | convolution fusion | flops 1082652672 | bytes 6311936 | tf_op jit(solution)/shard_map/fnk,fkc->nc/dot_general | solution.py:146
  167.1 11.4 %while.12 = (s32[]{:T(128)}, bf16[2,512,1,2,128]{4,3,1,0,2:T(2,128)(2,1)S(1)}, s32[2,512]{1,0:T(2,128)S(1)}, s32[2,512]{1,0:T(2,128)S(1)}, bf16[2,512,1,2,128]{4...) while((s32[]{:T(128)}, ...), condition=%wide.region_17.18_spmd.clone.clone, body=%wide.region_14.17_spmd.clone.clone.sunk | while | flops 551155712 | bytes 16285793 | solution.py:169
  167.7 2.0 fusion.72
  173.4 2.0 fusion.72
  176.6 1.6 fusion.74
  181.4 5.8 %all-to-all-start.3 = ((bf16[64,16,1,256]{3,1,2,0:T(8,128)(2,1)}), bf16[64,16,1,256]{3,1,2,0:T(8,128)(2,1)S(1)}, u32[]{:S(2)}, u32[]{:S(2)}) async-start(bf16[64,16,1,256]{3,1,2,0:T(8,128)(2,1)} %bitcast.34), calls=%async_computation.3 | async-start | bytes 1048576 | tf_op jit(solution)/shard_map/all_to_all | solution.py:202
  189.4 23.8 %all-gather.5.cloned.1.call-done = bf16[1024,2048]{1,0:T(8,128)(2,1)} async-done(((bf16[1024,256]{1,0:T(8,128)(2,1)}), bf16[1024,2048]{1,0:T(8,128)(2,1)}) %all-gather.5.cloned.1.call-update) | async-done | bytes 4194320 | tf_op jit(solution)/shard_map/all_gather | solution.py:178
  213.2 3.7 %convolution_convert_fusion = bf16[1024,256]{1,0:T(8,128)(2,1)S(1)} fusion(bf16[1024,2048]{1,0:T(8,128)(2,1)} %all-gather.5.cloned.1.call-done, bf16[2048,896]{1,0:T(8,128)(2,1)} %all-gather.3.cloned.1.call-done), kind=kOutput, calls=%fused_computation.41 | convolution fusion | flops 1074003968 | bytes 5767168 | tf_op jit(solution)/shard_map/dot_general | solution.py:185
  216.9 1.6 gather_fusion.2
  218.5 1.8 all-to-all-done.3
  220.4 13.8 %all-to-all-start.2 = ((bf16[64,32,256]{2,1,0:T(8,128)(2,1)}), bf16[64,32,256]{2,1,0:T(8,128)(2,1)S(1)}, u32[]{:S(2)}, u32[]{:S(2)}) async-start(bf16[64,32,256]{2,1,0:T(8,128)(2,1)} %bitcast.30), calls=%async_computation.2 | async-start | bytes 2097152 | tf_op jit(solution)/shard_map/all_to_all | solution.py:197
  234.2 11.9 %all_gather.23 = bf16[4,16,1,256]{3,1,2,0:T(8,128)(2,1)S(1)} all-gather(bf16[1,16,1,256]{3,1,2,0:T(8,128)(2,1)S(1)} %constant_dynamic-slice_fusion.2), channel_id=1, replica_groups=mesh['z'=16,'y'=4,'fsdp'=8] {'y'}, dimensions={0}, use_global_device_ids=true | all-gather | bytes 40960 | tf_op jit(solution)/shard_map/all_gather | solution.py:183
  246.2 61.8 %all_gather.24 = bf16[64,16,1,256]{3,1,2,0:T(8,128)(2,1)S(1)} all-gather(bf16[4,16,1,256]{3,1,2,0:T(8,128)(2,1)S(1)} %all_gather.23), channel_id=1, replica_groups=mesh['z'=16,'y'=4,'fsdp'=8] {'z'}, dimensions={0}, use_global_device_ids=true | all-gather | bytes 557056 | tf_op jit(solution)/shard_map/all_gather | solution.py:184
  (106 shorter events, 30.2 us)
Async XLA Ops:
  7.2 4.8 %copy-start = (bf16[1024,256]{1,0:T(8,128)(2,1)S(1)}, bf16[1024,256]{1,0:T(8,128)(2,1)}, u32[]{:S(2)}) copy-start(bf16[1024,256]{1,0:T(8,128)(2,1)} %param.12) | copy-start | bytes 1572868
  7.2 117.7 %all-gather.3.cloned.1.call-start = ((), (), s32[]{:S(2)}) async-start(), calls=%async_computation.4 | async-start | bytes 3899392 | tf_op jit(solution)/shard_map/all_gather | solution.py:104
  32.7 51.4 %all-to-all-start = ((bf16[64,16,256]{2,1,0:T(8,128)(2,1)}), bf16[64,16,256]{2,1,0:T(8,128)(2,1)S(1)}, u32[]{:S(2)}, u32[]{:S(2)}) async-start(bf16[64,16,256]{2,1,0:T(8,128)(2,1)} %gather_fusion), calls=%async_computation | async-start | bytes 1048576 | tf_op jit(solution)/shard_map/all_to_all | solution.py:109
  87.0 6.6 %copy-start.3 = (bf16[2048]{0:T(1024)(128)(2,1)S(1)}, bf16[2048]{0:T(1024)(128)(2,1)}, u32[]{:S(2)}) copy-start(bf16[2048]{0:T(1024)(128)(2,1)} %param.13) | copy-start | bytes 12292
  87.0 6.7 %copy-start.5 = (bf16[128]{0:T(256)(128)(2,1)S(1)}, bf16[128]{0:T(256)(128)(2,1)}, u32[]{:S(2)}) copy-start(bf16[128]{0:T(256)(128)(2,1)} %param.15) | copy-start | bytes 772
  87.0 6.7 %copy-start.4 = (s32[64,8]{0,1:T(8,128)S(1)}, s32[64,8]{0,1:T(8,128)}, u32[]{:S(2)}) copy-start(s32[64,8]{0,1:T(8,128)} %param.20) | copy-start | bytes 6148
  87.0 7.0 %copy-start.6 = (bf16[128]{0:T(256)(128)(2,1)S(1)}, bf16[128]{0:T(256)(128)(2,1)}, u32[]{:S(2)}) copy-start(bf16[128]{0:T(256)(128)(2,1)} %param.14) | copy-start | bytes 772
  87.0 60.2 %all-to-all-start.1 = ((bf16[8,1024,256]{2,1,0:T(8,128)(2,1)}), bf16[8,1024,256]{2,1,0:T(8,128)(2,1)}, u32[]{:S(2)}, u32[]{:S(2)}) async-start(bf16[8,1024,256]{2,1,0:T(8,128)(2,1)} %broadcast_in_dim.114), calls=%async_computation.1 | async-start | bytes 8388608 | tf_op jit(solution)/shard_map/all_to_all | solution.py:124
  91.7 121.5 %all-gather.5.cloned.1.call-start = ((), (), s32[]{:S(2)}) async-start(), calls=%async_computation.5 | async-start | bytes 4718592 | tf_op jit(solution)/shard_map/all_gather | solution.py:178
  156.1 4.5 %slice-start = ((bf16[2048,896]{1,0:T(8,128)(2,1)}), bf16[2048,256]{1,0:T(8,128)(2,1)S(1)}, s32[]{:S(2)}) async-start(bf16[2048,896]{1,0:T(8,128)(2,1)} %all-gather.3.cloned.1.call-done), calls=%async_computation.6 | async-start | bytes 2097152 | tf_op jit(solution)/shard_map/slice | solution.py:133
  161.6 4.0 %copy-start.1 = (f32[1024,64]{0,1:T(8,128)S(1)}, f32[1024,64]{0,1:T(8,128)}, u32[]{:S(2)}) copy-start(f32[1024,64]{0,1:T(8,128)} %get-tuple-element.158) | copy-start | bytes 786436
  165.4 1.7 copy-start.2
  181.4 39.0 %all-to-all-start.3 = ((bf16[64,16,1,256]{3,1,2,0:T(8,128)(2,1)}), bf16[64,16,1,256]{3,1,2,0:T(8,128)(2,1)S(1)}, u32[]{:S(2)}, u32[]{:S(2)}) async-start(bf16[64,16,1,256]{3,1,2,0:T(8,128)(2,1)} %bitcast.34), calls=%async_computation.3 | async-start | bytes 1048576 | tf_op jit(solution)/shard_map/all_to_all | solution.py:202
  220.4 89.1 %all-to-all-start.2 = ((bf16[64,32,256]{2,1,0:T(8,128)(2,1)}), bf16[64,32,256]{2,1,0:T(8,128)(2,1)S(1)}, u32[]{:S(2)}, u32[]{:S(2)}) async-start(bf16[64,32,256]{2,1,0:T(8,128)(2,1)} %bitcast.30), calls=%async_computation.2 | async-start | bytes 2097152 | tf_op jit(solution)/shard_map/all_to_all | solution.py:197
Sparse Core Ops, SparseCore 0:
  30.3 94.5 all-gather.2
  179.5 33.6 all-gather.4

commit v10 on v6

--- a/solution.py
+++ b/solution.py
@@ -13,14 +13,6 @@
 
 epsilon = 1e-06
 rope_base = 1000000.0
-
-
-def for_sending(x):
-
-    def short(part):
-        return part.astype(jnp.bfloat16) if part.dtype == jnp.float32 else part
-
-    return jax.tree.map(short, x)
 
 
 def head_norm(inputs, gains):
@@ -69,7 +61,7 @@
     ).astype(jnp.bfloat16)
 
 
-def local(
+def local_body(
     tokens,
     norm_gain,
     query_gain,
@@ -192,6 +184,7 @@
         return jnp.take(
             back.reshape((groups * 2, arrival_rows) + tail), block_mine, axis=0, mode="clip"
         ).reshape(rows.shape)
+
     cache_out = send_back(cache_rows)
     attention_out = send_back(update)
     return (attention_out, cache_out)
@@ -201,7 +194,7 @@
     z_size = mesh.shape["dp"] // 4
     fine = Mesh(mesh.devices.reshape(z_size, 4, mesh.shape["fsdp"]), ("z", "y", "fsdp"))
     return jax.shard_map(
-        local,
+        local_body,
         mesh=fine,
         in_specs=(
             P(DP, "fsdp"),

time: 312 us -> 312 us (level)
  no operation moved by 1% of the time
where the time goes in v10:
time: 312 us; the launch traced here: 311 us
  waiting for transfers between devices  166 us (53%)
  blocking collectives  35.7 us (11%)
  starting transfers between devices  32.6 us (10%)
  local copies, waits for them, and re-layouts  23.7 us (8%)
  matrix products  20.7 us (7%)
  between operations  19.2 us (6%)
  other arithmetic  13.4 us (4%)
    all_to_all x2, waiting for transfers between devices, send_back(): back = lax.all_to_all(sent, DP, split_axis=0, concat_axis=0, tiled=True)  78.3 us
    all_to_all x1, waiting for transfers between devices, local_body(): lax.all_to_all(outgoing, DP, split_axis=0, concat_axis=0, tiled=True)  33.7 us
    all_gather x1, waiting for transfers between devices, local_body(): packed = lax.all_gather(packed, 'z', axis=0, tiled=True)  28.2 us
    all_gather x1, waiting for transfers between devices, local_body(): heads_all = lax.all_gather(mixed, 'fsdp', axis=1, tiled=True)  25.5 us
    all_gather x1, blocking collectives, local_body(): dup_pieces = lax.all_gather(dup_mine, 'fsdp', axis=0, tiled=False)  20.5 us
    all_to_all x1, starting transfers between devices, local_body(): lax.all_to_all(outgoing, DP, split_axis=0, concat_axis=0, tiled=True)  16.1 us
    all_gather x1, blocking collectives, local_body(): packed = lax.all_gather(packed, 'y', axis=0, tiled=True)  15.3 us
    all_to_all x2, starting transfers between devices, send_back(): back = lax.all_to_all(sent, DP, split_axis=0, concat_axis=0, tiled=True)  11.7 us
  transfers between devices with their start and end apart: 6, of which 5 were waited for; matrix products, arithmetic and copies ran while one was open for 6% of the time, Pallas kernels for 0%

profile of v10, /device:TPU:24, one launch (start us, length us, event | category | flops | bytes accessed | tf_op | source)
XLA Modules:
  0.0 311.1 jit_solution(3458453829169546722)
XLA Ops:
  14.9 15.3 %all_gather.13 = bf16[128,896]{1,0:T(8,128)(2,1)} all-gather(bf16[32,896]{1,0:T(8,128)(2,1)S(1)} %constant_dynamic-update-slice_fusion), channel_id=1, replica_groups=mesh['z'=16,'y'=4,'fsdp'=8] {'y'}, dimensions={0}, use_global_device_ids=true | all-gather | bytes 286720 | tf_op jit(solution)/shard_map/all_gather | solution.py:94
  32.7 16.1 %all-to-all-start = ((bf16[64,16,256]{2,1,0:T(8,128)(2,1)}), bf16[64,16,256]{2,1,0:T(8,128)(2,1)S(1)}, u32[]{:S(2)}, u32[]{:S(2)}) async-start(bf16[64,16,256]{2,1,0:T(8,128)(2,1)} %gather_fusion), calls=%async_computation | async-start | bytes 1048576 | tf_op jit(solution)/shard_map/all_to_all | solution.py:101
  50.4 33.7 %all-to-all-done = bf16[64,16,256]{2,1,0:T(8,128)(2,1)S(1)} async-done(((bf16[64,16,256]{2,1,0:T(8,128)(2,1)}), bf16[64,16,256]{2,1,0:T(8,128)(2,1)S(1)}, u32[]{:S(2)}, u32[]{:S(2)}) %all-to-all-start) | async-done | bytes 524320 | tf_op jit(solution)/shard_map/all_to_all | solution.py:101
  84.7 2.2 broadcast_in_dim.115
  87.0 4.7 %all-to-all-start.1 = ((bf16[8,1024,256]{2,1,0:T(8,128)(2,1)}), bf16[8,1024,256]{2,1,0:T(8,128)(2,1)}, u32[]{:S(2)}, u32[]{:S(2)}) async-start(bf16[8,1024,256]{2,1,0:T(8,128)(2,1)} %broadcast_in_dim.115), calls=%async_computation.1 | async-start | bytes 8388608 | tf_op jit(solution)/shard_map/all_to_all | solution.py:116
  94.9 1.8 multiply_cosine_fusion.1
  96.7 28.2 %all-gather.3.cloned.1.call-done = bf16[2048,896]{1,0:T(8,128)(2,1)} async-done(((bf16[128,896]{1,0:T(8,128)(2,1)}), bf16[2048,896]{1,0:T(8,128)(2,1)}) %all-gather.3.cloned.1.call-update) | async-done | bytes 3670032 | tf_op jit(solution)/shard_map/all_gather | solution.py:96
  125.0 1.5 fusion.58
  126.7 20.5 %all_gather.15 = bf16[8,16,256]{2,1,0:T(8,128)(2,1)S(1)} all-gather(bf16[1,16,256]{2,1,0:T(8,128)(2,1)S(1)} %constant_dynamic-slice_fusion.2), channel_id=1, replica_groups=mesh['z'=16,'y'=4,'fsdp'=8] {'fsdp'}, dimensions={0}, use_global_device_ids=true | all-gather | bytes 73728 | tf_op jit(solution)/shard_map/all_gather | solution.py:120
  147.8 3.1 fusion.21
  150.9 4.2 %fusion.29 = bf16[1024,128]{1,0:T(8,128)(2,1)} fusion(bf16[8,256,128]{2,1,0:T(8,128)(2,1)S(1)} %bitcast.153, bf16[8,1024,256]{2,1,0:T(8,128)(2,1)} %constant_dynamic-update-slice_fusion.5, f32[8,256]{1,0:T(8,128)S(1)} %reshape.576, f32[1024]{0:T(1024)S(1)} %add_rsqrt_fusion.2), kind=kOutput, calls=%fused_computation.44 | convolution fusion | flops 545390592 | bytes 4993024 | tf_op jit(solution)/shard_map/fnk,fkc->nc/dot_general | solution.py:138
  155.1 3.7 %multiply_reduce_fusion.1 = (f32[1024]{0:T(1024)S(1)}, f32[1024,128]{0,1:T(8,128)S(1)}) fusion(bf16[8,256,128]{2,1,0:T(8,128)(2,1)S(1)} %bitcast.152, bf16[8,1024,256]{2,1,0:T(8,128)(2,1)} %constant_dynamic-update-slice_fusion.5, f32[8,256]{1,0:T(8,128)S(1)} %reshape.576, f32[1024]{0:T(1024)S(1)} %add_rsqrt_fusion.2), kind=kOutput, calls=%fused_computation.53 | convolution fusion | flops 545520640 | bytes 5259264 | tf_op jit(solution)/shard_map/fnk,fkc->nc/dot_general | solution.py:138
  162.2 3.8 %multiply_reduce_fusion = (f32[1024,2]{0,1:T(2,128)S(1)}, f32[1024,2,128]{0,2,1:T(8,128)S(1)}) fusion(bf16[2,128,8,256]{3,2,1,0:T(8,128)(2,1)S(1)} %bitcast.148, f32[8,256]{1,0:T(8,128)S(1)} %reshape.576, f32[1024]{0:T(1024)S(1)} %add_rsqrt_fusion.2, bf16[8,1024,256]{2,1,0:T(8,128)(2,1)} %constant_dynamic-update-slice_fusion.5), kind=kOutput, calls=%fused_computation.48 | convolution fusion | flops 1082652672 | bytes 6311936 | tf_op jit(solution)/shard_map/fnk,fkc->nc/dot_general | solution.py:138
  167.7 9.4 %while.12 = (s32[]{:T(128)}, bf16[2,512,1,2,128]{4,3,1,0,2:T(2,128)(2,1)S(1)}, s32[2,512]{1,0:T(2,128)S(1)}, s32[2,512]{1,0:T(2,128)S(1)}, bf16[2,512,1,2,128]{4...) while((s32[]{:T(128)}, ...), condition=%wide.region_17.18_spmd.clone.clone, body=%wide.region_14.17_spmd.clone.clone.sunk | while | flops 551155712 | bytes 16285793 | solution.py:161
  170.6 1.6 fusion.73
  175.3 1.6 fusion.73
  178.9 1.6 gather_fusion.4
  180.6 5.8 %all-to-all-start.3 = ((bf16[64,32,1,256]{3,1,2,0:T(8,128)(2,1)}), bf16[64,32,1,256]{3,1,2,0:T(8,128)(2,1)S(1)}, u32[]{:S(2)}, u32[]{:S(2)}) async-start(bf16[64,32,1,256]{3,1,2,0:T(8,128)(2,1)} %bitcast.31), calls=%async_computation.3 | async-start | bytes 2097152 | tf_op jit(solution)/shard_map/all_to_all | solution.py:183
  186.4 25.5 %all-gather.5.cloned.1.call-done = bf16[1024,2048]{1,0:T(8,128)(2,1)} async-done(((bf16[1024,256]{1,0:T(8,128)(2,1)}), bf16[1024,2048]{1,0:T(8,128)(2,1)}) %all-gather.5.cloned.1.call-update) | async-done | bytes 4194320 | tf_op jit(solution)/shard_map/all_gather | solution.py:170
  211.9 3.7 %convolution_convert_fusion = bf16[1024,256]{1,0:T(8,128)(2,1)S(1)} fusion(bf16[1024,2048]{1,0:T(8,128)(2,1)} %all-gather.5.cloned.1.call-done, bf16[2048,896]{1,0:T(8,128)(2,1)} %all-gather.3.cloned.1.call-done), kind=kOutput, calls=%fused_computation.41 | convolution fusion | flops 1074003968 | bytes 5767168 | tf_op jit(solution)/shard_map/dot_general | solution.py:171
  215.7 1.6 gather_fusion.2
  217.3 24.8 %all-to-all-done.3 = bf16[64,32,1,256]{3,1,2,0:T(8,128)(2,1)S(1)} async-done(((bf16[64,32,1,256]{3,1,2,0:T(8,128)(2,1)}), bf16[64,32,1,256]{3,1,2,0:T(8,128)(2,1)S(1)}, u32[]{:S(2)}, u32[]{:S(2)}) %all-to-all-start.3) | async-done | bytes 1048608 | tf_op jit(solution)/shard_map/all_to_all | solution.py:183
  242.1 5.9 %all-to-all-start.2 = ((bf16[64,32,256]{2,1,0:T(8,128)(2,1)}), bf16[64,32,256]{2,1,0:T(8,128)(2,1)S(1)}, u32[]{:S(2)}, u32[]{:S(2)}) async-start(bf16[64,32,256]{2,1,0:T(8,128)(2,1)} %bitcast.24), calls=%async_computation.2 | async-start | bytes 2097152 | tf_op jit(solution)/shard_map/all_to_all | solution.py:183
  249.4 53.5 %all-to-all-done.2 = bf16[64,32,256]{2,1,0:T(8,128)(2,1)S(1)} async-done(((bf16[64,32,256]{2,1,0:T(8,128)(2,1)}), bf16[64,32,256]{2,1,0:T(8,128)(2,1)S(1)}, u32[]{:S(2)}, u32[]{:S(2)}) %all-to-all-start.2) | async-done | bytes 1048608 | tf_op jit(solution)/shard_map/all_to_all | solution.py:183
  (105 shorter events, 27.5 us)
Async XLA Ops:
  7.2 4.9 %copy-start = (bf16[1024,256]{1,0:T(8,128)(2,1)S(1)}, bf16[1024,256]{1,0:T(8,128)(2,1)}, u32[]{:S(2)}) copy-start(bf16[1024,256]{1,0:T(8,128)(2,1)} %param.12) | copy-start | bytes 1572868
  7.2 117.8 %all-gather.3.cloned.1.call-start = ((), (), s32[]{:S(2)}) async-start(), calls=%async_computation.4 | async-start | bytes 3899392 | tf_op jit(solution)/shard_map/all_gather | solution.py:96
  32.7 51.4 %all-to-all-start = ((bf16[64,16,256]{2,1,0:T(8,128)(2,1)}), bf16[64,16,256]{2,1,0:T(8,128)(2,1)S(1)}, u32[]{:S(2)}, u32[]{:S(2)}) async-start(bf16[64,16,256]{2,1,0:T(8,128)(2,1)} %gather_fusion), calls=%async_computation | async-start | bytes 1048576 | tf_op jit(solution)/shard_map/all_to_all | solution.py:101
  86.9 6.8 %copy-start.6 = (bf16[2048]{0:T(1024)(128)(2,1)S(1)}, bf16[2048]{0:T(1024)(128)(2,1)}, u32[]{:S(2)}) copy-start(bf16[2048]{0:T(1024)(128)(2,1)} %param.13) | copy-start | bytes 12292
  86.9 6.8 %copy-start.8 = (bf16[128]{0:T(256)(128)(2,1)S(1)}, bf16[128]{0:T(256)(128)(2,1)}, u32[]{:S(2)}) copy-start(bf16[128]{0:T(256)(128)(2,1)} %param.15) | copy-start | bytes 772
  86.9 6.8 %copy-start.7 = (s32[64,8]{0,1:T(8,128)S(1)}, s32[64,8]{0,1:T(8,128)}, u32[]{:S(2)}) copy-start(s32[64,8]{0,1:T(8,128)} %param.20) | copy-start | bytes 6148
  86.9 7.2 %copy-start.9 = (bf16[128]{0:T(256)(128)(2,1)S(1)}, bf16[128]{0:T(256)(128)(2,1)}, u32[]{:S(2)}) copy-start(bf16[128]{0:T(256)(128)(2,1)} %param.14) | copy-start | bytes 772
  87.0 60.2 %all-to-all-start.1 = ((bf16[8,1024,256]{2,1,0:T(8,128)(2,1)}), bf16[8,1024,256]{2,1,0:T(8,128)(2,1)}, u32[]{:S(2)}, u32[]{:S(2)}) async-start(bf16[8,1024,256]{2,1,0:T(8,128)(2,1)} %broadcast_in_dim.115), calls=%async_computation.1 | async-start | bytes 8388608 | tf_op jit(solution)/shard_map/all_to_all | solution.py:116
  91.6 120.3 %all-gather.5.cloned.1.call-start = ((), (), s32[]{:S(2)}) async-start(), calls=%async_computation.5 | async-start | bytes 4718592 | tf_op jit(solution)/shard_map/all_gather | solution.py:170
  158.8 2.3 slice-start
  162.1 4.1 %copy-start.1 = (f32[1024,64]{0,1:T(8,128)S(1)}, f32[1024,64]{0,1:T(8,128)}, u32[]{:S(2)}) copy-start(f32[1024,64]{0,1:T(8,128)} %get-tuple-element.151) | copy-start | bytes 786436
  162.1 4.1 %copy-start.2 = (f32[1024,64]{0,1:T(8,128)S(1)}, f32[1024,64]{0,1:T(8,128)}, u32[]{:S(2)}) copy-start(f32[1024,64]{0,1:T(8,128)} %get-tuple-element.152) | copy-start | bytes 786436
  166.0 1.7 copy-start.3
  166.0 1.7 copy-start.4
  166.0 1.7 copy-start.5
  180.6 61.5 %all-to-all-start.3 = ((bf16[64,32,1,256]{3,1,2,0:T(8,128)(2,1)}), bf16[64,32,1,256]{3,1,2,0:T(8,128)(2,1)S(1)}, u32[]{:S(2)}, u32[]{:S(2)}) async-start(bf16[64,32,1,256]{3,1,2,0:T(8,128)(2,1)} %bitcast.31), calls=%async_computation.3 | async-start | bytes 2097152 | tf_op jit(solution)/shard_map/all_to_all | solution.py:183
  242.1 60.8 %all-to-all-start.2 = ((bf16[64,32,256]{2,1,0:T(8,128)(2,1)}), bf16[64,32,256]{2,1,0:T(8,128)(2,1)S(1)}, u32[]{:S(2)}, u32[]{:S(2)}) async-start(bf16[64,32,256]{2,1,0:T(8,128)(2,1)} %bitcast.24), calls=%async_computation.2 | async-start | bytes 2097152 | tf_op jit(solution)/shard_map/all_to_all | solution.py:183
Sparse Core Ops, SparseCore 0:
  30.3 94.5 all-gather.2
  178.2 33.6 all-gather.4

commit v11 on v6

--- a/solution.py
+++ b/solution.py
@@ -125,7 +125,8 @@
     dup_source = jnp.sum(jnp.where(counts == 2, block_ids, 0))
     dup_target = jnp.sum(jnp.where(counts == 2, offsets + 1, 0))
     dup_mine = lax.dynamic_index_in_dim(dup_all, dup_source, 0, keepdims=False)
-    dup_pieces = lax.all_gather(dup_mine, "fsdp", axis=0, tiled=False)
+    dup_pieces = lax.all_gather(dup_mine, "fsdp", axis=1, tiled=True)
+    dup_pieces = dup_pieces.reshape(arrival_rows, fsdp_size, width_local).transpose(1, 0, 2)
     pieces = lax.dynamic_update_slice_in_dim(pieces, dup_pieces, dup_target * arrival_rows, 1)
     cuts = [w_query.shape[1], w_key.shape[1], w_value.shape[1], w_out.shape[1]]
     bounds = [sum(cuts[:k]) for k in range(5)]

time: 312 us -> 312 us (level)
  no operation moved by 1% of the time
where the time goes in v11:
time: 312 us; the launch traced here: 311 us
  waiting for transfers between devices  166 us (53%)
  blocking collectives  35.7 us (11%)
  starting transfers between devices  32.6 us (10%)
  local copies, waits for them, and re-layouts  23.8 us (8%)
  matrix products  20.6 us (7%)
  between operations  19.1 us (6%)
  other arithmetic  13.4 us (4%)
    all_to_all x2, waiting for transfers between devices, send_back(): back = lax.all_to_all(sent, DP, split_axis=0, concat_axis=0, tiled=True)  78.2 us
    all_to_all x1, waiting for transfers between devices, local(): lax.all_to_all(outgoing, DP, split_axis=0, concat_axis=0, tiled=True)  33.7 us
    all_gather x1, waiting for transfers between devices, local(): packed = lax.all_gather(packed, 'z', axis=0, tiled=True)  28.3 us
    all_gather x1, waiting for transfers between devices, local(): heads_all = lax.all_gather(mixed, 'fsdp', axis=1, tiled=True)  25.6 us
    all_gather x1, blocking collectives, local(): dup_pieces = lax.all_gather(dup_mine, 'fsdp', axis=1, tiled=True)  20.4 us
    all_to_all x1, starting transfers between devices, local(): lax.all_to_all(outgoing, DP, split_axis=0, concat_axis=0, tiled=True)  16.1 us
    all_gather x1, blocking collectives, local(): packed = lax.all_gather(packed, 'y', axis=0, tiled=True)  15.3 us
    all_to_all x2, starting transfers between devices, send_back(): back = lax.all_to_all(sent, DP, split_axis=0, concat_axis=0, tiled=True)  11.8 us
  transfers between devices with their start and end apart: 6, of which 5 were waited for; matrix products, arithmetic and copies ran while one was open for 6% of the time, Pallas kernels for 0%

profile of v11, /device:TPU:24, one launch (start us, length us, event | category | flops | bytes accessed | tf_op | source)
XLA Modules:
  0.0 311.1 jit_solution(12330760654486404157)
XLA Ops:
  14.9 15.3 %all_gather.12 = bf16[128,896]{1,0:T(8,128)(2,1)} all-gather(bf16[32,896]{1,0:T(8,128)(2,1)S(1)} %constant_dynamic-update-slice_fusion), channel_id=1, replica_groups=mesh['z'=16,'y'=4,'fsdp'=8] {'y'}, dimensions={0}, use_global_device_ids=true | all-gather | bytes 286720 | tf_op jit(solution)/shard_map/all_gather | solution.py:102
  32.7 16.1 %all-to-all-start = ((bf16[64,16,256]{2,1,0:T(8,128)(2,1)}), bf16[64,16,256]{2,1,0:T(8,128)(2,1)S(1)}, u32[]{:S(2)}, u32[]{:S(2)}) async-start(bf16[64,16,256]{2,1,0:T(8,128)(2,1)} %gather_fusion), calls=%async_computation | async-start | bytes 1048576 | tf_op jit(solution)/shard_map/all_to_all | solution.py:109
  50.4 33.7 %all-to-all-done = bf16[64,16,256]{2,1,0:T(8,128)(2,1)S(1)} async-done(((bf16[64,16,256]{2,1,0:T(8,128)(2,1)}), bf16[64,16,256]{2,1,0:T(8,128)(2,1)S(1)}, u32[]{:S(2)}, u32[]{:S(2)}) %all-to-all-start) | async-done | bytes 524320 | tf_op jit(solution)/shard_map/all_to_all | solution.py:109
  84.7 2.2 broadcast_in_dim.115
  86.9 4.7 %all-to-all-start.1 = ((bf16[8,1024,256]{2,1,0:T(8,128)(2,1)}), bf16[8,1024,256]{2,1,0:T(8,128)(2,1)}, u32[]{:S(2)}, u32[]{:S(2)}) async-start(bf16[8,1024,256]{2,1,0:T(8,128)(2,1)} %broadcast_in_dim.115), calls=%async_computation.1 | async-start | bytes 8388608 | tf_op jit(solution)/shard_map/all_to_all | solution.py:124
  94.9 1.8 multiply_cosine_fusion.1
  96.7 28.3 %all-gather.4.cloned.1.call-done = bf16[2048,896]{1,0:T(8,128)(2,1)} async-done(((bf16[128,896]{1,0:T(8,128)(2,1)}), bf16[2048,896]{1,0:T(8,128)(2,1)}) %all-gather.4.cloned.1.call-update) | async-done | bytes 3670032 | tf_op jit(solution)/shard_map/all_gather | solution.py:104
  125.0 1.5 fusion.58
  126.7 20.4 %all-gather = bf16[1,16,2048]{2,1,0:T(8,128)(2,1)S(1)} all-gather(bf16[1,16,256]{2,1,0:T(8,128)(2,1)S(1)} %constant_dynamic-slice_fusion.2), channel_id=2, replica_groups=mesh['z'=16,'y'=4,'fsdp'=8] {'fsdp'}, dimensions={2}, use_global_device_ids=true | all-gather | bytes 73728 | tf_op jit(solution)/shard_map/all_gather | solution.py:128
  147.8 3.1 fusion.21
  150.9 4.2 %fusion.29 = bf16[1024,128]{1,0:T(8,128)(2,1)} fusion(bf16[8,256,128]{2,1,0:T(8,128)(2,1)S(1)} %bitcast.158, bf16[8,1024,256]{2,1,0:T(8,128)(2,1)} %copy_dynamic-update-slice_fusion.1, f32[8,256]{1,0:T(8,128)S(1)} %reshape.580, f32[1024]{0:T(1024)S(1)} %add_rsqrt_fusion.2), kind=kOutput, calls=%fused_computation.44 | convolution fusion | flops 545390592 | bytes 4993024 | tf_op jit(solution)/shard_map/fnk,fkc->nc/dot_general | solution.py:147
  155.1 3.7 %multiply_reduce_fusion.1 = (f32[1024]{0:T(1024)S(1)}, f32[1024,128]{0,1:T(8,128)S(1)}) fusion(bf16[8,256,128]{2,1,0:T(8,128)(2,1)S(1)} %bitcast.157, bf16[8,1024,256]{2,1,0:T(8,128)(2,1)} %copy_dynamic-update-slice_fusion.1, f32[8,256]{1,0:T(8,128)S(1)} %reshape.580, f32[1024]{0:T(1024)S(1)} %add_rsqrt_fusion.2), kind=kOutput, calls=%fused_computation.53 | convolution fusion | flops 545520640 | bytes 5259264 | tf_op jit(solution)/shard_map/fnk,fkc->nc/dot_general | solution.py:147
  162.2 3.8 %multiply_reduce_fusion = (f32[1024,2]{0,1:T(2,128)S(1)}, f32[1024,2,128]{0,2,1:T(8,128)S(1)}) fusion(bf16[2,128,8,256]{3,2,1,0:T(8,128)(2,1)S(1)} %bitcast.153, f32[8,256]{1,0:T(8,128)S(1)} %reshape.580, f32[1024]{0:T(1024)S(1)} %add_rsqrt_fusion.2, bf16[8,1024,256]{2,1,0:T(8,128)(2,1)} %copy_dynamic-update-slice_fusion.1), kind=kOutput, calls=%fused_computation.48 | convolution fusion | flops 1082652672 | bytes 6311936 | tf_op jit(solution)/shard_map/fnk,fkc->nc/dot_general | solution.py:147
  167.7 9.4 %while.12 = (s32[]{:T(128)}, bf16[2,512,1,2,128]{4,3,1,0,2:T(2,128)(2,1)S(1)}, s32[2,512]{1,0:T(2,128)S(1)}, s32[2,512]{1,0:T(2,128)S(1)}, bf16[2,512,1,2,128]{4...) while((s32[]{:T(128)}, ...), condition=%wide.region_17.18_spmd.clone.clone, body=%wide.region_14.17_spmd.clone.clone.sunk | while | flops 551155712 | bytes 16285793 | solution.py:170
  170.6 1.6 fusion.73
  175.3 1.6 fusion.73
  178.9 1.6 gather_fusion.4
  180.6 5.8 %all-to-all-start.3 = ((bf16[64,32,1,256]{3,1,2,0:T(8,128)(2,1)}), bf16[64,32,1,256]{3,1,2,0:T(8,128)(2,1)S(1)}, u32[]{:S(2)}, u32[]{:S(2)}) async-start(bf16[64,32,1,256]{3,1,2,0:T(8,128)(2,1)} %bitcast.32), calls=%async_computation.3 | async-start | bytes 2097152 | tf_op jit(solution)/shard_map/all_to_all | solution.py:192
  186.4 25.6 %all-gather.6.cloned.1.call-done = bf16[1024,2048]{1,0:T(8,128)(2,1)} async-done(((bf16[1024,256]{1,0:T(8,128)(2,1)}), bf16[1024,2048]{1,0:T(8,128)(2,1)}) %all-gather.6.cloned.1.call-update) | async-done | bytes 4194320 | tf_op jit(solution)/shard_map/all_gather | solution.py:179
  212.0 3.7 %convolution_convert_fusion = bf16[1024,256]{1,0:T(8,128)(2,1)S(1)} fusion(bf16[1024,2048]{1,0:T(8,128)(2,1)} %all-gather.6.cloned.1.call-done, bf16[2048,896]{1,0:T(8,128)(2,1)} %all-gather.4.cloned.1.call-done), kind=kOutput, calls=%fused_computation.41 | convolution fusion | flops 1074003968 | bytes 5767168 | tf_op jit(solution)/shard_map/dot_general | solution.py:180
  215.7 1.6 gather_fusion.2
  217.4 24.8 %all-to-all-done.3 = bf16[64,32,1,256]{3,1,2,0:T(8,128)(2,1)S(1)} async-done(((bf16[64,32,1,256]{3,1,2,0:T(8,128)(2,1)}), bf16[64,32,1,256]{3,1,2,0:T(8,128)(2,1)S(1)}, u32[]{:S(2)}, u32[]{:S(2)}) %all-to-all-start.3) | async-done | bytes 1048608 | tf_op jit(solution)/shard_map/all_to_all | solution.py:192
  242.1 5.9 %all-to-all-start.2 = ((bf16[64,32,256]{2,1,0:T(8,128)(2,1)}), bf16[64,32,256]{2,1,0:T(8,128)(2,1)S(1)}, u32[]{:S(2)}, u32[]{:S(2)}) async-start(bf16[64,32,256]{2,1,0:T(8,128)(2,1)} %bitcast.25), calls=%async_computation.2 | async-start | bytes 2097152 | tf_op jit(solution)/shard_map/all_to_all | solution.py:192
  249.4 53.5 %all-to-all-done.2 = bf16[64,32,256]{2,1,0:T(8,128)(2,1)S(1)} async-done(((bf16[64,32,256]{2,1,0:T(8,128)(2,1)}), bf16[64,32,256]{2,1,0:T(8,128)(2,1)S(1)}, u32[]{:S(2)}, u32[]{:S(2)}) %all-to-all-start.2) | async-done | bytes 1048608 | tf_op jit(solution)/shard_map/all_to_all | solution.py:192
  (106 shorter events, 27.5 us)
Async XLA Ops:
  7.2 4.9 %copy-start = (bf16[1024,256]{1,0:T(8,128)(2,1)S(1)}, bf16[1024,256]{1,0:T(8,128)(2,1)}, u32[]{:S(2)}) copy-start(bf16[1024,256]{1,0:T(8,128)(2,1)} %param.12) | copy-start | bytes 1572868
  7.2 117.8 %all-gather.4.cloned.1.call-start = ((), (), s32[]{:S(2)}) async-start(), calls=%async_computation.4 | async-start | bytes 3899392 | tf_op jit(solution)/shard_map/all_gather | solution.py:104
  32.7 51.4 %all-to-all-start = ((bf16[64,16,256]{2,1,0:T(8,128)(2,1)}), bf16[64,16,256]{2,1,0:T(8,128)(2,1)S(1)}, u32[]{:S(2)}, u32[]{:S(2)}) async-start(bf16[64,16,256]{2,1,0:T(8,128)(2,1)} %gather_fusion), calls=%async_computation | async-start | bytes 1048576 | tf_op jit(solution)/shard_map/all_to_all | solution.py:109
  86.9 6.7 %copy-start.6 = (bf16[2048]{0:T(1024)(128)(2,1)S(1)}, bf16[2048]{0:T(1024)(128)(2,1)}, u32[]{:S(2)}) copy-start(bf16[2048]{0:T(1024)(128)(2,1)} %param.13) | copy-start | bytes 12292
  86.9 6.8 %copy-start.8 = (bf16[128]{0:T(256)(128)(2,1)S(1)}, bf16[128]{0:T(256)(128)(2,1)}, u32[]{:S(2)}) copy-start(bf16[128]{0:T(256)(128)(2,1)} %param.15) | copy-start | bytes 772
  86.9 6.8 %copy-start.7 = (s32[64,8]{0,1:T(8,128)S(1)}, s32[64,8]{0,1:T(8,128)}, u32[]{:S(2)}) copy-start(s32[64,8]{0,1:T(8,128)} %param.20) | copy-start | bytes 6148
  86.9 7.1 %copy-start.9 = (bf16[128]{0:T(256)(128)(2,1)S(1)}, bf16[128]{0:T(256)(128)(2,1)}, u32[]{:S(2)}) copy-start(bf16[128]{0:T(256)(128)(2,1)} %param.14) | copy-start | bytes 772
  86.9 60.2 %all-to-all-start.1 = ((bf16[8,1024,256]{2,1,0:T(8,128)(2,1)}), bf16[8,1024,256]{2,1,0:T(8,128)(2,1)}, u32[]{:S(2)}, u32[]{:S(2)}) async-start(bf16[8,1024,256]{2,1,0:T(8,128)(2,1)} %broadcast_in_dim.115), calls=%async_computation.1 | async-start | bytes 8388608 | tf_op jit(solution)/shard_map/all_to_all | solution.py:124
  91.6 120.3 %all-gather.6.cloned.1.call-start = ((), (), s32[]{:S(2)}) async-start(), calls=%async_computation.5 | async-start | bytes 4718592 | tf_op jit(solution)/shard_map/all_gather | solution.py:179
  158.8 2.3 slice-start
  162.1 4.1 %copy-start.1 = (f32[1024,64]{0,1:T(8,128)S(1)}, f32[1024,64]{0,1:T(8,128)}, u32[]{:S(2)}) copy-start(f32[1024,64]{0,1:T(8,128)} %get-tuple-element.151) | copy-start | bytes 786436
  162.1 4.1 %copy-start.2 = (f32[1024,64]{0,1:T(8,128)S(1)}, f32[1024,64]{0,1:T(8,128)}, u32[]{:S(2)}) copy-start(f32[1024,64]{0,1:T(8,128)} %get-tuple-element.152) | copy-start | bytes 786436
  166.0 1.7 copy-start.3
  166.0 1.7 copy-start.4
  166.0 1.7 copy-start.5
  180.6 61.5 %all-to-all-start.3 = ((bf16[64,32,1,256]{3,1,2,0:T(8,128)(2,1)}), bf16[64,32,1,256]{3,1,2,0:T(8,128)(2,1)S(1)}, u32[]{:S(2)}, u32[]{:S(2)}) async-start(bf16[64,32,1,256]{3,1,2,0:T(8,128)(2,1)} %bitcast.32), calls=%async_computation.3 | async-start | bytes 2097152 | tf_op jit(solution)/shard_map/all_to_all | solution.py:192
  242.1 60.8 %all-to-all-start.2 = ((bf16[64,32,256]{2,1,0:T(8,128)(2,1)}), bf16[64,32,256]{2,1,0:T(8,128)(2,1)S(1)}, u32[]{:S(2)}, u32[]{:S(2)}) async-start(bf16[64,32,256]{2,1,0:T(8,128)(2,1)} %bitcast.25), calls=%async_computation.2 | async-start | bytes 2097152 | tf_op jit(solution)/shard_map/all_to_all | solution.py:192
Sparse Core Ops, SparseCore 0:
  30.3 94.5 all-gather.3
  178.2 33.7 all-gather.5
